TPU v7x, 32 devices: a whole 2x2x4 slice. The times are simulated.
32 devices in a mesh: vol: 8 (over z, y), ptcl: 4 (over x, core).
Axes of the slice: x: 2, y: 2, z: 4, core: 2. Of those that a mesh axis runs over, the one named last changes fastest.
Arguments:
- images: bfloat16 [32, 256, 256], P(('vol', 'ptcl')), may hold values from -6 to 6
- defocus: bfloat16 [32], P(('vol', 'ptcl')), may hold values from 20 to 200
- volume: float32 [4096, 256], P('vol'), may hold values from -6 to 6
- counts: int32 [8, 4, 8], P('vol', 'ptcl'), may hold values from 1 to 96, as said below
- slot_pixel: int32 [8, 4, 8, 96], P('vol', 'ptcl'), may hold values from 0 to 511, as said below
- slot_taps: int32 [8, 4, 8, 8, 96], P('vol', 'ptcl'), may hold values from 0 to 511, as said below
- slot_weights: bfloat16 [8, 4, 8, 8, 96], P('vol', 'ptcl'), may hold values from 0.019897461 to 0.25
Outputs:
- volume_next: float32 [4096, 256], P('vol')
Inputs may be any that keep to these rules, and one draw needn't show every extreme that they name: The 8 counts of each holder sum to 512; in each particle shard one owner receives exactly 96 live slots from every holder of that shard. `slot_pixel`: the live slots of a holder (slot index below its count) name each of its 512 pixel blocks exactly once; the other slots hold valid ids. `slot_taps`: the 8 taps of one slot name 8 different blocks.
All inputs are finite; a program needn't handle non-finite values.
Results may differ from a plain program's by a relative error of at most 0.0034.
Values may be sent and summed in bfloat16 or wider, within the bound.
No kernel may reach another device: no remote copies, remote signals or barrier semaphores. Data moves between devices by JAX's collectives and lax.ppermute only.
A program may use at most 64 MiB of HBM per device.

v0:
```python
import math

import jax
import jax.numpy as jnp
from jax import lax
from jax.sharding import PartitionSpec as P

L = 256
BLK = 128
PB = 512


learn_rate = 1.0
phase_shift = 0.1


def dft_tables():
    freq_ids = jnp.arange(L, dtype=jnp.int32)
    product = (freq_ids[:, None] - L // 2) * freq_ids[None, :] % L
    angle = 2.0 * math.pi / L * product.astype(jnp.float32)
    return (jnp.cos(angle).astype(jnp.bfloat16), jnp.sin(angle).astype(jnp.bfloat16))


def transform(pictures, cos_table, sin_table):
    row_cos = jnp.einsum(
        "iyx,kx->iyk", pictures, cos_table, preferred_element_type=jnp.float32
    ).astype(jnp.bfloat16)
    row_sin = jnp.einsum(
        "iyx,kx->iyk", pictures, sin_table, preferred_element_type=jnp.float32
    ).astype(jnp.bfloat16)
    real_part = (
        jnp.einsum("ay,iyb->iab", cos_table, row_cos, preferred_element_type=jnp.float32)
        - jnp.einsum("ay,iyb->iab", sin_table, row_sin, preferred_element_type=jnp.float32)
    ) / L
    imag_part = (
        -(
            jnp.einsum("ay,iyb->iab", sin_table, row_cos, preferred_element_type=jnp.float32)
            + jnp.einsum("ay,iyb->iab", cos_table, row_sin, preferred_element_type=jnp.float32)
        )
        / L
    )
    count_img = pictures.shape[0]
    blocks = jnp.concatenate(
        [real_part.reshape(count_img, PB, BLK), imag_part.reshape(count_img, PB, BLK)], axis=2
    )
    return blocks.reshape(count_img * PB, 2 * BLK).astype(jnp.bfloat16)


def ctf_rows(pixel_ids, focus):
    block_id = pixel_ids % PB
    row_id = block_id // (L // BLK)
    col_id = block_id % (L // BLK) * BLK
    lane_ids = jnp.arange(BLK, dtype=jnp.int32)
    freq_y = (row_id - L // 2).astype(jnp.float32) / L
    freq_x = (col_id[..., None] + lane_ids - L // 2).astype(jnp.float32) / L
    radius = freq_x * freq_x + (freq_y * freq_y)[..., None]
    return -jnp.sin(math.pi * focus.astype(jnp.float32)[..., None] * radius + phase_shift)


def residual_terms(prediction, observed, ctf_values, live_slots):
    shape = prediction.shape
    pred_wide = prediction.astype(jnp.float32).reshape(shape[:-1] + (2, BLK))
    obs_wide = observed.astype(jnp.float32).reshape(shape[:-1] + (2, BLK))
    factor = ctf_values[..., None, :]
    misfit = factor * (factor * pred_wide - obs_wide)
    misfit = jnp.where(live_slots[..., None, None], misfit, 0.0)
    return misfit.reshape(shape).astype(jnp.bfloat16)


def tap_matrix(tap_ids, weights, block_count):
    owners, taps, slots = tap_ids.shape
    flat_taps = jnp.transpose(tap_ids, (0, 2, 1)).reshape(owners * slots, taps)
    flat_weights = jnp.transpose(weights, (0, 2, 1)).reshape(owners * slots, taps)
    block_ids = jnp.arange(block_count, dtype=jnp.int32)
    picked = jnp.where(
        flat_taps[:, :, None] == block_ids[None, None, :],
        flat_weights[:, :, None],
        jnp.zeros((), jnp.bfloat16),
    )
    return jnp.sum(picked, axis=1, dtype=jnp.bfloat16)


def predict_rows(matrix, extract, owners):
    summed = jnp.dot(matrix, extract, preferred_element_type=jnp.float32)
    return summed.reshape(owners, -1, extract.shape[1])


def local(images, defocus, volume, counts, slot_pixel, slot_taps, slot_weights):
    cos_table, sin_table = dft_tables()
    extract = volume.astype(jnp.bfloat16)
    slot_count = counts[0, 0]
    pixel_ids = slot_pixel[0, 0]
    tap_ids = slot_taps[0, 0]
    weights = slot_weights[0, 0]
    owners = pixel_ids.shape[0]
    capacity = pixel_ids.shape[1]
    live_slots = jnp.arange(capacity, dtype=jnp.int32)[None, :] < slot_count[:, None]
    got_taps, got_weights = (
        lax.all_to_all(tap_ids, "vol", split_axis=0, concat_axis=0, tiled=True),
        lax.all_to_all(weights, "vol", split_axis=0, concat_axis=0, tiled=True),
    )
    matrix = tap_matrix(got_taps, got_weights, volume.shape[0])
    prediction = predict_rows(matrix, extract, owners).astype(jnp.bfloat16)
    returned = lax.all_to_all(prediction, "vol", split_axis=0, concat_axis=0, tiled=True)
    observed = transform(images, cos_table, sin_table)
    ctf_values = ctf_rows(pixel_ids, defocus[pixel_ids // PB])
    weighted = residual_terms(returned, observed[pixel_ids], ctf_values, live_slots)
    got_residual = lax.all_to_all(weighted, "vol", split_axis=0, concat_axis=0, tiled=True)
    flat_residual = got_residual.reshape(-1, volume.shape[1])
    gradient = lax.dot_general(
        matrix, flat_residual, (((0,), (0,)), ((), ())), preferred_element_type=jnp.float32
    )
    gradient = lax.psum(gradient, "ptcl")
    return volume - learn_rate * gradient


def solution(mesh):
    placed = (
        P(("vol", "ptcl"), None, None),
        P(("vol", "ptcl")),
        P("vol", None),
        P("vol", "ptcl", None),
        P("vol", "ptcl", None, None),
        P("vol", "ptcl", None, None, None),
        P("vol", "ptcl", None, None, None),
    )
    return jax.shard_map(
        local, mesh=mesh, in_specs=placed, out_specs=P("vol", None), check_vma=False
    )
```

profile of v0, /device:TPU:0, one launch (start us, length us, event | category | flops | bytes accessed | tf_op | source)
XLA Modules:
  0.0 113.2 jit_solution(16446139586523251480)
XLA Ops:
  6.5 7.4 %all-to-all-start.1 = ((bf16[8,8,96]{2,1,0:T(8,128)(2,1)}), bf16[8,8,96]{2,1,0:T(8,128)(2,1)S(1)}, u32[]{:S(2)}, u32[]{:S(2)}) async-start(bf16[8,8,96]{2,1,0:T(8,128)(2,1)} %bitcast.56), calls=%async_computation.1 | async-start | bytes 32768 | tf_op jit(solution)/shard_map/all_to_all | solution.py:100
  14.0 0.7 fusion.29
  14.7 0.7 fusion.25
  15.4 1.1 %convolution_convert_fusion.2 = bf16[256,256]{1,0:T(8,128)(2,1)S(1)} fusion(bf16[1,256,256]{2,1,0:T(8,128)(2,1)S(1)} %copy-done, s32[256]{0:T(256)S(1)} %iota_add_fusion), kind=kOutput, calls=%fused_computation.13 | convolution fusion | flops 34603008 | bytes 263168 | tf_op jit(solution)/shard_map/iyx,kx->iyk/dot_general | solution.py:25
  16.5 1.2 %fusion.23 = f32[256,256]{1,0:T(8,128)S(1)} fusion(bf16[256,256]{1,0:T(8,128)(2,1)S(1)} %convolution_convert_fusion.2, s32[256]{0:T(256)S(1)} %iota_add_fusion), kind=kOutput, calls=%fused_computation.38 | convolution fusion | flops 34537472 | bytes 394240 | tf_op jit(solution)/shard_map/ay,iyb->iab/dot_general | solution.py:37
  17.7 1.2 %fusion.22 = f32[256,256]{1,0:T(8,128)S(1)} fusion(bf16[256,256]{1,0:T(8,128)(2,1)S(1)} %convolution_convert_fusion.2, s32[256]{0:T(256)S(1)} %iota_add_fusion), kind=kOutput, calls=%fused_computation.37 | convolution fusion | flops 34537472 | bytes 394240 | tf_op jit(solution)/shard_map/ay,iyb->iab/dot_general | solution.py:32
  19.6 1.5 %sine_negate_fusion = f32[8,96,128]{2,1,0:T(8,128)S(1)} fusion(f32[8,96]{1,0:T(8,128)S(1)} %fusion.29, s32[8,96]{1,0:T(8,128)S(1)} %fusion.25, f32[]{:T(128)} %bitcast.7), kind=kLoop, calls=%fused_computation.23 | loop fusion | flops 884736 | bytes 399364 | tf_op jit(solution)/shard_map/neg | solution.py:57
  21.1 1.2 %convolution_convert_fusion.1 = bf16[256,256]{1,0:T(8,128)(2,1)S(1)} fusion(bf16[1,256,256]{2,1,0:T(8,128)(2,1)S(1)} %copy-done, s32[256]{0:T(256)S(1)} %iota_add_fusion), kind=kOutput, calls=%fused_computation.12 | convolution fusion | flops 34603008 | bytes 263168 | tf_op jit(solution)/shard_map/iyx,kx->iyk/dot_general | solution.py:28
  22.2 6.0 %all-to-all-start = ((s32[8,8,96]{2,1,0:T(8,128)}), s32[8,8,96]{2,1,0:T(8,128)S(1)}, u32[]{:S(2)}, u32[]{:S(2)}) async-start(s32[8,8,96]{2,1,0:T(8,128)} %bitcast), calls=%async_computation | async-start | bytes 65536 | tf_op jit(solution)/shard_map/all_to_all | solution.py:99
  28.2 1.2 %fusion.7 = bf16[1,256,256]{1,2,0:T(8,128)(2,1)S(1)} fusion(f32[256,256]{1,0:T(8,128)S(1)} %fusion.23, bf16[256,256]{1,0:T(8,128)(2,1)S(1)} %convolution_convert_fusion.1, s32[256]{0:T(256)S(1)} %iota_add_fusion), kind=kOutput, calls=%fused_computation.14 | convolution fusion | flops 34799616 | bytes 525312 | tf_op jit(solution)/shard_map/ay,iyb->iab/dot_general | solution.py:38
  29.6 5.3 %all-to-all-done = s32[8,8,96]{2,1,0:T(8,128)S(1)} async-done(((s32[8,8,96]{2,1,0:T(8,128)}), s32[8,8,96]{2,1,0:T(8,128)S(1)}, u32[]{:S(2)}, u32[]{:S(2)}) %all-to-all-start) | async-done | bytes 24608 | tf_op jit(solution)/shard_map/all_to_all | solution.py:99
  35.1 5.1 %fusion.1 = bf16[768,512]{1,0:T(8,128)(2,1)S(1)} fusion(s32[768,8]{1,0:T(8,128)S(1)} %bitcast.51, bf16[768,8]{1,0:T(8,128)(2,1)S(1)} %bitcast.52), kind=kLoop, calls=%fused_computation.3 | loop fusion | flops 9043968 | bytes 823296 | tf_op jit(solution)/shard_map/reduce_sum | solution.py:80
  40.2 1.1 convolution_convert_fusion
  41.3 4.1 %all-to-all-start.2 = ((bf16[8,96,256]{2,1,0:T(8,128)(2,1)}), bf16[8,96,256]{2,1,0:T(8,128)(2,1)}, u32[]{:S(2)}, u32[]{:S(2)}) async-start(bf16[8,96,256]{2,1,0:T(8,128)(2,1)} %convolution_convert_fusion), calls=%async_computation.2 | async-start | bytes 786432 | tf_op jit(solution)/shard_map/all_to_all | solution.py:104
  45.6 1.2 %fusion.8 = bf16[1,256,256]{1,2,0:T(8,128)(2,1)S(1)} fusion(f32[256,256]{1,0:T(8,128)S(1)} %fusion.22, bf16[256,256]{1,0:T(8,128)(2,1)S(1)} %convolution_convert_fusion.1, s32[256]{0:T(256)S(1)} %iota_add_fusion), kind=kOutput, calls=%fused_computation.15 | convolution fusion | flops 34734080 | bytes 525312 | tf_op jit(solution)/shard_map/ay,iyb->iab/dot_general | solution.py:33
  47.1 0.6 mul.128
  48.1 0.4 copy-done.2
  48.6 2.7 %gather_fusion = bf16[768,256]{1,0:T(8,128)(2,1)S(1)} fusion(bf16[512,256]{1,0:T(8,128)(2,1)S(1)} %maximum_bitcast_fusion, s32[1024]{0:T(1024)S(1)} %pad_clamp_fusion), kind=kCustom, calls=%fused_computation | custom fusion | bytes 789504 | tf_op jit(solution)/shard_map/gather | solution.py:107
  51.3 4.0 %all-to-all-done.2 = bf16[8,96,256]{2,1,0:T(8,128)(2,1)} async-done(((bf16[8,96,256]{2,1,0:T(8,128)(2,1)}), bf16[8,96,256]{2,1,0:T(8,128)(2,1)}, u32[]{:S(2)}, u32[]{:S(2)}) %all-to-all-start.2) | async-done | bytes 393248 | tf_op jit(solution)/shard_map/all_to_all | solution.py:104
  55.4 1.2 %fusion.11 = bf16[8,96,256]{2,1,0:T(8,128)(2,1)S(1)} fusion(f32[8,96,256]{2,1,0:T(8,128)S(1)} %mul.128, bf16[8,96,256]{2,1,0:T(8,128)(2,1)S(1)} %bitcast.50, bf16[8,96,256]{2,1,0:T(8,128)(2,1)} %all-to-all-done.2, pred[8,96]{1,0:T(8,128)(4,1)S(1)} %iota_compare_fusion.1), kind=kLoop, calls=%fused_computation.19 | loop fusion | flops 1376256 | bytes 1966848 | tf_op jit(solution)/shard_map/convert_element_type | solution.py:67
  56.6 14.6 %all_to_all.20 = bf16[8,96,256]{2,1,0:T(8,128)(2,1)S(1)} all-to-all(bf16[8,96,256]{2,1,0:T(8,128)(2,1)S(1)} %fusion.11), channel_id=1, replica_groups=mesh['vol'=8,'ptcl'=4] {'vol'}, dimensions={0} | all-to-all | bytes 786432 | tf_op jit(solution)/shard_map/all_to_all | solution.py:108
  71.2 1.2 %fusion.56 = f32[512,256]{1,0:T(8,128)} fusion(bf16[768,512]{1,0:T(8,128)(2,1)S(1)} %fusion.1, bf16[768,256]{1,0:T(8,128)(2,1)S(1)} %bitcast.53), kind=kOutput, calls=%fused_computation.84 | convolution fusion | flops 201326592 | bytes 1703936 | tf_op jit(solution)/shard_map/dot_general | solution.py:110
  72.4 32.0 %all-reduce.2.cloned.1.call-done = f32[512,256]{1,0:T(8,128)} async-done(((f32[512,256]{1,0:T(8,128)}), f32[512,256]{1,0:T(8,128)}) %all-reduce.2.cloned.1.call-update) | async-done | bytes 524304 | tf_op jit(solution)/shard_map/psum | solution.py:113
  104.4 1.9 %sub.47 = f32[512,256]{1,0:T(8,128)} subtract(f32[512,256]{1,0:T(8,128)S(1)} %copy-done.1, f32[512,256]{1,0:T(8,128)} %all-reduce.2.cloned.1.call-done) | non-fusion elementwise | flops 131072 | bytes 1572864 | tf_op jit(solution)/shard_map/sub | solution.py:114
  (23 shorter events, 1.3 us)
Async XLA Ops:
  6.5 8.8 %copy-start = (bf16[1,256,256]{2,1,0:T(8,128)(2,1)S(1)}, bf16[1,256,256]{2,1,0:T(8,128)(2,1)}, u32[]{:S(2)}) copy-start(bf16[1,256,256]{2,1,0:T(8,128)(2,1)} %param.7) | copy-start | bytes 393220
  6.5 15.7 %all-to-all-start.1 = ((bf16[8,8,96]{2,1,0:T(8,128)(2,1)}), bf16[8,8,96]{2,1,0:T(8,128)(2,1)S(1)}, u32[]{:S(2)}, u32[]{:S(2)}) async-start(bf16[8,8,96]{2,1,0:T(8,128)(2,1)} %bitcast.56), calls=%async_computation.1 | async-start | bytes 32768 | tf_op jit(solution)/shard_map/all_to_all | solution.py:100
  22.2 12.7 %all-to-all-start = ((s32[8,8,96]{2,1,0:T(8,128)}), s32[8,8,96]{2,1,0:T(8,128)S(1)}, u32[]{:S(2)}, u32[]{:S(2)}) async-start(s32[8,8,96]{2,1,0:T(8,128)} %bitcast), calls=%async_computation | async-start | bytes 65536 | tf_op jit(solution)/shard_map/all_to_all | solution.py:99
  35.1 5.1 %copy-start.1 = (f32[512,256]{1,0:T(8,128)S(1)}, f32[512,256]{1,0:T(8,128)}, u32[]{:S(2)}) copy-start(f32[512,256]{1,0:T(8,128)} %param.9) | copy-start | bytes 1572868
  41.3 14.1 %all-to-all-start.2 = ((bf16[8,96,256]{2,1,0:T(8,128)(2,1)}), bf16[8,96,256]{2,1,0:T(8,128)(2,1)}, u32[]{:S(2)}, u32[]{:S(2)}) async-start(bf16[8,96,256]{2,1,0:T(8,128)(2,1)} %convolution_convert_fusion), calls=%async_computation.2 | async-start | bytes 786432 | tf_op jit(solution)/shard_map/all_to_all | solution.py:104
  45.4 59.0 %all-reduce.2.cloned.1.call-start = ((), (), s32[]{:S(2)}) async-start(), calls=%async_computation.4 | async-start | bytes 1048576 | tf_op jit(solution)/shard_map/psum | solution.py:113
  47.8 0.7 copy-start.2
  48.6 2.7 %copy-start.3 = (s32[1,1,8]{2,1,0:T(1,128)S(1)}, s32[1,1,8]{2,1,0:T(1,128)}, u32[]{:S(2)}) copy-start(s32[1,1,8]{2,1,0:T(1,128)} %param.10) | copy-start | bytes 100
Sparse Core Ops, SparseCore 0:
  72.5 31.8 all-reduce.1
where the time goes:
time: 114 us; the launch traced here: 113 us
  waiting for transfers between devices  41.4 us (36%)
  starting transfers between devices  17.7 us (16%)
  blocking collectives  14.6 us (13%)
  between operations  14.2 us (12%)
  other arithmetic  11.1 us (10%)
  matrix products  9.4 us (8%)
  local copies, waits for them, and re-layouts  4.61 us (4%)
    psum x1, waiting for transfers between devices, local(): gradient = lax.psum(gradient, 'ptcl')  32 us
    all_to_all x1, blocking collectives, local(): lax.all_to_all(weighted, 'vol', split_axis=0, concat_axis=0, tiled=True)  14.6 us
    all_to_all x1, starting transfers between devices, local(): lax.all_to_all(weights, 'vol', split_axis=0, concat_axis=0, tiled=True)  7.41 us
    all_to_all x1, starting transfers between devices, local(): lax.all_to_all(tap_ids, 'vol', split_axis=0, concat_axis=0, tiled=True)  6.01 us
    all_to_all x1, waiting for transfers between devices, local(): lax.all_to_all(tap_ids, 'vol', split_axis=0, concat_axis=0, tiled=True)  5.34 us
    reduce_sum x1, other arithmetic, tap_matrix(): return jnp.sum(picked, axis=1, dtype=jnp.bfloat16)  5.06 us
    all_to_all x1, starting transfers between devices, local(): lax.all_to_all(prediction, 'vol', split_axis=0, concat_axis=0, tiled=True)  4.09 us
    all_to_all x1, waiting for transfers between devices, local(): lax.all_to_all(prediction, 'vol', split_axis=0, concat_axis=0, tiled=True)  4.04 us
  transfers between devices with their start and end apart: 4, of which 3 were waited for; matrix products, arithmetic and copies ran while one was open for 13% of the time, Pallas kernels for 0%

commit v1 on v0

--- a/solution.py
+++ b/solution.py
@@ -22,32 +22,27 @@
 
 
 def transform(pictures, cos_table, sin_table):
-    row_cos = jnp.einsum(
-        "iyx,kx->iyk", pictures, cos_table, preferred_element_type=jnp.float32
+    first = jnp.stack([cos_table, sin_table])
+    rows = jnp.einsum(
+        "iyx,jkx->ijyk", pictures, first, preferred_element_type=jnp.float32
     ).astype(jnp.bfloat16)
-    row_sin = jnp.einsum(
-        "iyx,kx->iyk", pictures, sin_table, preferred_element_type=jnp.float32
-    ).astype(jnp.bfloat16)
-    real_part = (
-        jnp.einsum("ay,iyb->iab", cos_table, row_cos, preferred_element_type=jnp.float32)
-        - jnp.einsum("ay,iyb->iab", sin_table, row_sin, preferred_element_type=jnp.float32)
-    ) / L
-    imag_part = (
-        -(
-            jnp.einsum("ay,iyb->iab", sin_table, row_cos, preferred_element_type=jnp.float32)
-            + jnp.einsum("ay,iyb->iab", cos_table, row_sin, preferred_element_type=jnp.float32)
-        )
-        / L
-    )
     count_img = pictures.shape[0]
-    blocks = jnp.concatenate(
-        [real_part.reshape(count_img, PB, BLK), imag_part.reshape(count_img, PB, BLK)], axis=2
-    )
+    rows = rows.reshape(count_img, 2 * L, L)
+    scale = jnp.asarray(1.0 / L, jnp.bfloat16)
+    second = jnp.concatenate(
+        [
+            jnp.concatenate([cos_table, -sin_table], axis=1),
+            jnp.concatenate([-sin_table, -cos_table], axis=1),
+        ],
+        axis=0,
+    ) * scale
+    parts = jnp.einsum("ay,iyb->iab", second, rows, preferred_element_type=jnp.float32)
+    parts = parts.reshape(count_img, 2, L, L // BLK, BLK)
+    blocks = jnp.transpose(parts, (0, 2, 3, 1, 4))
     return blocks.reshape(count_img * PB, 2 * BLK).astype(jnp.bfloat16)
 
 
-def ctf_rows(pixel_ids, focus):
-    block_id = pixel_ids % PB
+def ctf_rows(block_id, focus):
     row_id = block_id // (L // BLK)
     col_id = block_id % (L // BLK) * BLK
     lane_ids = jnp.arange(BLK, dtype=jnp.int32)
@@ -80,11 +75,6 @@
     return jnp.sum(picked, axis=1, dtype=jnp.bfloat16)
 
 
-def predict_rows(matrix, extract, owners):
-    summed = jnp.dot(matrix, extract, preferred_element_type=jnp.float32)
-    return summed.reshape(owners, -1, extract.shape[1])
-
-
 def local(images, defocus, volume, counts, slot_pixel, slot_taps, slot_weights):
     cos_table, sin_table = dft_tables()
     extract = volume.astype(jnp.bfloat16)
@@ -92,21 +82,33 @@
     pixel_ids = slot_pixel[0, 0]
     tap_ids = slot_taps[0, 0]
     weights = slot_weights[0, 0]
-    owners = pixel_ids.shape[0]
-    capacity = pixel_ids.shape[1]
+    owners, taps, capacity = tap_ids.shape
     live_slots = jnp.arange(capacity, dtype=jnp.int32)[None, :] < slot_count[:, None]
-    got_taps, got_weights = (
-        lax.all_to_all(tap_ids, "vol", split_axis=0, concat_axis=0, tiled=True),
-        lax.all_to_all(weights, "vol", split_axis=0, concat_axis=0, tiled=True),
+    meta = jnp.concatenate(
+        [
+            tap_ids.astype(jnp.float32),
+            weights.astype(jnp.float32),
+            (pixel_ids % PB).astype(jnp.float32)[:, None, :],
+            defocus[pixel_ids // PB].astype(jnp.float32)[:, None, :],
+            live_slots.astype(jnp.float32)[:, None, :],
+        ],
+        axis=1,
     )
+    got_meta = lax.all_to_all(meta, "vol", split_axis=0, concat_axis=0, tiled=True)
+    observed = transform(images, cos_table, sin_table)
+    rows = observed[pixel_ids]
+    got_rows = lax.all_to_all(rows, "vol", split_axis=0, concat_axis=0, tiled=True)
+    got_taps = got_meta[:, :taps, :].astype(jnp.int32)
+    got_weights = got_meta[:, taps : 2 * taps, :].astype(jnp.bfloat16)
+    got_block = got_meta[:, 2 * taps, :].astype(jnp.int32)
+    got_focus = got_meta[:, 2 * taps + 1, :]
+    got_live = got_meta[:, 2 * taps + 2, :] > 0.5
     matrix = tap_matrix(got_taps, got_weights, volume.shape[0])
-    prediction = predict_rows(matrix, extract, owners).astype(jnp.bfloat16)
-    returned = lax.all_to_all(prediction, "vol", split_axis=0, concat_axis=0, tiled=True)
-    observed = transform(images, cos_table, sin_table)
-    ctf_values = ctf_rows(pixel_ids, defocus[pixel_ids // PB])
-    weighted = residual_terms(returned, observed[pixel_ids], ctf_values, live_slots)
-    got_residual = lax.all_to_all(weighted, "vol", split_axis=0, concat_axis=0, tiled=True)
-    flat_residual = got_residual.reshape(-1, volume.shape[1])
+    prediction = jnp.dot(matrix, extract, preferred_element_type=jnp.float32)
+    prediction = prediction.astype(jnp.bfloat16).reshape(owners, capacity, -1)
+    ctf_values = ctf_rows(got_block, got_focus)
+    weighted = residual_terms(prediction, got_rows, ctf_values, got_live)
+    flat_residual = weighted.reshape(-1, volume.shape[1])
     gradient = lax.dot_general(
         matrix, flat_residual, (((0,), (0,)), ((), ())), preferred_element_type=jnp.float32
     )

time: 114 us -> 90.5 us (0.79)
  blocking collectives: 14.6 us -> 0 us
  matrix products: 9.4 us -> 2.18 us
  other arithmetic: 11.1 us -> 18 us
  waiting for transfers between devices: 41.4 us -> 34.8 us
  starting transfers between devices: 17.7 us -> 13.3 us
  local copies, waits for them, and re-layouts: 4.61 us -> 7.42 us
    all_to_all x1 -> x0, blocking collectives: 14.6 us -> none  [local(): lax.all_to_all(weighted, 'vol', split_axis=0, concat_axis=0, tiled=True)]
    all_to_all x3 -> x2, waiting for transfers between devices: 9.38 us -> 0.35 us  [the longest x1 0.35 us: local(): lax.all_to_all(rows, 'vol', split_axis=0, concat_axis=0, tiled=True)]
    dot_general x7 -> x3, matrix products: 8.19 us -> 0.98 us  [the longest x1 0.36 us: local(): prediction = jnp.dot(matrix, extract, preferred_element_type=jnp.float32)]
    convert_element_type x1 -> x6, other arithmetic: 0.03 us -> 5.23 us  [the longest x2 2.31 us: dft_tables(): jnp.cos(angle).astype(jnp.bfloat16)]
    all_to_all x3 -> x2, starting transfers between devices: 17.5 us -> 13.3 us  [the longest x1 7.28 us: local(): lax.all_to_all(meta, 'vol', split_axis=0, concat_axis=0, tiled=True)]
    psum x1, waiting for transfers between devices: 32 us -> 34.4 us  [local(): gradient = lax.psum(gradient, 'ptcl')]
    neg x1, other arithmetic: 1.47 us -> 3.56 us  [ctf_rows(): -jnp.sin(math.pi * focus.astype(jnp.float32)[..., None] * radius + phase_...]
    concatenate x0 -> x1, local copies, waits for them, and re-layouts: none -> 1.87 us  [local(): jnp.concatenate([tap_ids.astype(jnp.float32), weights.astype(jnp.float32)...]
  transfers between devices with their start and end apart: 4 -> 3, of which waited for: 3 -> 2; matrix products, arithmetic and copies ran while one was open for 13% -> 21% of each run, Pallas kernels for 0% -> 0%
where the time goes in v1:
time: 90.5 us; the launch traced here: 89.9 us
  waiting for transfers between devices  34.8 us (38%)
  other arithmetic  18 us (20%)
  between operations  14.3 us (16%)
  starting transfers between devices  13.3 us (15%)
  local copies, waits for them, and re-layouts  7.42 us (8%)
  matrix products  2.18 us (2%)
    psum x1, waiting for transfers between devices, local(): gradient = lax.psum(gradient, 'ptcl')  34.4 us
    all_to_all x1, starting transfers between devices, local(): lax.all_to_all(meta, 'vol', split_axis=0, concat_axis=0, tiled=True)  7.28 us
    all_to_all x1, starting transfers between devices, local(): lax.all_to_all(rows, 'vol', split_axis=0, concat_axis=0, tiled=True)  5.99 us
    reduce_sum x1, other arithmetic, tap_matrix(): return jnp.sum(picked, axis=1, dtype=jnp.bfloat16)  5.06 us
    neg x1, other arithmetic, ctf_rows(): -jnp.sin(math.pi * focus.astype(jnp.float32)[..., None] * radius + phase_...  3.56 us
    gather x1, local copies, waits for them, and re-layouts, local(): rows = observed[pixel_ids]  3.28 us
    convert_element_type x2, other arithmetic, dft_tables(): jnp.cos(angle).astype(jnp.bfloat16)  2.31 us
    sub x1, other arithmetic, local(): return volume - learn_rate * gradient  1.9 us
  transfers between devices with their start and end apart: 3, of which 2 were waited for; matrix products, arithmetic and copies ran while one was open for 21% of the time, Pallas kernels for 0%

profile of v1, /device:TPU:0, one launch (start us, length us, event | category | flops | bytes accessed | tf_op | source)
XLA Modules:
  0.0 89.9 jit_solution(17016676902778621159)
XLA Ops:
  7.2 0.7 compare_convert_fusion
  8.0 0.7 fusion.40
  8.7 0.8 convert_bitcast_fusion
  9.4 0.7 bitcast_convert_fusion
  10.2 1.9 %concatenate.12 = f32[8,19,96]{2,1,0:T(8,128)} concatenate(f32[8,8,96]{2,1,0:T(8,128)S(1)} %convert_bitcast_fusion, f32[8,8,96]{2,1,0:T(8,128)S(1)} %bitcast_convert_fusion, f32[8,1,96]{2,1,0:T(1,128)S(1)} %fusion.40, f32[8,1,96]{2,1,0:T(1,128)S(1)} %gather.6, f32[8,1,96]{2,1,0:T(1,128)S(1)} %compare_convert_fusion), dimensions={1} | concatenate | bytes 116736 | tf_op jit(solution)/shard_map/concatenate | solution.py:87
  12.0 7.3 %all-to-all-start = ((f32[8,19,96]{2,1,0:T(8,128)}), f32[8,19,96]{2,1,0:T(8,128)S(1)}, u32[]{:S(2)}, u32[]{:S(2)}) async-start(f32[8,19,96]{2,1,0:T(8,128)} %concatenate.12), calls=%async_computation | async-start | bytes 196608 | tf_op jit(solution)/shard_map/all_to_all | solution.py:97
  19.3 0.7 compare_select_fusion.2
  20.0 1.1 %cosine_convert_fusion = bf16[256,256]{1,0:T(8,128)(2,1)S(1)} fusion(s32[256]{0:T(256)S(1)} %iota_add_fusion), kind=kLoop, calls=%fused_computation.39 | loop fusion | flops 983040 | bytes 132096 | tf_op jit(solution)/shard_map/convert_element_type | solution.py:21
  21.1 1.3 %fusion.30 = (bf16[256,256]{1,0:T(8,128)(2,1)S(1)}, bf16[256,256]{1,0:T(8,128)(2,1)S(1)}) fusion(s32[256]{0:T(256)S(1)} %iota_add_fusion), kind=kLoop, calls=%fused_computation.49 | loop fusion | flops 1441792 | bytes 263168 | tf_op jit(solution)/shard_map/neg | solution.py:34
  22.4 1.3 %cosine_convert_fusion.1 = (bf16[1,256,256]{2,1,0:T(8,128)(2,1)S(1)}, bf16[1,256,256]{2,1,0:T(8,128)(2,1)S(1)}) fusion(s32[256]{0:T(256)S(1)} %iota_add_fusion), kind=kLoop, calls=%fused_computation.43 | loop fusion | flops 1048576 | bytes 263168 | tf_op jit(solution)/shard_map/convert_element_type | solution.py:21
  24.0 0.4 fusion.2
  24.4 0.5 copy.25
  25.0 3.3 %gather_fusion = bf16[768,256]{1,0:T(8,128)(2,1)} fusion(bf16[512,256]{1,0:T(8,128)(2,1)S(1)} %bitcast.54, s32[1024]{0:T(1024)S(1)} %pad_clamp_fusion), kind=kCustom, calls=%fused_computation | custom fusion | bytes 789504 | tf_op jit(solution)/shard_map/gather | solution.py:99
  28.2 6.0 %all-to-all-start.1 = ((bf16[8,96,256]{2,1,0:T(8,128)(2,1)}), bf16[8,96,256]{2,1,0:T(8,128)(2,1)S(1)}, u32[]{:S(2)}, u32[]{:S(2)}) async-start(bf16[8,96,256]{2,1,0:T(8,128)(2,1)} %bitcast.22), calls=%async_computation.1 | async-start | bytes 786432 | tf_op jit(solution)/shard_map/all_to_all | solution.py:100
  34.7 5.1 %fusion.1 = bf16[768,512]{1,0:T(8,128)(2,1)S(1)} fusion(s32[768,8]{1,0:T(8,128)S(1)} %bitcast.56, bf16[768,8]{1,0:T(8,128)(2,1)S(1)} %bitcast.59), kind=kLoop, calls=%fused_computation.3 | loop fusion | flops 9043968 | bytes 823296 | tf_op jit(solution)/shard_map/reduce_sum | solution.py:75
  39.7 3.6 %sine_negate_fusion = f32[8,96,128]{2,1,0:T(8,128)S(1)} fusion(f32[8,96]{1,0:T(8,128)S(1)} %fusion.39, s32[8,96]{1,0:T(8,128)S(1)} %fusion.35, f32[8,96]{1,0:T(8,128)S(1)} %bitcast.63), kind=kLoop, calls=%fused_computation.26 | loop fusion | flops 884736 | bytes 402432 | tf_op jit(solution)/shard_map/neg | solution.py:52
  43.3 0.3 mul.162
  43.6 0.6 mul.163
  44.3 0.4 copy-done.1
  44.6 0.4 convolution_convert_fusion
  45.0 0.3 all-to-all-done.1
  45.5 1.2 %fusion.48 = f32[512,256]{1,0:T(8,128)} fusion(bf16[768,512]{1,0:T(8,128)(2,1)S(1)} %fusion.1, bf16[768,256]{1,0:T(8,128)(2,1)S(1)} %bitcast.60), kind=kOutput, calls=%fused_computation.87 | convolution fusion | flops 201326592 | bytes 1703936 | tf_op jit(solution)/shard_map/dot_general | solution.py:112
  46.8 34.4 %all-reduce.2.cloned.1.call-done = f32[512,256]{1,0:T(8,128)} async-done(((f32[512,256]{1,0:T(8,128)}), f32[512,256]{1,0:T(8,128)}) %all-reduce.2.cloned.1.call-update) | async-done | bytes 524304 | tf_op jit(solution)/shard_map/psum | solution.py:115
  81.2 1.9 %sub.41 = f32[512,256]{1,0:T(8,128)} subtract(f32[512,256]{1,0:T(8,128)S(1)} %copy-done.1, f32[512,256]{1,0:T(8,128)} %all-reduce.2.cloned.1.call-done) | non-fusion elementwise | flops 131072 | bytes 1572864 | tf_op jit(solution)/shard_map/sub | solution.py:116
  (22 shorter events, 1.1 us)
Async XLA Ops:
  6.5 17.2 %copy-start = (bf16[1,256,256]{2,1,0:T(8,128)(2,1)S(1)}, bf16[1,256,256]{2,1,0:T(8,128)(2,1)}, u32[]{:S(2)}) copy-start(bf16[1,256,256]{2,1,0:T(8,128)(2,1)} %param.7) | copy-start | bytes 393220
  12.0 16.2 %all-to-all-start = ((f32[8,19,96]{2,1,0:T(8,128)}), f32[8,19,96]{2,1,0:T(8,128)S(1)}, u32[]{:S(2)}, u32[]{:S(2)}) async-start(f32[8,19,96]{2,1,0:T(8,128)} %concatenate.12), calls=%async_computation | async-start | bytes 196608 | tf_op jit(solution)/shard_map/all_to_all | solution.py:97
  28.2 17.1 %all-to-all-start.1 = ((bf16[8,96,256]{2,1,0:T(8,128)(2,1)}), bf16[8,96,256]{2,1,0:T(8,128)(2,1)S(1)}, u32[]{:S(2)}, u32[]{:S(2)}) async-start(bf16[8,96,256]{2,1,0:T(8,128)(2,1)} %bitcast.22), calls=%async_computation.1 | async-start | bytes 786432 | tf_op jit(solution)/shard_map/all_to_all | solution.py:100
  34.2 46.9 %all-reduce.2.cloned.1.call-start = ((), (), s32[]{:S(2)}) async-start(), calls=%async_computation.2 | async-start | bytes 1048576 | tf_op jit(solution)/shard_map/psum | solution.py:115
  43.6 1.0 %copy-start.1 = (f32[512,256]{1,0:T(8,128)S(1)}, f32[512,256]{1,0:T(8,128)}, u32[]{:S(2)}) copy-start(f32[512,256]{1,0:T(8,128)} %param.9) | copy-start | bytes 1572868
Sparse Core Ops, SparseCore 0:
  46.9 34.2 all-reduce.1

commit v2 on v1

--- a/solution.py
+++ b/solution.py
@@ -112,8 +112,15 @@
     gradient = lax.dot_general(
         matrix, flat_residual, (((0,), (0,)), ((), ())), preferred_element_type=jnp.float32
     )
-    gradient = lax.psum(gradient, "ptcl")
-    return volume - learn_rate * gradient
+    shards = lax.axis_size("ptcl")
+    parts = gradient.astype(jnp.bfloat16).reshape(shards, -1, gradient.shape[1])
+    got_parts = lax.all_to_all(parts, "ptcl", split_axis=0, concat_axis=0, tiled=True)
+    quarter = jnp.sum(got_parts.astype(jnp.float32), axis=0)
+    rows_each = quarter.shape[0]
+    start = lax.axis_index("ptcl") * rows_each
+    mine = lax.dynamic_slice_in_dim(volume, start, rows_each, axis=0)
+    updated = mine - learn_rate * quarter
+    return lax.all_gather(updated, "ptcl", axis=0, tiled=True)
 
 
 def solution(mesh):

time: 90.5 us -> 56.9 us (0.63)
  waiting for transfers between devices: 34.8 us -> 6.39 us
  between operations: 14.3 us -> 0.88 us
  blocking collectives: 0 us -> 6.58 us
  starting transfers between devices: 13.3 us -> 16.7 us
  other arithmetic: 18 us -> 15.5 us
    psum x1 -> x0, waiting for transfers between devices: 34.4 us -> none  [local(): gradient = lax.psum(gradient, 'ptcl')]
    all_gather x0 -> x1, blocking collectives: none -> 6.58 us  [local(): return lax.all_gather(updated, 'ptcl', axis=0, tiled=True)]
    all_to_all x0 -> x1, waiting for transfers between devices: none -> 6 us  [local(): lax.all_to_all(parts, 'ptcl', split_axis=0, concat_axis=0, tiled=True)]
    all_to_all x0 -> x1, starting transfers between devices: none -> 3.41 us  [local(): lax.all_to_all(parts, 'ptcl', split_axis=0, concat_axis=0, tiled=True)]
    sub x1, other arithmetic: 1.9 us -> 0.02 us  [local(): updated = mine - learn_rate * quarter]
  transfers between devices with their start and end apart: 3 -> 3, of which waited for: 2 -> 2; matrix products, arithmetic and copies ran while one was open for 21% -> 33% of each run, Pallas kernels for 0% -> 0%
where the time goes in v2:
time: 56.9 us; the launch traced here: 56.3 us
  starting transfers between devices  16.7 us (29%)
  other arithmetic  15.5 us (27%)
  local copies, waits for them, and re-layouts  8.21 us (14%)
  blocking collectives  6.58 us (12%)
  waiting for transfers between devices  6.39 us (11%)
  matrix products  2.1 us (4%)
  between operations  0.88 us (2%)
    all_to_all x1, starting transfers between devices, local(): lax.all_to_all(meta, 'vol', split_axis=0, concat_axis=0, tiled=True)  7.28 us
    all_gather x1, blocking collectives, local(): return lax.all_gather(updated, 'ptcl', axis=0, tiled=True)  6.58 us
    all_to_all x1, waiting for transfers between devices, local(): lax.all_to_all(parts, 'ptcl', split_axis=0, concat_axis=0, tiled=True)  6 us
    all_to_all x1, starting transfers between devices, local(): lax.all_to_all(rows, 'vol', split_axis=0, concat_axis=0, tiled=True)  5.98 us
    reduce_sum x1, other arithmetic, tap_matrix(): return jnp.sum(picked, axis=1, dtype=jnp.bfloat16)  5.06 us
    neg x1, other arithmetic, ctf_rows(): -jnp.sin(math.pi * focus.astype(jnp.float32)[..., None] * radius + phase_...  3.56 us
    all_to_all x1, starting transfers between devices, local(): lax.all_to_all(parts, 'ptcl', split_axis=0, concat_axis=0, tiled=True)  3.41 us
    gather x1, local copies, waits for them, and re-layouts, local(): rows = observed[pixel_ids]  3.27 us
  transfers between devices with their start and end apart: 3, of which 2 were waited for; matrix products, arithmetic and copies ran while one was open for 33% of the time, Pallas kernels for 0%

profile of v2, /device:TPU:0, one launch (start us, length us, event | category | flops | bytes accessed | tf_op | source)
XLA Modules:
  0.0 56.3 jit_solution(14978185410191173415)
XLA Ops:
  0.0 0.8 %bitcast_convert_fusion = f32[8,8,96]{2,1,0:T(8,128)S(1)} fusion(bf16[1,1,8,8,96]{4,3,2,1,0:T(8,128)(2,1)} %param.13), kind=kLoop, calls=%fused_computation.62 | loop fusion | flops 6144 | bytes 36864 | tf_op jit(solution)/shard_map/convert_element_type | solution.py:90
  0.8 0.8 %convert_bitcast_fusion = f32[8,8,96]{2,1,0:T(8,128)S(1)} fusion(s32[1,1,8,8,96]{4,3,2,1,0:T(8,128)} %param.12), kind=kLoop, calls=%fused_computation.58 | loop fusion | flops 6144 | bytes 49152 | tf_op jit(solution)/shard_map/convert_element_type | solution.py:89
  2.2 0.7 %compare_convert_fusion = f32[8,1,96]{2,1,0:T(1,128)S(1)} fusion(s32[8]{0:T(128)} %bitcast.67), kind=kLoop, calls=%fused_computation.63 | loop fusion | flops 1536 | bytes 3104 | tf_op jit(solution)/shard_map/convert_element_type | solution.py:93
  2.9 0.7 %fusion.40 = f32[8,1,96]{2,1,0:T(1,128)S(1)} fusion(s32[8,1,96]{2,1,0:T(1,128)} %bitcast.65), kind=kLoop, calls=%fused_computation.76 | loop fusion | flops 9216 | bytes 6144 | tf_op jit(solution)/shard_map/convert_element_type | solution.py:91
  3.6 1.9 %concatenate.12 = f32[8,19,96]{2,1,0:T(8,128)} concatenate(f32[8,8,96]{2,1,0:T(8,128)S(1)} %convert_bitcast_fusion, f32[8,8,96]{2,1,0:T(8,128)S(1)} %bitcast_convert_fusion, f32[8,1,96]{2,1,0:T(1,128)S(1)} %fusion.40, f32[8,1,96]{2,1,0:T(1,128)S(1)} %gather.6, f32[8,1,96]{2,1,0:T(1,128)S(1)} %compare_convert_fusion), dimensions={1} | concatenate | bytes 116736 | tf_op jit(solution)/shard_map/concatenate | solution.py:87
  5.5 7.3 %all-to-all-start = ((f32[8,19,96]{2,1,0:T(8,128)}), f32[8,19,96]{2,1,0:T(8,128)S(1)}, u32[]{:S(2)}, u32[]{:S(2)}) async-start(f32[8,19,96]{2,1,0:T(8,128)} %concatenate.12), calls=%async_computation | async-start | bytes 196608 | tf_op jit(solution)/shard_map/all_to_all | solution.py:97
  12.8 1.3 %cosine_convert_fusion.1 = (bf16[1,256,256]{2,1,0:T(8,128)(2,1)S(1)}, bf16[1,256,256]{2,1,0:T(8,128)(2,1)S(1)}) fusion(s32[256]{0:T(256)S(1)} %iota_add_fusion), kind=kLoop, calls=%fused_computation.45 | loop fusion | flops 1048576 | bytes 263168 | tf_op jit(solution)/shard_map/convert_element_type | solution.py:21
  14.1 1.3 %fusion.30 = (bf16[256,256]{1,0:T(8,128)(2,1)S(1)}, bf16[256,256]{1,0:T(8,128)(2,1)S(1)}) fusion(s32[256]{0:T(256)S(1)} %iota_add_fusion), kind=kLoop, calls=%fused_computation.51 | loop fusion | flops 1441792 | bytes 263168 | tf_op jit(solution)/shard_map/neg | solution.py:34
  15.4 1.1 %cosine_convert_fusion = bf16[256,256]{1,0:T(8,128)(2,1)S(1)} fusion(s32[256]{0:T(256)S(1)} %iota_add_fusion), kind=kLoop, calls=%fused_computation.41 | loop fusion | flops 983040 | bytes 132096 | tf_op jit(solution)/shard_map/convert_element_type | solution.py:21
  16.7 0.4 fusion.2
  17.2 0.5 copy.25
  17.8 3.3 %gather_fusion = bf16[768,256]{1,0:T(8,128)(2,1)} fusion(bf16[512,256]{1,0:T(8,128)(2,1)S(1)} %bitcast.55, s32[1024]{0:T(1024)S(1)} %pad_clamp_fusion), kind=kCustom, calls=%fused_computation | custom fusion | bytes 789504 | tf_op jit(solution)/shard_map/gather | solution.py:99
  21.1 6.0 %all-to-all-start.1 = ((bf16[8,96,256]{2,1,0:T(8,128)(2,1)}), bf16[8,96,256]{2,1,0:T(8,128)(2,1)S(1)}, u32[]{:S(2)}, u32[]{:S(2)}) async-start(bf16[8,96,256]{2,1,0:T(8,128)(2,1)} %bitcast.22), calls=%async_computation.1 | async-start | bytes 786432 | tf_op jit(solution)/shard_map/all_to_all | solution.py:100
  27.4 5.1 %fusion.1 = bf16[768,512]{1,0:T(8,128)(2,1)S(1)} fusion(s32[768,8]{1,0:T(8,128)S(1)} %bitcast.57, bf16[768,8]{1,0:T(8,128)(2,1)S(1)} %bitcast.60), kind=kLoop, calls=%fused_computation.3 | loop fusion | flops 9043968 | bytes 823296 | tf_op jit(solution)/shard_map/reduce_sum | solution.py:75
  32.5 3.6 %sine_negate_fusion = f32[8,96,128]{2,1,0:T(8,128)S(1)} fusion(f32[8,96]{1,0:T(8,128)S(1)} %fusion.39, s32[8,96]{1,0:T(8,128)S(1)} %fusion.35, f32[8,96]{1,0:T(8,128)S(1)} %bitcast.64), kind=kLoop, calls=%fused_computation.28 | loop fusion | flops 884736 | bytes 402432 | tf_op jit(solution)/shard_map/neg | solution.py:52
  36.4 0.6 %mul.167 = f32[8,96,256]{2,1,0:T(8,128)S(1)} reshape(f32[8,96,2,128]{3,2,1,0:T(2,128)S(1)} %mul.166) | data formatting | bytes 1572864 | tf_op jit(solution)/shard_map/mul | solution.py:60
  37.0 0.4 copy-done.1
  37.4 0.4 convolution_convert_fusion
  37.8 0.4 all-to-all-done.1
  38.3 1.1 %convolution_convert_fusion.1 = bf16[512,256]{1,0:T(8,128)(2,1)} fusion(bf16[768,512]{1,0:T(8,128)(2,1)S(1)} %fusion.1, bf16[768,256]{1,0:T(8,128)(2,1)S(1)} %bitcast.61), kind=kOutput, calls=%fused_computation.5 | convolution fusion | flops 201457664 | bytes 1441792 | tf_op jit(solution)/shard_map/dot_general | solution.py:112
  39.5 3.4 %all-to-all-start.2 = ((bf16[4,128,256]{2,1,0:T(8,128)(2,1)}), bf16[4,128,256]{2,1,0:T(8,128)(2,1)S(1)}, u32[]{:S(2)}, u32[]{:S(2)}) async-start(bf16[4,128,256]{2,1,0:T(8,128)(2,1)} %bitcast.24), calls=%async_computation.2 | async-start | bytes 524288 | tf_op jit(solution)/shard_map/all_to_all | solution.py:117
  42.9 6.0 %all-to-all-done.2 = bf16[4,128,256]{2,1,0:T(8,128)(2,1)S(1)} async-done(((bf16[4,128,256]{2,1,0:T(8,128)(2,1)}), bf16[4,128,256]{2,1,0:T(8,128)(2,1)S(1)}, u32[]{:S(2)}, u32[]{:S(2)}) %all-to-all-start.2) | async-done | bytes 262176 | tf_op jit(solution)/shard_map/all_to_all | solution.py:117
  48.9 6.6 %all_gather.3 = f32[512,256]{1,0:T(8,128)S(1)} all-gather(f32[128,256]{1,0:T(8,128)S(1)} %dynamic-slice_subtract_fusion), channel_id=1, replica_groups=mesh['vol'=8,'ptcl'=4] {'ptcl'}, dimensions={0}, use_global_device_ids=true | all-gather | bytes 655360 | tf_op jit(solution)/shard_map/all_gather | solution.py:123
  55.5 0.8 %copy.36 = f32[512,256]{1,0:T(8,128)} copy(f32[512,256]{1,0:T(8,128)S(1)} %all_gather.3) | data formatting | bytes 1048576
  (26 shorter events, 1.3 us)
Async XLA Ops:
  0.0 16.4 %copy-start = (bf16[1,256,256]{2,1,0:T(8,128)(2,1)S(1)}, bf16[1,256,256]{2,1,0:T(8,128)(2,1)}, u32[]{:S(2)}) copy-start(bf16[1,256,256]{2,1,0:T(8,128)(2,1)} %param.7) | copy-start | bytes 393220
  0.0 16.4 %copy-start.2 = (s32[1,1,8,96]{3,2,1,0:T(8,128)S(1)}, s32[1,1,8,96]{3,2,1,0:T(8,128)}, u32[]{:S(2)}) copy-start(s32[1,1,8,96]{3,2,1,0:T(8,128)} %param.11) | copy-start | bytes 9220
  5.5 15.5 %all-to-all-start = ((f32[8,19,96]{2,1,0:T(8,128)}), f32[8,19,96]{2,1,0:T(8,128)S(1)}, u32[]{:S(2)}, u32[]{:S(2)}) async-start(f32[8,19,96]{2,1,0:T(8,128)} %concatenate.12), calls=%async_computation | async-start | bytes 196608 | tf_op jit(solution)/shard_map/all_to_all | solution.py:97
  21.1 17.1 %all-to-all-start.1 = ((bf16[8,96,256]{2,1,0:T(8,128)(2,1)}), bf16[8,96,256]{2,1,0:T(8,128)(2,1)S(1)}, u32[]{:S(2)}, u32[]{:S(2)}) async-start(bf16[8,96,256]{2,1,0:T(8,128)(2,1)} %bitcast.22), calls=%async_computation.1 | async-start | bytes 786432 | tf_op jit(solution)/shard_map/all_to_all | solution.py:100
  36.3 1.0 %copy-start.1 = (f32[512,256]{1,0:T(8,128)S(1)}, f32[512,256]{1,0:T(8,128)}, u32[]{:S(2)}) copy-start(f32[512,256]{1,0:T(8,128)} %param.9) | copy-start | bytes 1572868
  39.5 9.4 %all-to-all-start.2 = ((bf16[4,128,256]{2,1,0:T(8,128)(2,1)}), bf16[4,128,256]{2,1,0:T(8,128)(2,1)S(1)}, u32[]{:S(2)}, u32[]{:S(2)}) async-start(bf16[4,128,256]{2,1,0:T(8,128)(2,1)} %bitcast.24), calls=%async_computation.2 | async-start | bytes 524288 | tf_op jit(solution)/shard_map/all_to_all | solution.py:117

commit v3 on v2

v3 whole, which is shorter than its diff:
```python
import math

import jax
import jax.numpy as jnp
import ml_dtypes
import numpy as np
from jax import lax
from jax.sharding import PartitionSpec as P

L = 256
BLK = 128
PB = 512


learn_rate = 1.0
phase_shift = 0.1


def dft_tables():
    freq_ids = np.arange(L, dtype=np.int64)
    product = (freq_ids[:, None] - L // 2) * freq_ids[None, :] % L
    angle = np.float32(2.0 * math.pi / L) * product.astype(np.float32)
    cos_table = np.cos(angle.astype(np.float64)).astype(ml_dtypes.bfloat16)
    sin_table = np.sin(angle.astype(np.float64)).astype(ml_dtypes.bfloat16)
    first = np.stack([cos_table, sin_table])
    second = np.concatenate(
        [
            np.concatenate([cos_table, -sin_table], axis=1),
            np.concatenate([-sin_table, -cos_table], axis=1),
        ],
        axis=0,
    ).astype(np.float32) / L
    return first, second.astype(ml_dtypes.bfloat16)


def transform(pictures, first, second):
    rows = jnp.einsum(
        "iyx,jkx->ijyk", pictures, jnp.asarray(first), preferred_element_type=jnp.float32
    ).astype(jnp.bfloat16)
    count_img = pictures.shape[0]
    rows = rows.reshape(count_img, 2 * L, L)
    parts = jnp.einsum(
        "ay,iyb->iab", jnp.asarray(second), rows, preferred_element_type=jnp.float32
    )
    parts = parts.reshape(count_img, 2, L, L // BLK, BLK)
    blocks = jnp.transpose(parts, (0, 2, 3, 1, 4))
    return blocks.reshape(count_img * PB, 2 * BLK).astype(jnp.bfloat16)


def ctf_rows(block_id, focus):
    row_id = block_id // (L // BLK)
    col_id = block_id % (L // BLK) * BLK
    lane_ids = jnp.arange(BLK, dtype=jnp.int32)
    freq_y = (row_id - L // 2).astype(jnp.float32) / L
    freq_x = (col_id[..., None] + lane_ids - L // 2).astype(jnp.float32) / L
    radius = freq_x * freq_x + (freq_y * freq_y)[..., None]
    return -jnp.sin(math.pi * focus.astype(jnp.float32)[..., None] * radius + phase_shift)


def residual_terms(prediction, observed, ctf_values, live_slots):
    shape = prediction.shape
    pred_wide = prediction.astype(jnp.float32).reshape(shape[:-1] + (2, BLK))
    obs_wide = observed.astype(jnp.float32).reshape(shape[:-1] + (2, BLK))
    factor = ctf_values[..., None, :]
    misfit = factor * (factor * pred_wide - obs_wide)
    misfit = jnp.where(live_slots[..., None, None], misfit, 0.0)
    return misfit.reshape(shape).astype(jnp.bfloat16)


def tap_matrix_t(tap_ids, weights, block_count):
    owners, taps, slots = tap_ids.shape
    flat_taps = jnp.transpose(tap_ids, (1, 0, 2)).reshape(taps, owners * slots)
    flat_weights = jnp.transpose(weights, (1, 0, 2)).reshape(taps, owners * slots)
    block_ids = jnp.arange(block_count, dtype=jnp.int32)
    picked = jnp.where(
        flat_taps[:, None, :] == block_ids[None, :, None],
        flat_weights[:, None, :],
        jnp.zeros((), jnp.bfloat16),
    )
    return jnp.sum(picked, axis=0, dtype=jnp.bfloat16)


def split_whole(values):
    return (values // 256).astype(jnp.bfloat16), (values % 256).astype(jnp.bfloat16)


def local(images, defocus, volume, counts, slot_pixel, slot_taps, slot_weights):
    first, second = dft_tables()
    extract = volume.astype(jnp.bfloat16)
    width = volume.shape[1]
    slot_count = counts[0, 0]
    pixel_ids = slot_pixel[0, 0]
    tap_ids = slot_taps[0, 0]
    weights = slot_weights[0, 0]
    owners, taps, capacity = tap_ids.shape
    live_slots = jnp.arange(capacity, dtype=jnp.int32)[None, :] < slot_count[:, None]
    observed = transform(images, first, second)
    flat_pixels = pixel_ids.reshape(-1)
    onehot = (flat_pixels[:, None] == jnp.arange(observed.shape[0], dtype=jnp.int32)[None, :])
    rows = jnp.dot(onehot.astype(jnp.bfloat16), observed, preferred_element_type=jnp.float32)
    rows = rows.astype(jnp.bfloat16).reshape(owners, capacity, width)
    tap_hi, tap_lo = split_whole(tap_ids)
    block_hi, block_lo = split_whole(pixel_ids % PB)
    meta = jnp.concatenate(
        [
            tap_hi,
            tap_lo,
            weights,
            block_hi[:, None, :],
            block_lo[:, None, :],
            defocus[pixel_ids // PB][:, None, :],
            live_slots.astype(jnp.bfloat16)[:, None, :],
        ],
        axis=1,
    )
    fields = meta.shape[1]
    meta_rows = -(-fields * capacity // width)
    flat_meta = meta.reshape(owners, fields * capacity)
    flat_meta = jnp.pad(flat_meta, ((0, 0), (0, meta_rows * width - fields * capacity)))
    packet = jnp.concatenate([rows, flat_meta.reshape(owners, meta_rows, width)], axis=1)
    got = lax.all_to_all(packet, "vol", split_axis=0, concat_axis=0, tiled=True)
    got_rows = got[:, :capacity]
    got_meta = got[:, capacity:].reshape(owners, meta_rows * width)[:, : fields * capacity]
    got_meta = got_meta.reshape(owners, fields, capacity)
    whole = got_meta[:, : 2 * taps].astype(jnp.int32)
    got_taps = whole[:, :taps] * 256 + whole[:, taps:]
    got_weights = got_meta[:, 2 * taps : 3 * taps]
    block_parts = got_meta[:, 3 * taps : 3 * taps + 2].astype(jnp.int32)
    got_block = block_parts[:, 0] * 256 + block_parts[:, 1]
    got_focus = got_meta[:, 3 * taps + 2]
    got_live = got_meta[:, 3 * taps + 3] > 0.5
    matrix_t = tap_matrix_t(got_taps, got_weights, volume.shape[0])
    prediction = lax.dot_general(
        matrix_t, extract, (((0,), (0,)), ((), ())), preferred_element_type=jnp.float32
    )
    prediction = prediction.astype(jnp.bfloat16).reshape(owners, capacity, -1)
    ctf_values = ctf_rows(got_block, got_focus)
    weighted = residual_terms(prediction, got_rows, ctf_values, got_live)
    flat_residual = weighted.reshape(-1, width)
    gradient = jnp.dot(matrix_t, flat_residual, preferred_element_type=jnp.float32)
    shards = lax.axis_size("ptcl")
    parts = gradient.astype(jnp.bfloat16).reshape(shards, -1, gradient.shape[1])
    got_parts = lax.all_to_all(parts, "ptcl", split_axis=0, concat_axis=0, tiled=True)
    quarter = jnp.sum(got_parts.astype(jnp.float32), axis=0)
    rows_each = quarter.shape[0]
    start = lax.axis_index("ptcl") * rows_each
    mine = lax.dynamic_slice_in_dim(volume, start, rows_each, axis=0)
    updated = mine - learn_rate * quarter
    return lax.all_gather(updated, "ptcl", axis=0, tiled=True)


def solution(mesh):
    placed = (
        P(("vol", "ptcl"), None, None),
        P(("vol", "ptcl")),
        P("vol", None),
        P("vol", "ptcl", None),
        P("vol", "ptcl", None, None),
        P("vol", "ptcl", None, None, None),
        P("vol", "ptcl", None, None, None),
    )
    return jax.shard_map(
        local, mesh=mesh, in_specs=placed, out_specs=P("vol", None), check_vma=False
    )
```

time: 56.9 us -> 53.4 us (0.938)
  blocking collectives: 6.58 us -> 26.9 us
  starting transfers between devices: 16.7 us -> 3.41 us
  other arithmetic: 15.5 us -> 7.85 us
  local copies, waits for them, and re-layouts: 8.21 us -> 4.4 us
  matrix products: 2.1 us -> 3.49 us
    all_to_all x0 -> x1, blocking collectives: none -> 20.3 us  [local(): got = lax.all_to_all(packet, 'vol', split_axis=0, concat_axis=0, tiled=True)]
    all_to_all x2 -> x0, starting transfers between devices: 13.3 us -> none  [the longest x1 7.28 us: local(): lax.all_to_all(meta, 'vol', split_axis=0, concat_axis=0, tiled=True)]
    reduce_sum x1, other arithmetic: 5.06 us -> 1.66 us  [tap_matrix_t(): return jnp.sum(picked, axis=0, dtype=jnp.bfloat16)]
    gather x2 -> x0, local copies, waits for them, and re-layouts: 3.27 us -> none  [the longest x1 3.27 us: local(): rows = observed[pixel_ids]]
    convert_element_type x6, other arithmetic: 5.28 us -> 2.29 us  [the longest x2 1.52 us: split_whole(): (values % 256).astype(jnp.bfloat16)]
    dot_general x4 -> x5, matrix products: 2.1 us -> 3.49 us  [the longest x1 1.21 us: transform(): jnp.einsum('iyx,jkx->ijyk', pictures, jnp.asarray(first), preferred_eleme...]
    neg x1 -> x0, other arithmetic: 1.28 us -> none  [transform(): -sin_table]
    concatenate x1, local copies, waits for them, and re-layouts: 1.87 us -> 0.8 us  [local(): jnp.concatenate([tap_hi, tap_lo, weights, block_hi[:, None, :], block_lo[...]
  transfers between devices with their start and end apart: 3 -> 1, of which waited for: 2 -> 1; matrix products, arithmetic and copies ran while one was open for 33% -> 0% of each run, Pallas kernels for 0% -> 0%
where the time goes in v3:
time: 53.4 us; the launch traced here: 53 us
  blocking collectives  26.9 us (50%)
  other arithmetic  7.85 us (15%)
  waiting for transfers between devices  6 us (11%)
  local copies, waits for them, and re-layouts  4.4 us (8%)
  matrix products  3.49 us (7%)
  starting transfers between devices  3.41 us (6%)
  between operations  0.93 us (2%)
    all_to_all x1, blocking collectives, local(): got = lax.all_to_all(packet, 'vol', split_axis=0, concat_axis=0, tiled=True)  20.3 us
    all_gather x1, blocking collectives, local(): return lax.all_gather(updated, 'ptcl', axis=0, tiled=True)  6.58 us
    all_to_all x1, waiting for transfers between devices, local(): lax.all_to_all(parts, 'ptcl', split_axis=0, concat_axis=0, tiled=True)  6 us
    neg x1, other arithmetic, ctf_rows(): -jnp.sin(math.pi * focus.astype(jnp.float32)[..., None] * radius + phase_...  3.56 us
    all_to_all x1, starting transfers between devices, local(): lax.all_to_all(parts, 'ptcl', split_axis=0, concat_axis=0, tiled=True)  3.41 us
    reduce_sum x1, other arithmetic, tap_matrix_t(): return jnp.sum(picked, axis=0, dtype=jnp.bfloat16)  1.66 us
    convert_element_type x2, other arithmetic, split_whole(): (values % 256).astype(jnp.bfloat16)  1.52 us
    dot_general x1, matrix products, transform(): jnp.einsum('iyx,jkx->ijyk', pictures, jnp.asarray(first), preferred_eleme...  1.21 us
  transfers between devices with their start and end apart: 1, of which 1 were waited for; matrix products, arithmetic and copies ran while one was open for 0% of the time, Pallas kernels for 0%

profile of v3, /device:TPU:0, one launch (start us, length us, event | category | flops | bytes accessed | tf_op | source)
XLA Modules:
  0.0 53.0 jit_solution(12773775913098607957)
XLA Ops:
  0.0 0.8 %eq.36 = s32[768]{0:T(1024)S(1)} reshape(s32[1,1,8,96]{3,2,1,0:T(8,128)} %param.13) | data formatting | bytes 6144 | tf_op jit(solution)/shard_map/eq | solution.py:99
  0.8 0.7 %fusion.25 = (bf16[8,1,96]{2,1,0:T(2,128)(2,1)S(1)}, s32[8,1,96]{2,1,0:T(1,128)S(1)}, s32[8,1,96]{2,1,0:T(1,128)S(1)}) fusion(s32[8,1,96]{2,1,0:T(1,128)} %bitcast.86), kind=kLoop, calls=%fused_computation.61 | loop fusion | flops 17664 | bytes 10752 | tf_op jit(solution)/shard_map/convert_element_type | solution.py:84
  1.6 0.8 %fusion.15 = (bf16[8,8,96]{2,1,0:T(8,128)(2,1)S(1)}, bf16[8,8,96]{2,1,0:T(8,128)(2,1)S(1)}) fusion(s32[1,1,8,8,96]{4,3,2,1,0:T(8,128)} %param.14), kind=kLoop, calls=%fused_computation.31 | loop fusion | flops 129024 | bytes 49152 | tf_op jit(solution)/shard_map/convert_element_type | solution.py:84
  3.0 0.7 %compare_convert_fusion = bf16[8,1,96]{2,1,0:T(2,128)(2,1)S(1)} fusion(s32[8]{0:T(128)} %bitcast.89), kind=kLoop, calls=%fused_computation.44 | loop fusion | flops 1536 | bytes 1568 | tf_op jit(solution)/shard_map/convert_element_type | solution.py:112
  3.8 0.8 %concatenate.6 = bf16[8,28,96]{2,1,0:T(8,128)(2,1)S(1)} concatenate(bf16[8,8,96]{2,1,0:T(8,128)(2,1)S(1)} %get-tuple-element.9, bf16[8,8,96]{2,1,0:T(8,128)(2,1)S(1)} %get-tuple-element.8, bf16[8,8,96]{2,1,0:T(8,128)(2,1)} %bitcast.87, bf16[8,1,96]{2,1,0:T(2,128)(2,1)S(1)} %fusion.29, bf16[8,1,96]{2,1,0:T(2,128)(2,1)S(1)} %get-tuple-element.5, ...), dimensions={1} | concatenate | bytes 86016 | tf_op jit(solution)/shard_map/concatenate | solution.py:104
  4.6 0.1 reshape.306
  4.8 1.2 %convolution_convert_fusion.3 = bf16[2,256,256]{1,2,0:T(8,128)(2,1)S(1)} fusion(bf16[2,256,256]{2,1,0:T(8,128)(2,1)} %constant.116.clone, bf16[1,256,256]{2,1,0:T(8,128)(2,1)S(1)} %copy-done), kind=kOutput, calls=%fused_computation.9 | convolution fusion | flops 67239936 | bytes 655360 | tf_op jit(solution)/shard_map/iyx,jkx->ijyk/dot_general | solution.py:37
  6.0 0.4 fusion.4
  6.4 0.5 copy.34
  6.9 0.4 fusion.3
  7.4 20.3 %all_to_all.10 = bf16[8,107,256]{2,1,0:T(8,128)(2,1)S(1)} all-to-all(bf16[8,107,256]{2,1,0:T(8,128)(2,1)S(1)} %pad_maximum_fusion), channel_id=1, replica_groups=mesh['vol'=8,'ptcl'=4] {'vol'}, dimensions={0} | all-to-all | bytes 876544 | tf_op jit(solution)/shard_map/all_to_all | solution.py:121
  27.8 0.1 reshape.309
  28.0 3.6 %sine_negate_fusion = f32[8,96,128]{2,1,0:T(8,128)S(1)} fusion(f32[8,96]{1,0:T(8,128)S(1)} %fusion.24, s32[8,96]{1,0:T(8,128)S(1)} %fusion.20, f32[8,96]{1,0:T(8,128)S(1)} %bitcast.85), kind=kLoop, calls=%fused_computation.19 | loop fusion | flops 884736 | bytes 402432 | tf_op jit(solution)/shard_map/neg | solution.py:57
  31.6 0.3 mul.95
  31.9 0.6 %mul.96 = f32[8,96,256]{2,1,0:T(8,128)S(1)} reshape(f32[8,96,2,128]{3,2,1,0:T(2,128)S(1)} %mul.95) | data formatting | bytes 1572864 | tf_op jit(solution)/shard_map/mul | solution.py:65
  32.6 0.1 broadcast_in_dim.25
  32.7 1.7 %fusion.1 = bf16[512,768]{1,0:T(8,128)(2,1)S(1)} fusion(s32[8,768]{1,0:T(8,128)S(1)} %eq.40, bf16[8,768]{1,0:T(8,128)(2,1)S(1)} %broadcast_in_dim.25), kind=kLoop, calls=%fused_computation.2 | loop fusion | flops 9043968 | bytes 823296 | tf_op jit(solution)/shard_map/reduce_sum | solution.py:80
  34.4 0.4 convolution_convert_fusion
  34.8 0.2 fusion.8
  35.0 1.1 %convolution_convert_fusion.1 = bf16[512,256]{1,0:T(8,128)(2,1)} fusion(bf16[512,768]{1,0:T(8,128)(2,1)S(1)} %fusion.1, bf16[768,256]{1,0:T(8,128)(2,1)S(1)} %bitcast.76), kind=kOutput, calls=%fused_computation.7 | convolution fusion | flops 201457664 | bytes 1441792 | tf_op jit(solution)/shard_map/dot_general | solution.py:140
  36.1 3.4 %all-to-all-start.1 = ((bf16[4,128,256]{2,1,0:T(8,128)(2,1)}), bf16[4,128,256]{2,1,0:T(8,128)(2,1)S(1)}, u32[]{:S(2)}, u32[]{:S(2)}) async-start(bf16[4,128,256]{2,1,0:T(8,128)(2,1)} %bitcast.22), calls=%async_computation.1 | async-start | bytes 524288 | tf_op jit(solution)/shard_map/all_to_all | solution.py:143
  39.5 6.0 %all-to-all-done.1 = bf16[4,128,256]{2,1,0:T(8,128)(2,1)S(1)} async-done(((bf16[4,128,256]{2,1,0:T(8,128)(2,1)}), bf16[4,128,256]{2,1,0:T(8,128)(2,1)S(1)}, u32[]{:S(2)}, u32[]{:S(2)}) %all-to-all-start.1) | async-done | bytes 262176 | tf_op jit(solution)/shard_map/all_to_all | solution.py:143
  45.6 6.6 %all_gather.3 = f32[512,256]{1,0:T(8,128)S(1)} all-gather(f32[128,256]{1,0:T(8,128)S(1)} %dynamic-slice_subtract_fusion), channel_id=1, replica_groups=mesh['vol'=8,'ptcl'=4] {'ptcl'}, dimensions={0}, use_global_device_ids=true | all-gather | bytes 655360 | tf_op jit(solution)/shard_map/all_gather | solution.py:149
  52.2 0.8 %copy.50 = f32[512,256]{1,0:T(8,128)} copy(f32[512,256]{1,0:T(8,128)S(1)} %all_gather.3) | data formatting | bytes 1048576
  (30 shorter events, 0.4 us)
Async XLA Ops:
  0.0 4.8 %copy-start = (bf16[1,256,256]{2,1,0:T(8,128)(2,1)S(1)}, bf16[1,256,256]{2,1,0:T(8,128)(2,1)}, u32[]{:S(2)}) copy-start(bf16[1,256,256]{2,1,0:T(8,128)(2,1)} %param.9) | copy-start | bytes 393220
  0.0 6.0 %copy-start.2 = (bf16[512,512]{1,0:T(8,128)(2,1)S(1)}, bf16[512,512]{1,0:T(8,128)(2,1)}, u32[]{:S(2)}) copy-start(bf16[512,512]{1,0:T(8,128)(2,1)} %constant.117.clone) | copy-start | bytes 1572868
  32.5 1.9 %copy-start.1 = (f32[512,256]{1,0:T(8,128)S(1)}, f32[512,256]{1,0:T(8,128)}, u32[]{:S(2)}) copy-start(f32[512,256]{1,0:T(8,128)} %param.11) | copy-start | bytes 1572868
  36.1 9.4 %all-to-all-start.1 = ((bf16[4,128,256]{2,1,0:T(8,128)(2,1)}), bf16[4,128,256]{2,1,0:T(8,128)(2,1)S(1)}, u32[]{:S(2)}, u32[]{:S(2)}) async-start(bf16[4,128,256]{2,1,0:T(8,128)(2,1)} %bitcast.22), calls=%async_computation.1 | async-start | bytes 524288 | tf_op jit(solution)/shard_map/all_to_all | solution.py:143

commit v4 on v3

--- a/solution.py
+++ b/solution.py
@@ -94,11 +94,6 @@
     weights = slot_weights[0, 0]
     owners, taps, capacity = tap_ids.shape
     live_slots = jnp.arange(capacity, dtype=jnp.int32)[None, :] < slot_count[:, None]
-    observed = transform(images, first, second)
-    flat_pixels = pixel_ids.reshape(-1)
-    onehot = (flat_pixels[:, None] == jnp.arange(observed.shape[0], dtype=jnp.int32)[None, :])
-    rows = jnp.dot(onehot.astype(jnp.bfloat16), observed, preferred_element_type=jnp.float32)
-    rows = rows.astype(jnp.bfloat16).reshape(owners, capacity, width)
     tap_hi, tap_lo = split_whole(tap_ids)
     block_hi, block_lo = split_whole(pixel_ids % PB)
     meta = jnp.concatenate(
@@ -113,15 +108,13 @@
         ],
         axis=1,
     )
-    fields = meta.shape[1]
-    meta_rows = -(-fields * capacity // width)
-    flat_meta = meta.reshape(owners, fields * capacity)
-    flat_meta = jnp.pad(flat_meta, ((0, 0), (0, meta_rows * width - fields * capacity)))
-    packet = jnp.concatenate([rows, flat_meta.reshape(owners, meta_rows, width)], axis=1)
-    got = lax.all_to_all(packet, "vol", split_axis=0, concat_axis=0, tiled=True)
-    got_rows = got[:, :capacity]
-    got_meta = got[:, capacity:].reshape(owners, meta_rows * width)[:, : fields * capacity]
-    got_meta = got_meta.reshape(owners, fields, capacity)
+    got_meta = lax.all_to_all(meta, "vol", split_axis=0, concat_axis=0, tiled=True)
+    observed = transform(images, first, second)
+    flat_pixels = pixel_ids.reshape(-1)
+    onehot = (flat_pixels[:, None] == jnp.arange(observed.shape[0], dtype=jnp.int32)[None, :])
+    rows = jnp.dot(onehot.astype(jnp.bfloat16), observed, preferred_element_type=jnp.float32)
+    rows = rows.astype(jnp.bfloat16).reshape(owners, capacity, width)
+    got_rows = lax.all_to_all(rows, "vol", split_axis=0, concat_axis=0, tiled=True)
     whole = got_meta[:, : 2 * taps].astype(jnp.int32)
     got_taps = whole[:, :taps] * 256 + whole[:, taps:]
     got_weights = got_meta[:, 2 * taps : 3 * taps]

time: 53.4 us -> 53.5 us (level)
  blocking collectives: 26.9 us -> 6.58 us
  starting transfers between devices: 3.41 us -> 14.1 us
  waiting for transfers between devices: 6 us -> 12.7 us
  local copies, waits for them, and re-layouts: 4.4 us -> 6.41 us
  matrix products: 3.49 us -> 4.24 us
    all_to_all x1 -> x0, blocking collectives: 20.3 us -> none  [local(): got = lax.all_to_all(packet, 'vol', split_axis=0, concat_axis=0, tiled=True)]
    all_to_all x0 -> x2, starting transfers between devices: none -> 10.7 us  [the longest x1 7.28 us: local(): lax.all_to_all(meta, 'vol', split_axis=0, concat_axis=0, tiled=True)]
    all_to_all x0 -> x2, waiting for transfers between devices: none -> 6.72 us  [the longest x1 3.92 us: local(): lax.all_to_all(rows, 'vol', split_axis=0, concat_axis=0, tiled=True)]
    concatenate x1, local copies, waits for them, and re-layouts: 0.8 us -> 3.19 us  [local(): jnp.concatenate([tap_hi, tap_lo, weights, block_hi[:, None, :], block_lo[...]
    dot_general x1, matrix products: 0.44 us -> 1.19 us  [local(): jnp.dot(onehot.astype(jnp.bfloat16), observed, preferred_element_type=jnp...]
  transfers between devices with their start and end apart: 1 -> 3, of which waited for: 1 -> 3; matrix products, arithmetic and copies ran while one was open for 0% -> 21% of each run, Pallas kernels for 0% -> 0%
where the time goes in v4:
time: 53.5 us; the launch traced here: 52.9 us
  starting transfers between devices  14.1 us (26%)
  waiting for transfers between devices  12.7 us (24%)
  other arithmetic  7.81 us (15%)
  blocking collectives  6.58 us (12%)
  local copies, waits for them, and re-layouts  6.41 us (12%)
  matrix products  4.24 us (8%)
  between operations  0.95 us (2%)
    all_to_all x1, starting transfers between devices, local(): lax.all_to_all(meta, 'vol', split_axis=0, concat_axis=0, tiled=True)  7.28 us
    all_gather x1, blocking collectives, local(): return lax.all_gather(updated, 'ptcl', axis=0, tiled=True)  6.58 us
    all_to_all x1, waiting for transfers between devices, local(): lax.all_to_all(parts, 'ptcl', split_axis=0, concat_axis=0, tiled=True)  6 us
    all_to_all x1, waiting for transfers between devices, local(): lax.all_to_all(rows, 'vol', split_axis=0, concat_axis=0, tiled=True)  3.92 us
    neg x1, other arithmetic, ctf_rows(): -jnp.sin(math.pi * focus.astype(jnp.float32)[..., None] * radius + phase_...  3.56 us
    all_to_all x1, starting transfers between devices, local(): lax.all_to_all(rows, 'vol', split_axis=0, concat_axis=0, tiled=True)  3.45 us
    all_to_all x1, starting transfers between devices, local(): lax.all_to_all(parts, 'ptcl', split_axis=0, concat_axis=0, tiled=True)  3.41 us
    concatenate x1, local copies, waits for them, and re-layouts, local(): jnp.concatenate([tap_hi, tap_lo, weights, block_hi[:, None, :], block_lo[...  3.19 us
  transfers between devices with their start and end apart: 3, of which 3 were waited for; matrix products, arithmetic and copies ran while one was open for 21% of the time, Pallas kernels for 0%

profile of v4, /device:TPU:0, one launch (start us, length us, event | category | flops | bytes accessed | tf_op | source)
XLA Modules:
  0.0 52.9 jit_solution(12678046120495260193)
XLA Ops:
  0.7 0.7 %compare_convert_fusion = bf16[8,1,96]{2,1,0:T(2,128)(2,1)S(1)} fusion(s32[8]{0:T(128)} %bitcast.82), kind=kLoop, calls=%fused_computation.43 | loop fusion | flops 1536 | bytes 1568 | tf_op jit(solution)/shard_map/convert_element_type | solution.py:107
  1.5 0.7 %fusion.25 = (bf16[8,1,96]{2,1,0:T(2,128)(2,1)S(1)}, s32[8,1,96]{2,1,0:T(1,128)S(1)}, s32[8,1,96]{2,1,0:T(1,128)S(1)}) fusion(s32[8,1,96]{2,1,0:T(1,128)} %bitcast.80), kind=kLoop, calls=%fused_computation.60 | loop fusion | flops 17664 | bytes 10752 | tf_op jit(solution)/shard_map/convert_element_type | solution.py:84
  2.2 0.8 %fusion.15 = (bf16[8,8,96]{2,1,0:T(8,128)(2,1)S(1)}, bf16[8,8,96]{2,1,0:T(8,128)(2,1)S(1)}) fusion(s32[1,1,8,8,96]{4,3,2,1,0:T(8,128)} %param.14), kind=kLoop, calls=%fused_computation.30 | loop fusion | flops 129024 | bytes 49152 | tf_op jit(solution)/shard_map/convert_element_type | solution.py:84
  3.0 3.2 %concatenate.3 = bf16[8,28,96]{2,1,0:T(8,128)(2,1)} concatenate(bf16[8,8,96]{2,1,0:T(8,128)(2,1)S(1)} %get-tuple-element.9, bf16[8,8,96]{2,1,0:T(8,128)(2,1)S(1)} %get-tuple-element.8, bf16[8,8,96]{2,1,0:T(8,128)(2,1)} %bitcast.81, bf16[8,1,96]{2,1,0:T(2,128)(2,1)S(1)} %fusion.29, bf16[8,1,96]{2,1,0:T(2,128)(2,1)S(1)} %get-tuple-element.5, ...), dimensions={1} | concatenate | bytes 86016 | tf_op jit(solution)/shard_map/concatenate | solution.py:99
  6.2 7.3 %all-to-all-start = ((bf16[8,28,96]{2,1,0:T(8,128)(2,1)}), bf16[8,28,96]{2,1,0:T(8,128)(2,1)S(1)}, u32[]{:S(2)}, u32[]{:S(2)}) async-start(bf16[8,28,96]{2,1,0:T(8,128)(2,1)} %concatenate.3), calls=%async_computation | async-start | bytes 131072 | tf_op jit(solution)/shard_map/all_to_all | solution.py:111
  13.5 0.8 %eq.40 = s32[768]{0:T(1024)S(1)} reshape(s32[1,1,8,96]{3,2,1,0:T(8,128)} %param.13) | data formatting | bytes 6144 | tf_op jit(solution)/shard_map/eq | solution.py:114
  14.3 1.2 %convolution_convert_fusion.3 = bf16[2,256,256]{1,2,0:T(8,128)(2,1)S(1)} fusion(bf16[2,256,256]{2,1,0:T(8,128)(2,1)} %constant.115.clone, bf16[1,256,256]{2,1,0:T(8,128)(2,1)S(1)} %copy-done), kind=kOutput, calls=%fused_computation.9 | convolution fusion | flops 67239936 | bytes 655360 | tf_op jit(solution)/shard_map/iyx,jkx->ijyk/dot_general | solution.py:37
  15.5 0.4 fusion.4
  15.9 0.5 copy.20
  16.4 1.2 %fusion.3 = bf16[768,256]{1,0:T(8,128)(2,1)} fusion(s32[768]{0:T(1024)S(1)} %eq.40, bf16[64,8,2,128]{3,2,1,0:T(2,128)(2,1)S(1)} %bitcast.76), kind=kOutput, calls=%fused_computation.5 | convolution fusion | flops 201916416 | bytes 658432 | tf_op jit(solution)/shard_map/dot_general | solution.py:115
  17.6 2.8 %all-to-all-done = bf16[8,28,96]{2,1,0:T(8,128)(2,1)S(1)} async-done(((bf16[8,28,96]{2,1,0:T(8,128)(2,1)}), bf16[8,28,96]{2,1,0:T(8,128)(2,1)S(1)}, u32[]{:S(2)}, u32[]{:S(2)}) %all-to-all-start) | async-done | bytes 43040 | tf_op jit(solution)/shard_map/all_to_all | solution.py:111
  20.4 3.5 %all-to-all-start.1 = ((bf16[8,96,256]{2,1,0:T(8,128)(2,1)}), bf16[8,96,256]{2,1,0:T(8,128)(2,1)S(1)}, u32[]{:S(2)}, u32[]{:S(2)}) async-start(bf16[8,96,256]{2,1,0:T(8,128)(2,1)} %bitcast.19), calls=%async_computation.1 | async-start | bytes 786432 | tf_op jit(solution)/shard_map/all_to_all | solution.py:117
  24.0 3.6 %sine_negate_fusion = f32[8,96,128]{2,1,0:T(8,128)S(1)} fusion(f32[8,96]{1,0:T(8,128)S(1)} %fusion.24, s32[8,96]{1,0:T(8,128)S(1)} %fusion.20, f32[8,96]{1,0:T(8,128)S(1)} %bitcast.79), kind=kLoop, calls=%fused_computation.18 | loop fusion | flops 884736 | bytes 402432 | tf_op jit(solution)/shard_map/neg | solution.py:57
  27.8 0.3 mul.95
  28.1 0.6 %mul.96 = f32[8,96,256]{2,1,0:T(8,128)S(1)} reshape(f32[8,96,2,128]{3,2,1,0:T(2,128)S(1)} %mul.95) | data formatting | bytes 1572864 | tf_op jit(solution)/shard_map/mul | solution.py:65
  28.7 1.7 %fusion.1 = bf16[512,768]{1,0:T(8,128)(2,1)S(1)} fusion(s32[8,768]{1,0:T(8,128)S(1)} %eq.36, bf16[8,768]{1,0:T(8,128)(2,1)S(1)} %broadcast_in_dim.25), kind=kLoop, calls=%fused_computation.2 | loop fusion | flops 9043968 | bytes 823296 | tf_op jit(solution)/shard_map/reduce_sum | solution.py:80
  30.4 0.4 convolution_convert_fusion
  30.8 3.9 %all-to-all-done.1 = bf16[8,96,256]{2,1,0:T(8,128)(2,1)S(1)} async-done(((bf16[8,96,256]{2,1,0:T(8,128)(2,1)}), bf16[8,96,256]{2,1,0:T(8,128)(2,1)S(1)}, u32[]{:S(2)}, u32[]{:S(2)}) %all-to-all-start.1) | async-done | bytes 393248 | tf_op jit(solution)/shard_map/all_to_all | solution.py:117
  34.7 0.2 fusion.8
  34.9 1.1 %convolution_convert_fusion.1 = bf16[512,256]{1,0:T(8,128)(2,1)} fusion(bf16[512,768]{1,0:T(8,128)(2,1)S(1)} %fusion.1, bf16[768,256]{1,0:T(8,128)(2,1)S(1)} %bitcast.73), kind=kOutput, calls=%fused_computation.7 | convolution fusion | flops 201457664 | bytes 1441792 | tf_op jit(solution)/shard_map/dot_general | solution.py:133
  36.0 3.4 %all-to-all-start.2 = ((bf16[4,128,256]{2,1,0:T(8,128)(2,1)}), bf16[4,128,256]{2,1,0:T(8,128)(2,1)S(1)}, u32[]{:S(2)}, u32[]{:S(2)}) async-start(bf16[4,128,256]{2,1,0:T(8,128)(2,1)} %bitcast.21), calls=%async_computation.2 | async-start | bytes 524288 | tf_op jit(solution)/shard_map/all_to_all | solution.py:136
  39.4 6.0 %all-to-all-done.2 = bf16[4,128,256]{2,1,0:T(8,128)(2,1)S(1)} async-done(((bf16[4,128,256]{2,1,0:T(8,128)(2,1)}), bf16[4,128,256]{2,1,0:T(8,128)(2,1)S(1)}, u32[]{:S(2)}, u32[]{:S(2)}) %all-to-all-start.2) | async-done | bytes 262176 | tf_op jit(solution)/shard_map/all_to_all | solution.py:136
  45.5 6.6 %all_gather.3 = f32[512,256]{1,0:T(8,128)S(1)} all-gather(f32[128,256]{1,0:T(8,128)S(1)} %dynamic-slice_subtract_fusion), channel_id=1, replica_groups=mesh['vol'=8,'ptcl'=4] {'ptcl'}, dimensions={0}, use_global_device_ids=true | all-gather | bytes 655360 | tf_op jit(solution)/shard_map/all_gather | solution.py:142
  52.1 0.8 %copy.30 = f32[512,256]{1,0:T(8,128)} copy(f32[512,256]{1,0:T(8,128)S(1)} %all_gather.3) | data formatting | bytes 1048576
  (25 shorter events, 0.4 us)
Async XLA Ops:
  0.0 14.3 %copy-start = (bf16[1,256,256]{2,1,0:T(8,128)(2,1)S(1)}, bf16[1,256,256]{2,1,0:T(8,128)(2,1)}, u32[]{:S(2)}) copy-start(bf16[1,256,256]{2,1,0:T(8,128)(2,1)} %param.9) | copy-start | bytes 393220
  0.0 15.5 %copy-start.2 = (bf16[512,512]{1,0:T(8,128)(2,1)S(1)}, bf16[512,512]{1,0:T(8,128)(2,1)}, u32[]{:S(2)}) copy-start(bf16[512,512]{1,0:T(8,128)(2,1)} %constant.116.clone) | copy-start | bytes 1572868
  6.2 14.2 %all-to-all-start = ((bf16[8,28,96]{2,1,0:T(8,128)(2,1)}), bf16[8,28,96]{2,1,0:T(8,128)(2,1)S(1)}, u32[]{:S(2)}, u32[]{:S(2)}) async-start(bf16[8,28,96]{2,1,0:T(8,128)(2,1)} %concatenate.3), calls=%async_computation | async-start | bytes 131072 | tf_op jit(solution)/shard_map/all_to_all | solution.py:111
  20.4 14.3 %all-to-all-start.1 = ((bf16[8,96,256]{2,1,0:T(8,128)(2,1)}), bf16[8,96,256]{2,1,0:T(8,128)(2,1)S(1)}, u32[]{:S(2)}, u32[]{:S(2)}) async-start(bf16[8,96,256]{2,1,0:T(8,128)(2,1)} %bitcast.19), calls=%async_computation.1 | async-start | bytes 786432 | tf_op jit(solution)/shard_map/all_to_all | solution.py:117
  28.7 1.7 %copy-start.1 = (f32[512,256]{1,0:T(8,128)S(1)}, f32[512,256]{1,0:T(8,128)}, u32[]{:S(2)}) copy-start(f32[512,256]{1,0:T(8,128)} %param.11) | copy-start | bytes 1572868
  36.0 9.4 %all-to-all-start.2 = ((bf16[4,128,256]{2,1,0:T(8,128)(2,1)}), bf16[4,128,256]{2,1,0:T(8,128)(2,1)S(1)}, u32[]{:S(2)}, u32[]{:S(2)}) async-start(bf16[4,128,256]{2,1,0:T(8,128)(2,1)} %bitcast.21), calls=%async_computation.2 | async-start | bytes 524288 | tf_op jit(solution)/shard_map/all_to_all | solution.py:136

commit v5 on v4

--- a/solution.py
+++ b/solution.py
@@ -96,18 +96,22 @@
     live_slots = jnp.arange(capacity, dtype=jnp.int32)[None, :] < slot_count[:, None]
     tap_hi, tap_lo = split_whole(tap_ids)
     block_hi, block_lo = split_whole(pixel_ids % PB)
-    meta = jnp.concatenate(
-        [
-            tap_hi,
-            tap_lo,
-            weights,
-            block_hi[:, None, :],
-            block_lo[:, None, :],
-            defocus[pixel_ids // PB][:, None, :],
-            live_slots.astype(jnp.bfloat16)[:, None, :],
-        ],
-        axis=1,
-    )
+    pieces = [
+        tap_hi,
+        tap_lo,
+        weights,
+        block_hi[:, None, :],
+        block_lo[:, None, :],
+        defocus[pixel_ids // PB][:, None, :],
+        live_slots.astype(jnp.bfloat16)[:, None, :],
+    ]
+    fields = sum(piece.shape[1] for piece in pieces)
+    meta = jnp.zeros((owners, fields, capacity), jnp.bfloat16)
+    offset = 0
+    for piece in pieces:
+        rows_of = piece.shape[1]
+        meta = meta + jnp.pad(piece, ((0, 0), (offset, fields - offset - rows_of), (0, 0)))
+        offset += rows_of
     got_meta = lax.all_to_all(meta, "vol", split_axis=0, concat_axis=0, tiled=True)
     observed = transform(images, first, second)
     flat_pixels = pixel_ids.reshape(-1)

time: 53.5 us -> 51.8 us (0.968)
  local copies, waits for them, and re-layouts: 6.41 us -> 3.29 us
  other arithmetic: 7.81 us -> 9.22 us
    concatenate x1 -> x0, local copies, waits for them, and re-layouts: 3.19 us -> none  [local(): jnp.concatenate([tap_hi, tap_lo, weights, block_hi[:, None, :], block_lo[...]
    convert_element_type x2 -> x1, other arithmetic: 1.52 us -> 0.01 us  [split_whole(): (values % 256).astype(jnp.bfloat16)]
    convert_element_type x1 -> x2, other arithmetic: 0.02 us -> 1.53 us  [split_whole(): (values // 256).astype(jnp.bfloat16)]
    add x0 -> x1, other arithmetic: none -> 1.41 us  [local(): meta + jnp.pad(piece, ((0, 0), (offset, fields - offset - rows_of), (0, 0)))]
    lt x0 -> x1, other arithmetic: none -> 0.73 us  [local(): jnp.arange(capacity, dtype=jnp.int32)[None, :] < slot_count[:, None]]
    convert_element_type x1 -> x0, other arithmetic: 0.73 us -> none  [local(): live_slots.astype(jnp.bfloat16)[:, None, :]]
where the time goes in v5:
time: 51.8 us; the launch traced here: 51.1 us
  starting transfers between devices  14.1 us (27%)
  waiting for transfers between devices  12.7 us (25%)
  other arithmetic  9.22 us (18%)
  blocking collectives  6.58 us (13%)
  matrix products  4.24 us (8%)
  local copies, waits for them, and re-layouts  3.29 us (6%)
  between operations  0.95 us (2%)
    all_to_all x1, starting transfers between devices, local(): lax.all_to_all(meta, 'vol', split_axis=0, concat_axis=0, tiled=True)  7.28 us
    all_gather x1, blocking collectives, local(): return lax.all_gather(updated, 'ptcl', axis=0, tiled=True)  6.58 us
    all_to_all x1, waiting for transfers between devices, local(): lax.all_to_all(parts, 'ptcl', split_axis=0, concat_axis=0, tiled=True)  6 us
    all_to_all x1, waiting for transfers between devices, local(): lax.all_to_all(rows, 'vol', split_axis=0, concat_axis=0, tiled=True)  3.92 us
    neg x1, other arithmetic, ctf_rows(): -jnp.sin(math.pi * focus.astype(jnp.float32)[..., None] * radius + phase_...  3.56 us
    all_to_all x1, starting transfers between devices, local(): lax.all_to_all(rows, 'vol', split_axis=0, concat_axis=0, tiled=True)  3.45 us
    all_to_all x1, starting transfers between devices, local(): lax.all_to_all(parts, 'ptcl', split_axis=0, concat_axis=0, tiled=True)  3.41 us
    all_to_all x1, waiting for transfers between devices, local(): lax.all_to_all(meta, 'vol', split_axis=0, concat_axis=0, tiled=True)  2.8 us
  transfers between devices with their start and end apart: 3, of which 3 were waited for; matrix products, arithmetic and copies ran while one was open for 21% of the time, Pallas kernels for 0%

profile of v5, /device:TPU:0, one launch (start us, length us, event | category | flops | bytes accessed | tf_op | source)
XLA Modules:
  0.0 51.1 jit_solution(15496344457607084431)
XLA Ops:
  0.7 0.7 %iota_compare_fusion.5 = pred[8,1,96]{2,1,0:T(4,128)(4,1)S(1)} fusion(s32[8]{0:T(128)} %bitcast.80), kind=kLoop, calls=%fused_computation.69 | loop fusion | flops 768 | bytes 800 | tf_op jit(solution)/shard_map/lt | solution.py:96
  1.5 0.7 %fusion.30 = (bf16[8,1,96]{2,1,0:T(2,128)(2,1)S(1)}, s32[8,1,96]{2,1,0:T(1,128)S(1)}) fusion(s32[8,1,96]{2,1,0:T(1,128)} %bitcast.78), kind=kLoop, calls=%fused_computation.72 | loop fusion | flops 20736 | bytes 7680 | tf_op jit(solution)/shard_map/convert_element_type | solution.py:84
  2.2 0.8 %fusion.15 = (bf16[8,8,96]{2,1,0:T(8,128)(2,1)S(1)}, bf16[8,8,96]{2,1,0:T(8,128)(2,1)S(1)}) fusion(s32[1,1,8,8,96]{4,3,2,1,0:T(8,128)} %param.14), kind=kLoop, calls=%fused_computation.31 | loop fusion | flops 129024 | bytes 49152 | tf_op jit(solution)/shard_map/convert_element_type | solution.py:84
  3.1 1.4 %fusion.14 = bf16[8,28,96]{2,1,0:T(8,128)(2,1)} fusion(pred[8,1,96]{2,1,0:T(4,128)(4,1)S(1)} %iota_compare_fusion.5, bf16[8,1,96]{2,1,0:T(2,128)(2,1)S(1)} %fusion.26, bf16[8,1,96]{2,1,0:T(2,128)(2,1)S(1)} %get-tuple-element.5, bf16[8,8,96]{2,1,0:T(8,128)(2,1)} %bitcast.79, bf16[8,8,96]{2,1,0:T(8,128)(2,1)S(1)} %get-tuple-element.8, ...), kind=kLoop, calls=%fused_computation.25 | loop fusion | flops 322560 | bytes 83768 | tf_op jit(solution)/shard_map/add | solution.py:113
  4.5 7.3 %all-to-all-start = ((bf16[8,28,96]{2,1,0:T(8,128)(2,1)}), bf16[8,28,96]{2,1,0:T(8,128)(2,1)S(1)}, u32[]{:S(2)}, u32[]{:S(2)}) async-start(bf16[8,28,96]{2,1,0:T(8,128)(2,1)} %fusion.14), calls=%async_computation | async-start | bytes 131072 | tf_op jit(solution)/shard_map/all_to_all | solution.py:115
  11.8 0.8 %eq.40 = s32[768]{0:T(1024)S(1)} reshape(s32[1,1,8,96]{3,2,1,0:T(8,128)} %param.13) | data formatting | bytes 6144 | tf_op jit(solution)/shard_map/eq | solution.py:118
  12.6 1.2 %convolution_convert_fusion.3 = bf16[2,256,256]{1,2,0:T(8,128)(2,1)S(1)} fusion(bf16[2,256,256]{2,1,0:T(8,128)(2,1)} %constant.118.clone, bf16[1,256,256]{2,1,0:T(8,128)(2,1)S(1)} %copy-done), kind=kOutput, calls=%fused_computation.9 | convolution fusion | flops 67239936 | bytes 655360 | tf_op jit(solution)/shard_map/iyx,jkx->ijyk/dot_general | solution.py:37
  13.8 0.3 fusion.4
  14.2 0.5 copy.20
  14.7 1.2 %fusion.3 = bf16[768,256]{1,0:T(8,128)(2,1)} fusion(s32[768]{0:T(1024)S(1)} %eq.40, bf16[64,8,2,128]{3,2,1,0:T(2,128)(2,1)S(1)} %bitcast.74), kind=kOutput, calls=%fused_computation.5 | convolution fusion | flops 201916416 | bytes 658432 | tf_op jit(solution)/shard_map/dot_general | solution.py:119
  15.9 2.8 %all-to-all-done = bf16[8,28,96]{2,1,0:T(8,128)(2,1)S(1)} async-done(((bf16[8,28,96]{2,1,0:T(8,128)(2,1)}), bf16[8,28,96]{2,1,0:T(8,128)(2,1)S(1)}, u32[]{:S(2)}, u32[]{:S(2)}) %all-to-all-start) | async-done | bytes 43040 | tf_op jit(solution)/shard_map/all_to_all | solution.py:115
  18.7 3.5 %all-to-all-start.1 = ((bf16[8,96,256]{2,1,0:T(8,128)(2,1)}), bf16[8,96,256]{2,1,0:T(8,128)(2,1)S(1)}, u32[]{:S(2)}, u32[]{:S(2)}) async-start(bf16[8,96,256]{2,1,0:T(8,128)(2,1)} %bitcast.18), calls=%async_computation.1 | async-start | bytes 786432 | tf_op jit(solution)/shard_map/all_to_all | solution.py:121
  22.3 3.6 %sine_negate_fusion = f32[8,96,128]{2,1,0:T(8,128)S(1)} fusion(f32[8,96]{1,0:T(8,128)S(1)} %fusion.25, s32[8,96]{1,0:T(8,128)S(1)} %fusion.21, f32[8,96]{1,0:T(8,128)S(1)} %bitcast.77), kind=kLoop, calls=%fused_computation.18 | loop fusion | flops 884736 | bytes 402432 | tf_op jit(solution)/shard_map/neg | solution.py:57
  26.1 0.3 mul.95
  26.4 0.6 %mul.96 = f32[8,96,256]{2,1,0:T(8,128)S(1)} reshape(f32[8,96,2,128]{3,2,1,0:T(2,128)S(1)} %mul.95) | data formatting | bytes 1572864 | tf_op jit(solution)/shard_map/mul | solution.py:65
  27.0 1.7 %fusion.1 = bf16[512,768]{1,0:T(8,128)(2,1)S(1)} fusion(s32[8,768]{1,0:T(8,128)S(1)} %eq.36, bf16[8,768]{1,0:T(8,128)(2,1)S(1)} %broadcast_in_dim.22), kind=kLoop, calls=%fused_computation.2 | loop fusion | flops 9043968 | bytes 823296 | tf_op jit(solution)/shard_map/reduce_sum | solution.py:80
  28.7 0.4 convolution_convert_fusion
  29.1 3.9 %all-to-all-done.1 = bf16[8,96,256]{2,1,0:T(8,128)(2,1)S(1)} async-done(((bf16[8,96,256]{2,1,0:T(8,128)(2,1)}), bf16[8,96,256]{2,1,0:T(8,128)(2,1)S(1)}, u32[]{:S(2)}, u32[]{:S(2)}) %all-to-all-start.1) | async-done | bytes 393248 | tf_op jit(solution)/shard_map/all_to_all | solution.py:121
  33.0 0.2 fusion.8
  33.2 1.1 %convolution_convert_fusion.1 = bf16[512,256]{1,0:T(8,128)(2,1)} fusion(bf16[512,768]{1,0:T(8,128)(2,1)S(1)} %fusion.1, bf16[768,256]{1,0:T(8,128)(2,1)S(1)} %bitcast.71), kind=kOutput, calls=%fused_computation.7 | convolution fusion | flops 201457664 | bytes 1441792 | tf_op jit(solution)/shard_map/dot_general | solution.py:137
  34.3 3.4 %all-to-all-start.2 = ((bf16[4,128,256]{2,1,0:T(8,128)(2,1)}), bf16[4,128,256]{2,1,0:T(8,128)(2,1)S(1)}, u32[]{:S(2)}, u32[]{:S(2)}) async-start(bf16[4,128,256]{2,1,0:T(8,128)(2,1)} %bitcast.20), calls=%async_computation.2 | async-start | bytes 524288 | tf_op jit(solution)/shard_map/all_to_all | solution.py:140
  37.7 6.0 %all-to-all-done.2 = bf16[4,128,256]{2,1,0:T(8,128)(2,1)S(1)} async-done(((bf16[4,128,256]{2,1,0:T(8,128)(2,1)}), bf16[4,128,256]{2,1,0:T(8,128)(2,1)S(1)}, u32[]{:S(2)}, u32[]{:S(2)}) %all-to-all-start.2) | async-done | bytes 262176 | tf_op jit(solution)/shard_map/all_to_all | solution.py:140
  43.8 6.6 %all_gather.3 = f32[512,256]{1,0:T(8,128)S(1)} all-gather(f32[128,256]{1,0:T(8,128)S(1)} %dynamic-slice_subtract_fusion), channel_id=1, replica_groups=mesh['vol'=8,'ptcl'=4] {'ptcl'}, dimensions={0}, use_global_device_ids=true | all-gather | bytes 655360 | tf_op jit(solution)/shard_map/all_gather | solution.py:146
  50.4 0.8 %copy.30 = f32[512,256]{1,0:T(8,128)} copy(f32[512,256]{1,0:T(8,128)S(1)} %all_gather.3) | data formatting | bytes 1048576
  (25 shorter events, 0.5 us)
Async XLA Ops:
  0.0 12.6 %copy-start = (bf16[1,256,256]{2,1,0:T(8,128)(2,1)S(1)}, bf16[1,256,256]{2,1,0:T(8,128)(2,1)}, u32[]{:S(2)}) copy-start(bf16[1,256,256]{2,1,0:T(8,128)(2,1)} %param.9) | copy-start | bytes 393220
  0.0 13.8 %copy-start.2 = (bf16[512,512]{1,0:T(8,128)(2,1)S(1)}, bf16[512,512]{1,0:T(8,128)(2,1)}, u32[]{:S(2)}) copy-start(bf16[512,512]{1,0:T(8,128)(2,1)} %constant.119.clone) | copy-start | bytes 1572868
  4.5 14.2 %all-to-all-start = ((bf16[8,28,96]{2,1,0:T(8,128)(2,1)}), bf16[8,28,96]{2,1,0:T(8,128)(2,1)S(1)}, u32[]{:S(2)}, u32[]{:S(2)}) async-start(bf16[8,28,96]{2,1,0:T(8,128)(2,1)} %fusion.14), calls=%async_computation | async-start | bytes 131072 | tf_op jit(solution)/shard_map/all_to_all | solution.py:115
  18.7 14.3 %all-to-all-start.1 = ((bf16[8,96,256]{2,1,0:T(8,128)(2,1)}), bf16[8,96,256]{2,1,0:T(8,128)(2,1)S(1)}, u32[]{:S(2)}, u32[]{:S(2)}) async-start(bf16[8,96,256]{2,1,0:T(8,128)(2,1)} %bitcast.18), calls=%async_computation.1 | async-start | bytes 786432 | tf_op jit(solution)/shard_map/all_to_all | solution.py:121
  27.0 1.7 %copy-start.1 = (f32[512,256]{1,0:T(8,128)S(1)}, f32[512,256]{1,0:T(8,128)}, u32[]{:S(2)}) copy-start(f32[512,256]{1,0:T(8,128)} %param.11) | copy-start | bytes 1572868
  34.3 9.4 %all-to-all-start.2 = ((bf16[4,128,256]{2,1,0:T(8,128)(2,1)}), bf16[4,128,256]{2,1,0:T(8,128)(2,1)S(1)}, u32[]{:S(2)}, u32[]{:S(2)}) async-start(bf16[4,128,256]{2,1,0:T(8,128)(2,1)} %bitcast.20), calls=%async_computation.2 | async-start | bytes 524288 | tf_op jit(solution)/shard_map/all_to_all | solution.py:140

commit v6 on v5

--- a/solution.py
+++ b/solution.py
@@ -136,13 +136,24 @@
     flat_residual = weighted.reshape(-1, width)
     gradient = jnp.dot(matrix_t, flat_residual, preferred_element_type=jnp.float32)
     shards = lax.axis_size("ptcl")
-    parts = gradient.astype(jnp.bfloat16).reshape(shards, -1, gradient.shape[1])
+    partial = gradient.astype(jnp.bfloat16)
+    if shards in (2, 4):
+        arrived = [partial.astype(jnp.float32)]
+        for shift in range(1, shards):
+            pairs = [(i, (i + shift) % shards) for i in range(shards)]
+            arrived.append(lax.ppermute(partial, "ptcl", pairs).astype(jnp.float32))
+        if shards == 2:
+            total = arrived[0] + arrived[1]
+        else:
+            total = (arrived[0] + arrived[2]) + (arrived[1] + arrived[3])
+        return volume - learn_rate * total
+    parts = partial.reshape(shards, -1, gradient.shape[1])
     got_parts = lax.all_to_all(parts, "ptcl", split_axis=0, concat_axis=0, tiled=True)
-    quarter = jnp.sum(got_parts.astype(jnp.float32), axis=0)
-    rows_each = quarter.shape[0]
+    part_sum = jnp.sum(got_parts.astype(jnp.float32), axis=0)
+    rows_each = part_sum.shape[0]
     start = lax.axis_index("ptcl") * rows_each
     mine = lax.dynamic_slice_in_dim(volume, start, rows_each, axis=0)
-    updated = mine - learn_rate * quarter
+    updated = mine - learn_rate * part_sum
     return lax.all_gather(updated, "ptcl", axis=0, tiled=True)
 
 

time: 51.8 us -> 49.3 us (0.952)
  blocking collectives: 6.58 us -> 0 us
  waiting for transfers between devices: 12.7 us -> 19 us
  starting transfers between devices: 14.1 us -> 12.8 us
  other arithmetic: 9.22 us -> 10.1 us
  local copies, waits for them, and re-layouts: 3.29 us -> 2.5 us
  matrix products: 4.24 us -> 3.53 us
    ppermute x0 -> x3, waiting for transfers between devices: none -> 12.2 us  [local(): arrived.append(lax.ppermute(partial, 'ptcl', pairs).astype(jnp.float32))]
    all_gather x1 -> x0, blocking collectives: 6.58 us -> none  [local(): return lax.all_gather(updated, 'ptcl', axis=0, tiled=True)]
    all_to_all x1 -> x0, waiting for transfers between devices: 6 us -> none  [local(): lax.all_to_all(parts, 'ptcl', split_axis=0, concat_axis=0, tiled=True)]
    all_to_all x1 -> x0, starting transfers between devices: 3.41 us -> none  [local(): lax.all_to_all(parts, 'ptcl', split_axis=0, concat_axis=0, tiled=True)]
    ppermute x0 -> x3, starting transfers between devices: none -> 2.04 us  [local(): arrived.append(lax.ppermute(partial, 'ptcl', pairs).astype(jnp.float32))]
    sub x1, other arithmetic: 0.02 us -> 0.93 us  [local(): return volume - learn_rate * total]
    unnamed x7 -> x6, local copies, waits for them, and re-layouts: 0.81 us -> 0.01 us
    dot_general x1, matrix products: 1.08 us -> 0.37 us  [local(): jnp.dot(matrix_t, flat_residual, preferred_element_type=jnp.float32)]
  transfers between devices with their start and end apart: 3 -> 5, of which waited for: 3 -> 5; matrix products, arithmetic and copies ran while one was open for 21% -> 22% of each run, Pallas kernels for 0% -> 0%
where the time goes in v6:
time: 49.3 us; the launch traced here: 48.8 us
  waiting for transfers between devices  19 us (39%)
  starting transfers between devices  12.8 us (26%)
  other arithmetic  10.1 us (20%)
  matrix products  3.53 us (7%)
  local copies, waits for them, and re-layouts  2.5 us (5%)
  between operations  0.94 us (2%)
    ppermute x3, waiting for transfers between devices, local(): arrived.append(lax.ppermute(partial, 'ptcl', pairs).astype(jnp.float32))  12.2 us
    all_to_all x1, starting transfers between devices, local(): lax.all_to_all(meta, 'vol', split_axis=0, concat_axis=0, tiled=True)  7.28 us
    all_to_all x1, waiting for transfers between devices, local(): lax.all_to_all(rows, 'vol', split_axis=0, concat_axis=0, tiled=True)  3.92 us
    neg x1, other arithmetic, ctf_rows(): -jnp.sin(math.pi * focus.astype(jnp.float32)[..., None] * radius + phase_...  3.56 us
    all_to_all x1, starting transfers between devices, local(): lax.all_to_all(rows, 'vol', split_axis=0, concat_axis=0, tiled=True)  3.45 us
    all_to_all x1, waiting for transfers between devices, local(): lax.all_to_all(meta, 'vol', split_axis=0, concat_axis=0, tiled=True)  2.8 us
    ppermute x3, starting transfers between devices, local(): arrived.append(lax.ppermute(partial, 'ptcl', pairs).astype(jnp.float32))  2.04 us
    reduce_sum x1, other arithmetic, tap_matrix_t(): return jnp.sum(picked, axis=0, dtype=jnp.bfloat16)  1.66 us
  transfers between devices with their start and end apart: 5, of which 5 were waited for; matrix products, arithmetic and copies ran while one was open for 22% of the time, Pallas kernels for 0%

profile of v6, /device:TPU:0, one launch (start us, length us, event | category | flops | bytes accessed | tf_op | source)
XLA Modules:
  0.0 48.8 jit_solution(14875516194907540206)
XLA Ops:
  0.7 0.7 %iota_compare_fusion.5 = pred[8,1,96]{2,1,0:T(4,128)(4,1)S(1)} fusion(s32[8]{0:T(128)} %bitcast.79), kind=kLoop, calls=%fused_computation.68 | loop fusion | flops 768 | bytes 800 | tf_op jit(solution)/shard_map/lt | solution.py:96
  1.5 0.7 %fusion.30 = (bf16[8,1,96]{2,1,0:T(2,128)(2,1)S(1)}, s32[8,1,96]{2,1,0:T(1,128)S(1)}) fusion(s32[8,1,96]{2,1,0:T(1,128)} %bitcast.77), kind=kLoop, calls=%fused_computation.71 | loop fusion | flops 20736 | bytes 7680 | tf_op jit(solution)/shard_map/convert_element_type | solution.py:84
  2.2 0.8 %fusion.15 = (bf16[8,8,96]{2,1,0:T(8,128)(2,1)S(1)}, bf16[8,8,96]{2,1,0:T(8,128)(2,1)S(1)}) fusion(s32[1,1,8,8,96]{4,3,2,1,0:T(8,128)} %param.14), kind=kLoop, calls=%fused_computation.30 | loop fusion | flops 129024 | bytes 49152 | tf_op jit(solution)/shard_map/convert_element_type | solution.py:84
  3.1 1.4 %fusion.14 = bf16[8,28,96]{2,1,0:T(8,128)(2,1)} fusion(pred[8,1,96]{2,1,0:T(4,128)(4,1)S(1)} %iota_compare_fusion.5, bf16[8,1,96]{2,1,0:T(2,128)(2,1)S(1)} %fusion.26, bf16[8,1,96]{2,1,0:T(2,128)(2,1)S(1)} %get-tuple-element.5, bf16[8,8,96]{2,1,0:T(8,128)(2,1)} %bitcast.78, bf16[8,8,96]{2,1,0:T(8,128)(2,1)S(1)} %get-tuple-element.8, ...), kind=kLoop, calls=%fused_computation.24 | loop fusion | flops 322560 | bytes 83768 | tf_op jit(solution)/shard_map/add | solution.py:113
  4.5 7.3 %all-to-all-start = ((bf16[8,28,96]{2,1,0:T(8,128)(2,1)}), bf16[8,28,96]{2,1,0:T(8,128)(2,1)S(1)}, u32[]{:S(2)}, u32[]{:S(2)}) async-start(bf16[8,28,96]{2,1,0:T(8,128)(2,1)} %fusion.14), calls=%async_computation | async-start | bytes 131072 | tf_op jit(solution)/shard_map/all_to_all | solution.py:115
  11.8 0.8 %eq.40 = s32[768]{0:T(1024)S(1)} reshape(s32[1,1,8,96]{3,2,1,0:T(8,128)} %param.13) | data formatting | bytes 6144 | tf_op jit(solution)/shard_map/eq | solution.py:118
  12.6 1.2 %convolution_convert_fusion.3 = bf16[2,256,256]{1,2,0:T(8,128)(2,1)S(1)} fusion(bf16[2,256,256]{2,1,0:T(8,128)(2,1)} %constant.113.clone, bf16[1,256,256]{2,1,0:T(8,128)(2,1)S(1)} %copy-done), kind=kOutput, calls=%fused_computation.9 | convolution fusion | flops 67239936 | bytes 655360 | tf_op jit(solution)/shard_map/iyx,jkx->ijyk/dot_general | solution.py:37
  13.8 0.4 fusion.4
  14.2 0.5 %copy.20 = bf16[1,2,256,2,128]{4,1,3,2,0:T(2,128)(2,1)S(1)} copy(bf16[1,2,256,2,128]{2,1,4,3,0:T(2,128)(2,1)S(1)} %convert_element_type.154) | data formatting | bytes 524288 | tf_op jit(solution)/shard_map/convert_element_type | solution.py:47
  14.7 1.2 %fusion.3 = bf16[768,256]{1,0:T(8,128)(2,1)} fusion(s32[768]{0:T(1024)S(1)} %eq.40, bf16[64,8,2,128]{3,2,1,0:T(2,128)(2,1)S(1)} %bitcast.73), kind=kOutput, calls=%fused_computation.5 | convolution fusion | flops 201916416 | bytes 658432 | tf_op jit(solution)/shard_map/dot_general | solution.py:119
  15.9 2.8 %all-to-all-done = bf16[8,28,96]{2,1,0:T(8,128)(2,1)S(1)} async-done(((bf16[8,28,96]{2,1,0:T(8,128)(2,1)}), bf16[8,28,96]{2,1,0:T(8,128)(2,1)S(1)}, u32[]{:S(2)}, u32[]{:S(2)}) %all-to-all-start) | async-done | bytes 43040 | tf_op jit(solution)/shard_map/all_to_all | solution.py:115
  18.7 3.5 %all-to-all-start.1 = ((bf16[8,96,256]{2,1,0:T(8,128)(2,1)}), bf16[8,96,256]{2,1,0:T(8,128)(2,1)S(1)}, u32[]{:S(2)}, u32[]{:S(2)}) async-start(bf16[8,96,256]{2,1,0:T(8,128)(2,1)} %bitcast.18), calls=%async_computation.1 | async-start | bytes 786432 | tf_op jit(solution)/shard_map/all_to_all | solution.py:121
  22.3 3.6 %sine_negate_fusion = f32[8,96,128]{2,1,0:T(8,128)S(1)} fusion(f32[8,96]{1,0:T(8,128)S(1)} %fusion.25, s32[8,96]{1,0:T(8,128)S(1)} %fusion.21, f32[8,96]{1,0:T(8,128)S(1)} %bitcast.76), kind=kLoop, calls=%fused_computation.18 | loop fusion | flops 884736 | bytes 402432 | tf_op jit(solution)/shard_map/neg | solution.py:57
  26.4 0.6 %mul.92 = f32[8,96,256]{2,1,0:T(8,128)S(1)} reshape(f32[8,96,2,128]{3,2,1,0:T(2,128)S(1)} %mul.91) | data formatting | bytes 1572864 | tf_op jit(solution)/shard_map/mul | solution.py:65
  27.0 1.7 %fusion.1 = bf16[512,768]{1,0:T(8,128)(2,1)S(1)} fusion(s32[8,768]{1,0:T(8,128)S(1)} %eq.36, bf16[8,768]{1,0:T(8,128)(2,1)S(1)} %broadcast_in_dim.22), kind=kLoop, calls=%fused_computation.2 | loop fusion | flops 9043968 | bytes 823296 | tf_op jit(solution)/shard_map/reduce_sum | solution.py:80
  28.7 0.4 convolution_convert_fusion
  29.1 3.9 %all-to-all-done.1 = bf16[8,96,256]{2,1,0:T(8,128)(2,1)S(1)} async-done(((bf16[8,96,256]{2,1,0:T(8,128)(2,1)}), bf16[8,96,256]{2,1,0:T(8,128)(2,1)S(1)}, u32[]{:S(2)}, u32[]{:S(2)}) %all-to-all-start.1) | async-done | bytes 393248 | tf_op jit(solution)/shard_map/all_to_all | solution.py:121
  33.2 0.4 convolution_convert_fusion.1
  33.6 0.5 %collective-permute-start.1 = (bf16[512,256]{1,0:T(8,128)(2,1)S(1)}, bf16[512,256]{1,0:T(8,128)(2,1)S(1)}, u32[]{:S(2)}, u32[]{:S(2)}) collective-permute-start(bf16[512,256]{1,0:T(8,128)(2,1)S(1)} %convolution_convert_fusion.1), channel_id=1, source_target_pairs={{0,1},{1,2},{2,3},{3,0},{4,5},{5,6},{6,7},{7,4},{8,9},{9,10},{10,1... | collective-permute-start | bytes 786440 | tf_op jit(solution)/shard_map/ppermute | solution.py:144
  34.1 1.5 %collective-permute-start = (bf16[512,256]{1,0:T(8,128)(2,1)S(1)}, bf16[512,256]{1,0:T(8,128)(2,1)S(1)}, u32[]{:S(2)}, u32[]{:S(2)}) collective-permute-start(bf16[512,256]{1,0:T(8,128)(2,1)S(1)} %convolution_convert_fusion.1), channel_id=1, source_target_pairs={{0,2},{1,3},{2,0},{3,1},{4,6},{5,7},{6,4},{7,5},{8,10},{9,11},{10,... | collective-permute-start | bytes 786440 | tf_op jit(solution)/shard_map/ppermute | solution.py:144
  35.6 3.7 %collective-permute-done.2 = bf16[512,256]{1,0:T(8,128)(2,1)S(1)} collective-permute-done((bf16[512,256]{1,0:T(8,128)(2,1)S(1)}, bf16[512,256]{1,0:T(8,128)(2,1)S(1)}, u32[]{:S(2)}, u32[]{:S(2)}) %collective-permute-start.2) | collective-permute-done | bytes 262176 | tf_op jit(solution)/shard_map/ppermute | solution.py:144
  39.4 2.9 %collective-permute-done.1 = bf16[512,256]{1,0:T(8,128)(2,1)S(1)} collective-permute-done((bf16[512,256]{1,0:T(8,128)(2,1)S(1)}, bf16[512,256]{1,0:T(8,128)(2,1)S(1)}, u32[]{:S(2)}, u32[]{:S(2)}) %collective-permute-start.1) | collective-permute-done | bytes 262176 | tf_op jit(solution)/shard_map/ppermute | solution.py:144
  42.3 5.6 %collective-permute-done = bf16[512,256]{1,0:T(8,128)(2,1)S(1)} collective-permute-done((bf16[512,256]{1,0:T(8,128)(2,1)S(1)}, bf16[512,256]{1,0:T(8,128)(2,1)S(1)}, u32[]{:S(2)}, u32[]{:S(2)}) %collective-permute-start) | collective-permute-done | bytes 262176 | tf_op jit(solution)/shard_map/ppermute | solution.py:144
  47.9 0.9 %add_subtract_fusion = f32[512,256]{1,0:T(8,128)} fusion(f32[512,256]{1,0:T(8,128)S(1)} %copy-done.1, bf16[512,256]{1,0:T(8,128)(2,1)S(1)} %collective-permute-done.2, bf16[512,256]{1,0:T(8,128)(2,1)S(1)} %collective-permute-done.1, bf16[512,256]{1,0:T(8,128)(2,1)S(1)} %collective-permute-done, bf16[512,256]{1,0:T(8,128)(2,1)S(1)} %convolution_convert_fusion.1), kind=kLoop, calls=%fused_computation.17 | loop fusion | flops 1048576 | bytes 2097152 | tf_op jit(solution)/shard_map/sub | solution.py:149
  (26 shorter events, 1.0 us)
Async XLA Ops:
  0.0 12.6 %copy-start = (bf16[1,256,256]{2,1,0:T(8,128)(2,1)S(1)}, bf16[1,256,256]{2,1,0:T(8,128)(2,1)}, u32[]{:S(2)}) copy-start(bf16[1,256,256]{2,1,0:T(8,128)(2,1)} %param.9) | copy-start | bytes 393220
  0.0 13.8 %copy-start.2 = (bf16[512,512]{1,0:T(8,128)(2,1)S(1)}, bf16[512,512]{1,0:T(8,128)(2,1)}, u32[]{:S(2)}) copy-start(bf16[512,512]{1,0:T(8,128)(2,1)} %constant.114.clone) | copy-start | bytes 1572868
  4.5 14.2 %all-to-all-start = ((bf16[8,28,96]{2,1,0:T(8,128)(2,1)}), bf16[8,28,96]{2,1,0:T(8,128)(2,1)S(1)}, u32[]{:S(2)}, u32[]{:S(2)}) async-start(bf16[8,28,96]{2,1,0:T(8,128)(2,1)} %fusion.14), calls=%async_computation | async-start | bytes 131072 | tf_op jit(solution)/shard_map/all_to_all | solution.py:115
  18.7 14.3 %all-to-all-start.1 = ((bf16[8,96,256]{2,1,0:T(8,128)(2,1)}), bf16[8,96,256]{2,1,0:T(8,128)(2,1)S(1)}, u32[]{:S(2)}, u32[]{:S(2)}) async-start(bf16[8,96,256]{2,1,0:T(8,128)(2,1)} %bitcast.18), calls=%async_computation.1 | async-start | bytes 786432 | tf_op jit(solution)/shard_map/all_to_all | solution.py:121
  27.0 1.7 %copy-start.1 = (f32[512,256]{1,0:T(8,128)S(1)}, f32[512,256]{1,0:T(8,128)}, u32[]{:S(2)}) copy-start(f32[512,256]{1,0:T(8,128)} %param.11) | copy-start | bytes 1572868
  33.6 5.8 %collective-permute-start.2 = (bf16[512,256]{1,0:T(8,128)(2,1)S(1)}, bf16[512,256]{1,0:T(8,128)(2,1)S(1)}, u32[]{:S(2)}, u32[]{:S(2)}) collective-permute-start(bf16[512,256]{1,0:T(8,128)(2,1)S(1)} %convolution_convert_fusion.1), channel_id=1, source_target_pairs={{0,3},{1,0},{2,1},{3,2},{4,7},{5,4},{6,5},{7,6},{8,11},{9,8},{10,9... | collective-permute-start | bytes 786440 | tf_op jit(solution)/shard_map/ppermute | solution.py:144
  33.6 8.7 %collective-permute-start.1 = (bf16[512,256]{1,0:T(8,128)(2,1)S(1)}, bf16[512,256]{1,0:T(8,128)(2,1)S(1)}, u32[]{:S(2)}, u32[]{:S(2)}) collective-permute-start(bf16[512,256]{1,0:T(8,128)(2,1)S(1)} %convolution_convert_fusion.1), channel_id=1, source_target_pairs={{0,1},{1,2},{2,3},{3,0},{4,5},{5,6},{6,7},{7,4},{8,9},{9,10},{10,1... | collective-permute-start | bytes 786440 | tf_op jit(solution)/shard_map/ppermute | solution.py:144
  34.1 13.7 %collective-permute-start = (bf16[512,256]{1,0:T(8,128)(2,1)S(1)}, bf16[512,256]{1,0:T(8,128)(2,1)S(1)}, u32[]{:S(2)}, u32[]{:S(2)}) collective-permute-start(bf16[512,256]{1,0:T(8,128)(2,1)S(1)} %convolution_convert_fusion.1), channel_id=1, source_target_pairs={{0,2},{1,3},{2,0},{3,1},{4,6},{5,7},{6,4},{7,5},{8,10},{9,11},{10,... | collective-permute-start | bytes 786440 | tf_op jit(solution)/shard_map/ppermute | solution.py:144

commit v7 on v6

--- a/solution.py
+++ b/solution.py
@@ -84,6 +84,21 @@
     return (values // 256).astype(jnp.bfloat16), (values % 256).astype(jnp.bfloat16)
 
 
+def exchange(blocks, axis_name):
+    count = lax.axis_size(axis_name)
+    if count > 8:
+        return lax.all_to_all(blocks, axis_name, split_axis=0, concat_axis=0, tiled=True)
+    me = lax.axis_index(axis_name)
+    arrived = []
+    for shift in range(count):
+        block = lax.dynamic_index_in_dim(blocks, (me + shift) % count, 0, keepdims=False)
+        if shift:
+            pairs = [(i, (i + shift) % count) for i in range(count)]
+            block = lax.ppermute(block, axis_name, pairs)
+        arrived.append(block)
+    return jnp.stack(arrived)
+
+
 def local(images, defocus, volume, counts, slot_pixel, slot_taps, slot_weights):
     first, second = dft_tables()
     extract = volume.astype(jnp.bfloat16)
@@ -112,13 +127,13 @@
         rows_of = piece.shape[1]
         meta = meta + jnp.pad(piece, ((0, 0), (offset, fields - offset - rows_of), (0, 0)))
         offset += rows_of
-    got_meta = lax.all_to_all(meta, "vol", split_axis=0, concat_axis=0, tiled=True)
+    got_meta = exchange(meta, "vol")
     observed = transform(images, first, second)
     flat_pixels = pixel_ids.reshape(-1)
     onehot = (flat_pixels[:, None] == jnp.arange(observed.shape[0], dtype=jnp.int32)[None, :])
     rows = jnp.dot(onehot.astype(jnp.bfloat16), observed, preferred_element_type=jnp.float32)
     rows = rows.astype(jnp.bfloat16).reshape(owners, capacity, width)
-    got_rows = lax.all_to_all(rows, "vol", split_axis=0, concat_axis=0, tiled=True)
+    got_rows = exchange(rows, "vol")
     whole = got_meta[:, : 2 * taps].astype(jnp.int32)
     got_taps = whole[:, :taps] * 256 + whole[:, taps:]
     got_weights = got_meta[:, 2 * taps : 3 * taps]

time: 49.3 us -> 72.2 us (1.46)
  waiting for transfers between devices: 19 us -> 37.3 us
  starting transfers between devices: 12.8 us -> 18.9 us
  matrix products: 3.53 us -> 2.01 us
  other arithmetic: 10.1 us -> 9.32 us
    ppermute x0 -> x14, waiting for transfers between devices: none -> 25.1 us  [exchange(): block = lax.ppermute(block, axis_name, pairs)]
    ppermute x0 -> x14, starting transfers between devices: none -> 16.9 us  [exchange(): block = lax.ppermute(block, axis_name, pairs)]
    all_to_all x2 -> x0, starting transfers between devices: 10.7 us -> none  [the longest x1 7.28 us: local(): lax.all_to_all(meta, 'vol', split_axis=0, concat_axis=0, tiled=True)]
    all_to_all x2 -> x0, waiting for transfers between devices: 6.73 us -> none  [the longest x1 3.92 us: local(): lax.all_to_all(rows, 'vol', split_axis=0, concat_axis=0, tiled=True)]
    dot_general x1, matrix products: 1.21 us -> 0.26 us  [transform(): jnp.einsum('iyx,jkx->ijyk', pictures, jnp.asarray(first), preferred_eleme...]
    dot_general x1, matrix products: 1.19 us -> 0.44 us  [local(): jnp.dot(onehot.astype(jnp.bfloat16), observed, preferred_element_type=jnp...]
    unnamed x6 -> x20, local copies, waits for them, and re-layouts: 0.01 us -> 0.75 us
  transfers between devices with their start and end apart: 5 -> 17, of which waited for: 5 -> 9; matrix products, arithmetic and copies ran while one was open for 22% -> 11% of each run, Pallas kernels for 0% -> 0%
where the time goes in v7:
time: 72.2 us; the launch traced here: 71.4 us
  waiting for transfers between devices  37.3 us (52%)
  starting transfers between devices  18.9 us (26%)
  other arithmetic  9.32 us (13%)
  local copies, waits for them, and re-layouts  2.78 us (4%)
  matrix products  2.01 us (3%)
  between operations  1.05 us (1%)
    ppermute x14, waiting for transfers between devices, exchange(): block = lax.ppermute(block, axis_name, pairs)  25.1 us
    ppermute x14, starting transfers between devices, exchange(): block = lax.ppermute(block, axis_name, pairs)  16.9 us
    ppermute x3, waiting for transfers between devices, local(): arrived.append(lax.ppermute(partial, 'ptcl', pairs).astype(jnp.float32))  12.2 us
    neg x1, other arithmetic, ctf_rows(): -jnp.sin(math.pi * focus.astype(jnp.float32)[..., None] * radius + phase_...  3.56 us
    ppermute x3, starting transfers between devices, local(): arrived.append(lax.ppermute(partial, 'ptcl', pairs).astype(jnp.float32))  2.05 us
    reduce_sum x1, other arithmetic, tap_matrix_t(): return jnp.sum(picked, axis=0, dtype=jnp.bfloat16)  1.66 us
    convert_element_type x2, other arithmetic, split_whole(): (values // 256).astype(jnp.bfloat16)  1.53 us
  transfers between devices with their start and end apart: 17, of which 9 were waited for; matrix products, arithmetic and copies ran while one was open for 11% of the time, Pallas kernels for 0%

profile of v7, /device:TPU:0, one launch (start us, length us, event | category | flops | bytes accessed | tf_op | source)
XLA Modules:
  0.0 71.4 jit_solution(7743397019809882746)
XLA Ops:
  0.7 0.7 %iota_compare_fusion.5 = pred[8,1,96]{2,1,0:T(4,128)(4,1)S(1)} fusion(s32[8]{0:T(128)} %bitcast.146), kind=kLoop, calls=%fused_computation.102 | loop fusion | flops 768 | bytes 800 | tf_op jit(solution)/shard_map/lt | solution.py:111
  1.5 0.7 %fusion.34 = (bf16[8,1,96]{2,1,0:T(2,128)(2,1)S(1)}, s32[8,1,96]{2,1,0:T(1,128)S(1)}) fusion(s32[8,1,96]{2,1,0:T(1,128)} %bitcast.143), kind=kLoop, calls=%fused_computation.104 | loop fusion | flops 20736 | bytes 7680 | tf_op jit(solution)/shard_map/convert_element_type | solution.py:84
  2.2 0.8 %fusion.19 = (bf16[8,8,96]{2,1,0:T(8,128)(2,1)S(1)}, bf16[8,8,96]{2,1,0:T(8,128)(2,1)S(1)}) fusion(s32[1,1,8,8,96]{4,3,2,1,0:T(8,128)} %param.14), kind=kLoop, calls=%fused_computation.56 | loop fusion | flops 129024 | bytes 49152 | tf_op jit(solution)/shard_map/convert_element_type | solution.py:84
  3.2 0.8 %fusion.18 = bf16[8,28,96]{2,1,0:T(8,128)(2,1)S(1)} fusion(pred[8,1,96]{2,1,0:T(4,128)(4,1)S(1)} %iota_compare_fusion.5, bf16[8,1,96]{2,1,0:T(2,128)(2,1)S(1)} %fusion.30, bf16[8,1,96]{2,1,0:T(2,128)(2,1)S(1)} %get-tuple-element.5, bf16[8,8,96]{2,1,0:T(8,128)(2,1)} %bitcast.144, bf16[8,8,96]{2,1,0:T(8,128)(2,1)S(1)} %get-tuple-element.24, ...), kind=kLoop, calls=%fused_computation.27 | loop fusion | flops 322560 | bytes 83768 | tf_op jit(solution)/shard_map/add | solution.py:128
  4.0 6.2 %collective-permute-start.6 = (bf16[28,96]{1,0:T(8,128)(2,1)S(1)}, bf16[28,96]{1,0:T(8,128)(2,1)S(1)}, u32[]{:S(2)}, u32[]{:S(2)}) collective-permute-start(bf16[28,96]{1,0:T(8,128)(2,1)S(1)} %get-tuple-element.15), channel_id=1, source_target_pairs={{0,28},{4,0},{8,4},{12,8},{16,12},{20,16},{24,20},{28,24},{1,29},{... | collective-permute-start | bytes 16136 | tf_op jit(solution)/shard_map/ppermute | solution.py:97
  10.6 3.0 %collective-permute-start.3 = (bf16[28,96]{1,0:T(8,128)(2,1)S(1)}, bf16[28,96]{1,0:T(8,128)(2,1)S(1)}, u32[]{:S(2)}, u32[]{:S(2)}) collective-permute-start(bf16[28,96]{1,0:T(8,128)(2,1)S(1)} %get-tuple-element.18), channel_id=1, source_target_pairs={{0,16},{4,20},{8,24},{12,28},{16,0},{20,4},{24,8},{28,12},{1,17},{... | collective-permute-start | bytes 16136 | tf_op jit(solution)/shard_map/ppermute | solution.py:97
  13.6 1.5 %collective-permute-start = (bf16[28,96]{1,0:T(8,128)(2,1)S(1)}, bf16[28,96]{1,0:T(8,128)(2,1)S(1)}, u32[]{:S(2)}, u32[]{:S(2)}) collective-permute-start(bf16[28,96]{1,0:T(8,128)(2,1)S(1)} %get-tuple-element.21), channel_id=1, source_target_pairs={{0,4},{4,8},{8,12},{12,16},{16,20},{20,24},{24,28},{28,0},{1,5},{5... | collective-permute-start | bytes 16136 | tf_op jit(solution)/shard_map/ppermute | solution.py:97
  15.1 0.8 %eq.57 = s32[768]{0:T(1024)S(1)} reshape(s32[1,1,8,96]{3,2,1,0:T(8,128)} %param.13) | data formatting | bytes 6144 | tf_op jit(solution)/shard_map/eq | solution.py:133
  17.6 2.4 %collective-permute-done = bf16[28,96]{1,0:T(8,128)(2,1)S(1)} collective-permute-done((bf16[28,96]{1,0:T(8,128)(2,1)S(1)}, bf16[28,96]{1,0:T(8,128)(2,1)S(1)}, u32[]{:S(2)}, u32[]{:S(2)}) %collective-permute-start) | collective-permute-done | bytes 5408 | tf_op jit(solution)/shard_map/ppermute | solution.py:97
  19.9 5.4 %collective-permute-done.1 = bf16[28,96]{1,0:T(8,128)(2,1)S(1)} collective-permute-done((bf16[28,96]{1,0:T(8,128)(2,1)S(1)}, bf16[28,96]{1,0:T(8,128)(2,1)S(1)}, u32[]{:S(2)}, u32[]{:S(2)}) %collective-permute-start.1) | collective-permute-done | bytes 5408 | tf_op jit(solution)/shard_map/ppermute | solution.py:97
  25.4 5.5 %collective-permute-done.2 = bf16[28,96]{1,0:T(8,128)(2,1)S(1)} collective-permute-done((bf16[28,96]{1,0:T(8,128)(2,1)S(1)}, bf16[28,96]{1,0:T(8,128)(2,1)S(1)}, u32[]{:S(2)}, u32[]{:S(2)}) %collective-permute-start.2) | collective-permute-done | bytes 5408 | tf_op jit(solution)/shard_map/ppermute | solution.py:97
  30.9 1.1 %collective-permute-start.12 = (bf16[96,256]{1,0:T(8,128)(2,1)S(1)}, bf16[96,256]{1,0:T(8,128)(2,1)S(1)}, u32[]{:S(2)}, u32[]{:S(2)}) collective-permute-start(bf16[96,256]{1,0:T(8,128)(2,1)S(1)} %get-tuple-element.8), channel_id=1, source_target_pairs={{0,24},{4,28},{8,0},{12,4},{16,8},{20,12},{24,16},{28,20},{1,25},{... | collective-permute-start | bytes 147464 | tf_op jit(solution)/shard_map/ppermute | solution.py:97
  32.1 3.3 %collective-permute-start.10 = (bf16[96,256]{1,0:T(8,128)(2,1)S(1)}, bf16[96,256]{1,0:T(8,128)(2,1)S(1)}, u32[]{:S(2)}, u32[]{:S(2)}) collective-permute-start(bf16[96,256]{1,0:T(8,128)(2,1)S(1)} %get-tuple-element.10), channel_id=1, source_target_pairs={{0,16},{4,20},{8,24},{12,28},{16,0},{20,4},{24,8},{28,12},{1,17},{... | collective-permute-start | bytes 147464 | tf_op jit(solution)/shard_map/ppermute | solution.py:97
  36.3 1.7 %fusion.1 = bf16[512,768]{1,0:T(8,128)(2,1)S(1)} fusion(s32[8,768]{1,0:T(8,128)S(1)} %eq.53, bf16[8,768]{1,0:T(8,128)(2,1)S(1)} %broadcast_in_dim.22), kind=kLoop, calls=%fused_computation.2 | loop fusion | flops 9043968 | bytes 823296 | tf_op jit(solution)/shard_map/reduce_sum | solution.py:80
  38.0 3.6 %sine_negate_fusion = f32[8,96,128]{2,1,0:T(8,128)S(1)} fusion(f32[8,96]{1,0:T(8,128)S(1)} %fusion.29, s32[8,96]{1,0:T(8,128)S(1)} %fusion.25, f32[8,96]{1,0:T(8,128)S(1)} %bitcast.142), kind=kLoop, calls=%fused_computation.20 | loop fusion | flops 884736 | bytes 402432 | tf_op jit(solution)/shard_map/neg | solution.py:57
  42.4 0.7 %collective-permute-start.8 = (bf16[96,256]{1,0:T(8,128)(2,1)S(1)}, bf16[96,256]{1,0:T(8,128)(2,1)S(1)}, u32[]{:S(2)}, u32[]{:S(2)}) collective-permute-start(bf16[96,256]{1,0:T(8,128)(2,1)S(1)} %get-tuple-element.12), channel_id=1, source_target_pairs={{0,8},{4,12},{8,16},{12,20},{16,24},{20,28},{24,0},{28,4},{1,9},{5... | collective-permute-start | bytes 147464 | tf_op jit(solution)/shard_map/ppermute | solution.py:97
  43.1 5.1 %collective-permute-done.8 = bf16[96,256]{1,0:T(8,128)(2,1)S(1)} collective-permute-done((bf16[96,256]{1,0:T(8,128)(2,1)S(1)}, bf16[96,256]{1,0:T(8,128)(2,1)S(1)}, u32[]{:S(2)}, u32[]{:S(2)}) %collective-permute-start.8) | collective-permute-done | bytes 49184 | tf_op jit(solution)/shard_map/ppermute | solution.py:97
  48.3 5.9 %collective-permute-done.9 = bf16[96,256]{1,0:T(8,128)(2,1)S(1)} collective-permute-done((bf16[96,256]{1,0:T(8,128)(2,1)S(1)}, bf16[96,256]{1,0:T(8,128)(2,1)S(1)}, u32[]{:S(2)}, u32[]{:S(2)}) %collective-permute-start.9) | collective-permute-done | bytes 49184 | tf_op jit(solution)/shard_map/ppermute | solution.py:97
  55.2 1.0 %convolution_convert_fusion.1 = bf16[512,256]{1,0:T(8,128)(2,1)S(1)} fusion(bf16[512,768]{1,0:T(8,128)(2,1)S(1)} %fusion.1, bf16[768,256]{1,0:T(8,128)(2,1)S(1)} %bitcast.145, f32[96,8,2,128]{3,2,1,0:T(2,128)S(1)} %bitcast.137, pred[768]{0:T(1024)(128)(4,1)S(1)} %gt.15, f32[512,256]{1,0:T(8,128)S(1)} %copy-done.2), kind=kOutput, calls=%fused_computation.9 | convolution fusion | flops 404488192 | bytes 2753280 | tf_op jit(solution)/shard_map/dot_general | solution.py:152
  56.7 1.5 %collective-permute-start.14 = (bf16[512,256]{1,0:T(8,128)(2,1)S(1)}, bf16[512,256]{1,0:T(8,128)(2,1)S(1)}, u32[]{:S(2)}, u32[]{:S(2)}) collective-permute-start(bf16[512,256]{1,0:T(8,128)(2,1)S(1)} %convolution_convert_fusion.1), channel_id=1, source_target_pairs={{0,2},{1,3},{2,0},{3,1},{4,6},{5,7},{6,4},{7,5},{8,10},{9,11},{10,... | collective-permute-start | bytes 786440 | tf_op jit(solution)/shard_map/ppermute | solution.py:159
  58.2 3.7 %collective-permute-done.16 = bf16[512,256]{1,0:T(8,128)(2,1)S(1)} collective-permute-done((bf16[512,256]{1,0:T(8,128)(2,1)S(1)}, bf16[512,256]{1,0:T(8,128)(2,1)S(1)}, u32[]{:S(2)}, u32[]{:S(2)}) %collective-permute-start.16) | collective-permute-done | bytes 262176 | tf_op jit(solution)/shard_map/ppermute | solution.py:159
  61.9 2.9 %collective-permute-done.15 = bf16[512,256]{1,0:T(8,128)(2,1)S(1)} collective-permute-done((bf16[512,256]{1,0:T(8,128)(2,1)S(1)}, bf16[512,256]{1,0:T(8,128)(2,1)S(1)}, u32[]{:S(2)}, u32[]{:S(2)}) %collective-permute-start.15) | collective-permute-done | bytes 262176 | tf_op jit(solution)/shard_map/ppermute | solution.py:159
  64.9 5.6 %collective-permute-done.14 = bf16[512,256]{1,0:T(8,128)(2,1)S(1)} collective-permute-done((bf16[512,256]{1,0:T(8,128)(2,1)S(1)}, bf16[512,256]{1,0:T(8,128)(2,1)S(1)}, u32[]{:S(2)}, u32[]{:S(2)}) %collective-permute-start.14) | collective-permute-done | bytes 262176 | tf_op jit(solution)/shard_map/ppermute | solution.py:159
  70.5 0.9 %add_subtract_fusion = f32[512,256]{1,0:T(8,128)} fusion(f32[512,256]{1,0:T(8,128)S(1)} %copy-done.2, bf16[512,256]{1,0:T(8,128)(2,1)S(1)} %collective-permute-done.16, bf16[512,256]{1,0:T(8,128)(2,1)S(1)} %collective-permute-done.15, bf16[512,256]{1,0:T(8,128)(2,1)S(1)} %collective-permute-done.14, bf16[512,256]{1,0:T(8,128)(2,1)S(1)} %convolution_convert_fusion.1), kind=kLoop, calls=%fused_computation.18 | loop fusion | flops 1048576 | bytes 2097152 | tf_op jit(solution)/shard_map/sub | solution.py:164
  (65 shorter events, 5.5 us)
Async XLA Ops:
  0.0 15.9 %copy-start = (bf16[1,256,256]{2,1,0:T(8,128)(2,1)S(1)}, bf16[1,256,256]{2,1,0:T(8,128)(2,1)}, u32[]{:S(2)}) copy-start(bf16[1,256,256]{2,1,0:T(8,128)(2,1)} %param.9) | copy-start | bytes 393220
  0.0 15.9 %copy-start.3 = (bf16[2,256,256]{2,1,0:T(8,128)(2,1)S(1)}, bf16[2,256,256]{2,1,0:T(8,128)(2,1)}, u32[]{:S(2)}) copy-start(bf16[2,256,256]{2,1,0:T(8,128)(2,1)} %constant.220.clone) | copy-start | bytes 786436
  0.0 16.1 %copy-start.1 = (bf16[512,512]{1,0:T(8,128)(2,1)S(1)}, bf16[512,512]{1,0:T(8,128)(2,1)}, u32[]{:S(2)}) copy-start(bf16[512,512]{1,0:T(8,128)(2,1)} %constant.221.clone) | copy-start | bytes 1572868
  4.0 31.4 %collective-permute-start.6 = (bf16[28,96]{1,0:T(8,128)(2,1)S(1)}, bf16[28,96]{1,0:T(8,128)(2,1)S(1)}, u32[]{:S(2)}, u32[]{:S(2)}) collective-permute-start(bf16[28,96]{1,0:T(8,128)(2,1)S(1)} %get-tuple-element.15), channel_id=1, source_target_pairs={{0,28},{4,0},{8,4},{12,8},{16,12},{20,16},{24,20},{28,24},{1,29},{... | collective-permute-start | bytes 16136 | tf_op jit(solution)/shard_map/ppermute | solution.py:97
  10.1 21.9 %collective-permute-start.5 = (bf16[28,96]{1,0:T(8,128)(2,1)S(1)}, bf16[28,96]{1,0:T(8,128)(2,1)S(1)}, u32[]{:S(2)}, u32[]{:S(2)}) collective-permute-start(bf16[28,96]{1,0:T(8,128)(2,1)S(1)} %get-tuple-element.16), channel_id=1, source_target_pairs={{0,24},{4,28},{8,0},{12,4},{16,8},{20,12},{24,16},{28,20},{1,25},{... | collective-permute-start | bytes 16136 | tf_op jit(solution)/shard_map/ppermute | solution.py:97
  10.6 21.5 %collective-permute-start.4 = (bf16[28,96]{1,0:T(8,128)(2,1)S(1)}, bf16[28,96]{1,0:T(8,128)(2,1)S(1)}, u32[]{:S(2)}, u32[]{:S(2)}) collective-permute-start(bf16[28,96]{1,0:T(8,128)(2,1)S(1)} %get-tuple-element.17), channel_id=1, source_target_pairs={{0,20},{4,24},{8,28},{12,0},{16,4},{20,8},{24,12},{28,16},{1,21},{... | collective-permute-start | bytes 16136 | tf_op jit(solution)/shard_map/ppermute | solution.py:97
  10.6 20.3 %collective-permute-start.3 = (bf16[28,96]{1,0:T(8,128)(2,1)S(1)}, bf16[28,96]{1,0:T(8,128)(2,1)S(1)}, u32[]{:S(2)}, u32[]{:S(2)}) collective-permute-start(bf16[28,96]{1,0:T(8,128)(2,1)S(1)} %get-tuple-element.18), channel_id=1, source_target_pairs={{0,16},{4,20},{8,24},{12,28},{16,0},{20,4},{24,8},{28,12},{1,17},{... | collective-permute-start | bytes 16136 | tf_op jit(solution)/shard_map/ppermute | solution.py:97
  13.6 6.3 %collective-permute-start = (bf16[28,96]{1,0:T(8,128)(2,1)S(1)}, bf16[28,96]{1,0:T(8,128)(2,1)S(1)}, u32[]{:S(2)}, u32[]{:S(2)}) collective-permute-start(bf16[28,96]{1,0:T(8,128)(2,1)S(1)} %get-tuple-element.21), channel_id=1, source_target_pairs={{0,4},{4,8},{8,12},{12,16},{16,20},{20,24},{24,28},{28,0},{1,5},{5... | collective-permute-start | bytes 16136 | tf_op jit(solution)/shard_map/ppermute | solution.py:97
  19.9 5.4 %collective-permute-start.1 = (bf16[28,96]{1,0:T(8,128)(2,1)S(1)}, bf16[28,96]{1,0:T(8,128)(2,1)S(1)}, u32[]{:S(2)}, u32[]{:S(2)}) collective-permute-start(bf16[28,96]{1,0:T(8,128)(2,1)S(1)} %get-tuple-element.20), channel_id=1, source_target_pairs={{0,8},{4,12},{8,16},{12,20},{16,24},{20,28},{24,0},{28,4},{1,9},{5... | collective-permute-start | bytes 16136 | tf_op jit(solution)/shard_map/ppermute | solution.py:97
  25.4 5.6 %collective-permute-start.2 = (bf16[28,96]{1,0:T(8,128)(2,1)S(1)}, bf16[28,96]{1,0:T(8,128)(2,1)S(1)}, u32[]{:S(2)}, u32[]{:S(2)}) collective-permute-start(bf16[28,96]{1,0:T(8,128)(2,1)S(1)} %get-tuple-element.19), channel_id=1, source_target_pairs={{0,12},{4,16},{8,20},{12,24},{16,28},{20,0},{24,4},{28,8},{1,13},{... | collective-permute-start | bytes 16136 | tf_op jit(solution)/shard_map/ppermute | solution.py:97
  30.9 23.3 %collective-permute-start.13 = (bf16[96,256]{1,0:T(8,128)(2,1)S(1)}, bf16[96,256]{1,0:T(8,128)(2,1)S(1)}, u32[]{:S(2)}, u32[]{:S(2)}) collective-permute-start(bf16[96,256]{1,0:T(8,128)(2,1)S(1)} %get-tuple-element.7), channel_id=1, source_target_pairs={{0,28},{4,0},{8,4},{12,8},{16,12},{20,16},{24,20},{28,24},{1,29},{... | collective-permute-start | bytes 147464 | tf_op jit(solution)/shard_map/ppermute | solution.py:97
  30.9 23.2 %collective-permute-start.12 = (bf16[96,256]{1,0:T(8,128)(2,1)S(1)}, bf16[96,256]{1,0:T(8,128)(2,1)S(1)}, u32[]{:S(2)}, u32[]{:S(2)}) collective-permute-start(bf16[96,256]{1,0:T(8,128)(2,1)S(1)} %get-tuple-element.8), channel_id=1, source_target_pairs={{0,24},{4,28},{8,0},{12,4},{16,8},{20,12},{24,16},{28,20},{1,25},{... | collective-permute-start | bytes 147464 | tf_op jit(solution)/shard_map/ppermute | solution.py:97
  32.1 22.1 %collective-permute-start.11 = (bf16[96,256]{1,0:T(8,128)(2,1)S(1)}, bf16[96,256]{1,0:T(8,128)(2,1)S(1)}, u32[]{:S(2)}, u32[]{:S(2)}) collective-permute-start(bf16[96,256]{1,0:T(8,128)(2,1)S(1)} %get-tuple-element.9), channel_id=1, source_target_pairs={{0,20},{4,24},{8,28},{12,0},{16,4},{20,8},{24,12},{28,16},{1,21},{... | collective-permute-start | bytes 147464 | tf_op jit(solution)/shard_map/ppermute | solution.py:97
  32.1 22.1 %collective-permute-start.10 = (bf16[96,256]{1,0:T(8,128)(2,1)S(1)}, bf16[96,256]{1,0:T(8,128)(2,1)S(1)}, u32[]{:S(2)}, u32[]{:S(2)}) collective-permute-start(bf16[96,256]{1,0:T(8,128)(2,1)S(1)} %get-tuple-element.10), channel_id=1, source_target_pairs={{0,16},{4,20},{8,24},{12,28},{16,0},{20,4},{24,8},{28,12},{1,17},{... | collective-permute-start | bytes 147464 | tf_op jit(solution)/shard_map/ppermute | solution.py:97
  35.4 6.9 %collective-permute-start.7 = (bf16[96,256]{1,0:T(8,128)(2,1)S(1)}, bf16[96,256]{1,0:T(8,128)(2,1)S(1)}, u32[]{:S(2)}, u32[]{:S(2)}) collective-permute-start(bf16[96,256]{1,0:T(8,128)(2,1)S(1)} %get-tuple-element.13), channel_id=1, source_target_pairs={{0,4},{4,8},{8,12},{12,16},{16,20},{20,24},{24,28},{28,0},{1,5},{5... | collective-permute-start | bytes 147464 | tf_op jit(solution)/shard_map/ppermute | solution.py:97
  42.4 5.9 %collective-permute-start.8 = (bf16[96,256]{1,0:T(8,128)(2,1)S(1)}, bf16[96,256]{1,0:T(8,128)(2,1)S(1)}, u32[]{:S(2)}, u32[]{:S(2)}) collective-permute-start(bf16[96,256]{1,0:T(8,128)(2,1)S(1)} %get-tuple-element.12), channel_id=1, source_target_pairs={{0,8},{4,12},{8,16},{12,20},{16,24},{20,28},{24,0},{28,4},{1,9},{5... | collective-permute-start | bytes 147464 | tf_op jit(solution)/shard_map/ppermute | solution.py:97
  48.2 5.9 %collective-permute-start.9 = (bf16[96,256]{1,0:T(8,128)(2,1)S(1)}, bf16[96,256]{1,0:T(8,128)(2,1)S(1)}, u32[]{:S(2)}, u32[]{:S(2)}) collective-permute-start(bf16[96,256]{1,0:T(8,128)(2,1)S(1)} %get-tuple-element.11), channel_id=1, source_target_pairs={{0,12},{4,16},{8,20},{12,24},{16,28},{20,0},{24,4},{28,8},{1,13},{... | collective-permute-start | bytes 147464 | tf_op jit(solution)/shard_map/ppermute | solution.py:97
  54.1 1.0 %copy-start.2 = (f32[512,256]{1,0:T(8,128)S(1)}, f32[512,256]{1,0:T(8,128)}, u32[]{:S(2)}) copy-start(f32[512,256]{1,0:T(8,128)} %param.11) | copy-start | bytes 1572868
  56.2 5.8 %collective-permute-start.16 = (bf16[512,256]{1,0:T(8,128)(2,1)S(1)}, bf16[512,256]{1,0:T(8,128)(2,1)S(1)}, u32[]{:S(2)}, u32[]{:S(2)}) collective-permute-start(bf16[512,256]{1,0:T(8,128)(2,1)S(1)} %convolution_convert_fusion.1), channel_id=1, source_target_pairs={{0,3},{1,0},{2,1},{3,2},{4,7},{5,4},{6,5},{7,6},{8,11},{9,8},{10,9... | collective-permute-start | bytes 786440 | tf_op jit(solution)/shard_map/ppermute | solution.py:159
  56.2 8.7 %collective-permute-start.15 = (bf16[512,256]{1,0:T(8,128)(2,1)S(1)}, bf16[512,256]{1,0:T(8,128)(2,1)S(1)}, u32[]{:S(2)}, u32[]{:S(2)}) collective-permute-start(bf16[512,256]{1,0:T(8,128)(2,1)S(1)} %convolution_convert_fusion.1), channel_id=1, source_target_pairs={{0,1},{1,2},{2,3},{3,0},{4,5},{5,6},{6,7},{7,4},{8,9},{9,10},{10,1... | collective-permute-start | bytes 786440 | tf_op jit(solution)/shard_map/ppermute | solution.py:159
  56.7 13.7 %collective-permute-start.14 = (bf16[512,256]{1,0:T(8,128)(2,1)S(1)}, bf16[512,256]{1,0:T(8,128)(2,1)S(1)}, u32[]{:S(2)}, u32[]{:S(2)}) collective-permute-start(bf16[512,256]{1,0:T(8,128)(2,1)S(1)} %convolution_convert_fusion.1), channel_id=1, source_target_pairs={{0,2},{1,3},{2,0},{3,1},{4,6},{5,7},{6,4},{7,5},{8,10},{9,11},{10,... | collective-permute-start | bytes 786440 | tf_op jit(solution)/shard_map/ppermute | solution.py:159

commit v8 on v5

--- a/solution.py
+++ b/solution.py
@@ -136,13 +136,30 @@
     flat_residual = weighted.reshape(-1, width)
     gradient = jnp.dot(matrix_t, flat_residual, preferred_element_type=jnp.float32)
     shards = lax.axis_size("ptcl")
-    parts = gradient.astype(jnp.bfloat16).reshape(shards, -1, gradient.shape[1])
+    if shards == 4:
+        me = lax.axis_index("ptcl")
+        on_chip = [(i, i ^ 1) for i in range(shards)]
+        across = [(i, i ^ 2) for i in range(shards)]
+        pair_sum = gradient + lax.ppermute(gradient, "ptcl", on_chip)
+        half = gradient.shape[0] // 2
+        core = me % 2
+        mine = lax.dynamic_slice_in_dim(pair_sum, core * half, half, axis=0)
+        total = mine + lax.ppermute(mine, "ptcl", across)
+        updated = lax.dynamic_slice_in_dim(volume, core * half, half, axis=0) - learn_rate * total
+        other = lax.ppermute(updated, "ptcl", on_chip)
+        return jnp.where(
+            core == 0,
+            jnp.concatenate([updated, other], axis=0),
+            jnp.concatenate([other, updated], axis=0),
+        )
+    partial = gradient.astype(jnp.bfloat16)
+    parts = partial.reshape(shards, -1, gradient.shape[1])
     got_parts = lax.all_to_all(parts, "ptcl", split_axis=0, concat_axis=0, tiled=True)
-    quarter = jnp.sum(got_parts.astype(jnp.float32), axis=0)
-    rows_each = quarter.shape[0]
+    part_sum = jnp.sum(got_parts.astype(jnp.float32), axis=0)
+    rows_each = part_sum.shape[0]
     start = lax.axis_index("ptcl") * rows_each
     mine = lax.dynamic_slice_in_dim(volume, start, rows_each, axis=0)
-    updated = mine - learn_rate * quarter
+    updated = mine - learn_rate * part_sum
     return lax.all_gather(updated, "ptcl", axis=0, tiled=True)
 
 

time: 51.8 us -> 47 us (0.907)
  blocking collectives: 6.58 us -> 0 us
  waiting for transfers between devices: 12.7 us -> 17 us
  starting transfers between devices: 14.1 us -> 12.4 us
  other arithmetic: 9.22 us -> 10.1 us
  local copies, waits for them, and re-layouts: 3.29 us -> 2.5 us
  matrix products: 4.24 us -> 3.53 us
    ppermute x0 -> x3, waiting for transfers between devices: none -> 10.3 us  [the longest x1 6.86 us: local(): total = mine + lax.ppermute(mine, 'ptcl', across)]
    all_gather x1 -> x0, blocking collectives: 6.58 us -> none  [local(): return lax.all_gather(updated, 'ptcl', axis=0, tiled=True)]
    all_to_all x1 -> x0, waiting for transfers between devices: 6 us -> none  [local(): lax.all_to_all(parts, 'ptcl', split_axis=0, concat_axis=0, tiled=True)]
    all_to_all x1 -> x0, starting transfers between devices: 3.41 us -> none  [local(): lax.all_to_all(parts, 'ptcl', split_axis=0, concat_axis=0, tiled=True)]
    ppermute x0 -> x3, starting transfers between devices: none -> 1.7 us  [the longest x1 1.55 us: local(): total = mine + lax.ppermute(mine, 'ptcl', across)]
    select_n x0 -> x1, other arithmetic: none -> 0.84 us  [local(): jnp.where(core == 0, jnp.concatenate([updated, other], axis=0), jnp.conca...]
    unnamed x7 -> x6, local copies, waits for them, and re-layouts: 0.81 us -> 0.01 us
    dot_general x1, matrix products: 1.08 us -> 0.37 us  [local(): jnp.dot(matrix_t, flat_residual, preferred_element_type=jnp.float32)]
  transfers between devices with their start and end apart: 3 -> 5, of which waited for: 3 -> 5; matrix products, arithmetic and copies ran while one was open for 21% -> 23% of each run, Pallas kernels for 0% -> 0%
where the time goes in v8:
time: 47 us; the launch traced here: 46.5 us
  waiting for transfers between devices  17 us (36%)
  starting transfers between devices  12.4 us (26%)
  other arithmetic  10.1 us (21%)
  matrix products  3.53 us (8%)
  local copies, waits for them, and re-layouts  2.5 us (5%)
  between operations  0.98 us (2%)
    all_to_all x1, starting transfers between devices, local(): lax.all_to_all(meta, 'vol', split_axis=0, concat_axis=0, tiled=True)  7.28 us
    ppermute x1, waiting for transfers between devices, local(): total = mine + lax.ppermute(mine, 'ptcl', across)  6.86 us
    all_to_all x1, waiting for transfers between devices, local(): lax.all_to_all(rows, 'vol', split_axis=0, concat_axis=0, tiled=True)  3.92 us
    neg x1, other arithmetic, ctf_rows(): -jnp.sin(math.pi * focus.astype(jnp.float32)[..., None] * radius + phase_...  3.56 us
    all_to_all x1, starting transfers between devices, local(): lax.all_to_all(rows, 'vol', split_axis=0, concat_axis=0, tiled=True)  3.45 us
    all_to_all x1, waiting for transfers between devices, local(): lax.all_to_all(meta, 'vol', split_axis=0, concat_axis=0, tiled=True)  2.8 us
    ppermute x1, waiting for transfers between devices, local(): pair_sum = gradient + lax.ppermute(gradient, 'ptcl', on_chip)  1.88 us
    reduce_sum x1, other arithmetic, tap_matrix_t(): return jnp.sum(picked, axis=0, dtype=jnp.bfloat16)  1.66 us
  transfers between devices with their start and end apart: 5, of which 5 were waited for; matrix products, arithmetic and copies ran while one was open for 23% of the time, Pallas kernels for 0%

profile of v8, /device:TPU:0, one launch (start us, length us, event | category | flops | bytes accessed | tf_op | source)
XLA Modules:
  0.0 46.5 jit_solution(1013234592467460933)
XLA Ops:
  0.7 0.7 %iota_compare_fusion.5 = pred[8,1,96]{2,1,0:T(4,128)(4,1)S(1)} fusion(s32[8]{0:T(128)} %bitcast.79), kind=kLoop, calls=%fused_computation.69 | loop fusion | flops 768 | bytes 800 | tf_op jit(solution)/shard_map/lt | solution.py:96
  1.5 0.7 %fusion.30 = (bf16[8,1,96]{2,1,0:T(2,128)(2,1)S(1)}, s32[8,1,96]{2,1,0:T(1,128)S(1)}) fusion(s32[8,1,96]{2,1,0:T(1,128)} %bitcast.77), kind=kLoop, calls=%fused_computation.72 | loop fusion | flops 20736 | bytes 7680 | tf_op jit(solution)/shard_map/convert_element_type | solution.py:84
  2.2 0.8 %fusion.15 = (bf16[8,8,96]{2,1,0:T(8,128)(2,1)S(1)}, bf16[8,8,96]{2,1,0:T(8,128)(2,1)S(1)}) fusion(s32[1,1,8,8,96]{4,3,2,1,0:T(8,128)} %param.14), kind=kLoop, calls=%fused_computation.31 | loop fusion | flops 129024 | bytes 49152 | tf_op jit(solution)/shard_map/convert_element_type | solution.py:84
  3.1 1.4 %fusion.14 = bf16[8,28,96]{2,1,0:T(8,128)(2,1)} fusion(pred[8,1,96]{2,1,0:T(4,128)(4,1)S(1)} %iota_compare_fusion.5, bf16[8,1,96]{2,1,0:T(2,128)(2,1)S(1)} %fusion.26, bf16[8,1,96]{2,1,0:T(2,128)(2,1)S(1)} %get-tuple-element.5, bf16[8,8,96]{2,1,0:T(8,128)(2,1)} %bitcast.78, bf16[8,8,96]{2,1,0:T(8,128)(2,1)S(1)} %get-tuple-element.8, ...), kind=kLoop, calls=%fused_computation.25 | loop fusion | flops 322560 | bytes 83768 | tf_op jit(solution)/shard_map/add | solution.py:113
  4.5 7.3 %all-to-all-start = ((bf16[8,28,96]{2,1,0:T(8,128)(2,1)}), bf16[8,28,96]{2,1,0:T(8,128)(2,1)S(1)}, u32[]{:S(2)}, u32[]{:S(2)}) async-start(bf16[8,28,96]{2,1,0:T(8,128)(2,1)} %fusion.14), calls=%async_computation | async-start | bytes 131072 | tf_op jit(solution)/shard_map/all_to_all | solution.py:115
  11.8 0.8 %eq.46 = s32[768]{0:T(1024)S(1)} reshape(s32[1,1,8,96]{3,2,1,0:T(8,128)} %param.13) | data formatting | bytes 6144 | tf_op jit(solution)/shard_map/eq | solution.py:118
  12.6 1.2 %convolution_convert_fusion.2 = bf16[2,256,256]{1,2,0:T(8,128)(2,1)S(1)} fusion(bf16[2,256,256]{2,1,0:T(8,128)(2,1)} %constant.123.clone, bf16[1,256,256]{2,1,0:T(8,128)(2,1)S(1)} %copy-done), kind=kOutput, calls=%fused_computation.8 | convolution fusion | flops 67239936 | bytes 655360 | tf_op jit(solution)/shard_map/iyx,jkx->ijyk/dot_general | solution.py:37
  13.8 0.4 fusion.4
  14.2 0.5 %copy.20 = bf16[1,2,256,2,128]{4,1,3,2,0:T(2,128)(2,1)S(1)} copy(bf16[1,2,256,2,128]{2,1,4,3,0:T(2,128)(2,1)S(1)} %convert_element_type.139) | data formatting | bytes 524288 | tf_op jit(solution)/shard_map/convert_element_type | solution.py:47
  14.7 1.2 %fusion.3 = bf16[768,256]{1,0:T(8,128)(2,1)} fusion(s32[768]{0:T(1024)S(1)} %eq.46, bf16[64,8,2,128]{3,2,1,0:T(2,128)(2,1)S(1)} %bitcast.73), kind=kOutput, calls=%fused_computation.5 | convolution fusion | flops 201916416 | bytes 658432 | tf_op jit(solution)/shard_map/dot_general | solution.py:119
  15.9 2.8 %all-to-all-done = bf16[8,28,96]{2,1,0:T(8,128)(2,1)S(1)} async-done(((bf16[8,28,96]{2,1,0:T(8,128)(2,1)}), bf16[8,28,96]{2,1,0:T(8,128)(2,1)S(1)}, u32[]{:S(2)}, u32[]{:S(2)}) %all-to-all-start) | async-done | bytes 43040 | tf_op jit(solution)/shard_map/all_to_all | solution.py:115
  18.7 3.5 %all-to-all-start.1 = ((bf16[8,96,256]{2,1,0:T(8,128)(2,1)}), bf16[8,96,256]{2,1,0:T(8,128)(2,1)S(1)}, u32[]{:S(2)}, u32[]{:S(2)}) async-start(bf16[8,96,256]{2,1,0:T(8,128)(2,1)} %bitcast.18), calls=%async_computation.1 | async-start | bytes 786432 | tf_op jit(solution)/shard_map/all_to_all | solution.py:121
  22.3 3.6 %sine_negate_fusion = f32[8,96,128]{2,1,0:T(8,128)S(1)} fusion(f32[8,96]{1,0:T(8,128)S(1)} %fusion.25, s32[8,96]{1,0:T(8,128)S(1)} %fusion.21, f32[8,96]{1,0:T(8,128)S(1)} %bitcast.76), kind=kLoop, calls=%fused_computation.17 | loop fusion | flops 884736 | bytes 402432 | tf_op jit(solution)/shard_map/neg | solution.py:57
  26.1 0.3 mul.96
  26.4 0.6 %mul.97 = f32[8,96,256]{2,1,0:T(8,128)S(1)} reshape(f32[8,96,2,128]{3,2,1,0:T(2,128)S(1)} %mul.96) | data formatting | bytes 1572864 | tf_op jit(solution)/shard_map/mul | solution.py:65
  27.0 1.7 %fusion.1 = bf16[512,768]{1,0:T(8,128)(2,1)S(1)} fusion(s32[8,768]{1,0:T(8,128)S(1)} %eq.42, bf16[8,768]{1,0:T(8,128)(2,1)S(1)} %broadcast_in_dim.22), kind=kLoop, calls=%fused_computation.2 | loop fusion | flops 9043968 | bytes 823296 | tf_op jit(solution)/shard_map/reduce_sum | solution.py:80
  28.7 0.4 convolution_convert_fusion
  29.1 3.9 %all-to-all-done.1 = bf16[8,96,256]{2,1,0:T(8,128)(2,1)S(1)} async-done(((bf16[8,96,256]{2,1,0:T(8,128)(2,1)}), bf16[8,96,256]{2,1,0:T(8,128)(2,1)S(1)}, u32[]{:S(2)}, u32[]{:S(2)}) %all-to-all-start.1) | async-done | bytes 393248 | tf_op jit(solution)/shard_map/all_to_all | solution.py:121
  33.2 0.4 fusion.32
  33.7 1.9 %collective-permute-done = f32[512,256]{1,0:T(8,128)S(1)} collective-permute-done((f32[512,256]{1,0:T(8,128)S(1)}, f32[512,256]{1,0:T(8,128)S(1)}, u32[]{:S(2)}, u32[]{:S(2)}) %collective-permute-start) | collective-permute-done | bytes 524320 | tf_op jit(solution)/shard_map/ppermute | solution.py:143
  35.6 1.6 %collective-permute-start.1 = (f32[256,256]{1,0:T(8,128)S(1)}, f32[256,256]{1,0:T(8,128)S(1)}, u32[]{:S(2)}, u32[]{:S(2)}) collective-permute-start(f32[256,256]{1,0:T(8,128)S(1)} %dynamic-slice_add_fusion), channel_id=1, source_target_pairs={{0,2},{1,3},{2,0},{3,1},{4,6},{5,7},{6,4},{7,5},{8,10},{9,11},{10,... | collective-permute-start | bytes 786440 | tf_op jit(solution)/shard_map/ppermute | solution.py:147
  37.2 6.9 %collective-permute-done.1 = f32[256,256]{1,0:T(8,128)S(1)} collective-permute-done((f32[256,256]{1,0:T(8,128)S(1)}, f32[256,256]{1,0:T(8,128)S(1)}, u32[]{:S(2)}, u32[]{:S(2)}) %collective-permute-start.1) | collective-permute-done | bytes 262176 | tf_op jit(solution)/shard_map/ppermute | solution.py:147
  44.2 1.5 %collective-permute-done.2 = f32[256,256]{1,0:T(8,128)S(1)} collective-permute-done((f32[256,256]{1,0:T(8,128)S(1)}, f32[256,256]{1,0:T(8,128)S(1)}, u32[]{:S(2)}, u32[]{:S(2)}) %collective-permute-start.2) | collective-permute-done | bytes 262176 | tf_op jit(solution)/shard_map/ppermute | solution.py:149
  45.7 0.8 %maximum_select_fusion = f32[512,256]{1,0:T(8,128)} fusion(f32[256,256]{1,0:T(8,128)S(1)} %collective-permute-done.2, f32[256,256]{1,0:T(8,128)S(1)} %add_subtract_fusion, pred[]{:T(512)S(6)} %eq.41), kind=kLoop, calls=%fused_computation.16 | loop fusion | flops 393216 | bytes 1048577 | tf_op jit(solution)/shard_map/jit(_where)/select_n | solution.py:150
  (28 shorter events, 0.8 us)
Async XLA Ops:
  0.0 12.6 %copy-start = (bf16[1,256,256]{2,1,0:T(8,128)(2,1)S(1)}, bf16[1,256,256]{2,1,0:T(8,128)(2,1)}, u32[]{:S(2)}) copy-start(bf16[1,256,256]{2,1,0:T(8,128)(2,1)} %param.9) | copy-start | bytes 393220
  0.0 13.8 %copy-start.2 = (bf16[512,512]{1,0:T(8,128)(2,1)S(1)}, bf16[512,512]{1,0:T(8,128)(2,1)}, u32[]{:S(2)}) copy-start(bf16[512,512]{1,0:T(8,128)(2,1)} %constant.124.clone) | copy-start | bytes 1572868
  4.5 14.2 %all-to-all-start = ((bf16[8,28,96]{2,1,0:T(8,128)(2,1)}), bf16[8,28,96]{2,1,0:T(8,128)(2,1)S(1)}, u32[]{:S(2)}, u32[]{:S(2)}) async-start(bf16[8,28,96]{2,1,0:T(8,128)(2,1)} %fusion.14), calls=%async_computation | async-start | bytes 131072 | tf_op jit(solution)/shard_map/all_to_all | solution.py:115
  18.7 14.3 %all-to-all-start.1 = ((bf16[8,96,256]{2,1,0:T(8,128)(2,1)}), bf16[8,96,256]{2,1,0:T(8,128)(2,1)S(1)}, u32[]{:S(2)}, u32[]{:S(2)}) async-start(bf16[8,96,256]{2,1,0:T(8,128)(2,1)} %bitcast.18), calls=%async_computation.1 | async-start | bytes 786432 | tf_op jit(solution)/shard_map/all_to_all | solution.py:121
  27.0 1.7 %copy-start.1 = (f32[512,256]{1,0:T(8,128)S(1)}, f32[512,256]{1,0:T(8,128)}, u32[]{:S(2)}) copy-start(f32[512,256]{1,0:T(8,128)} %param.11) | copy-start | bytes 1572868
  33.6 2.0 %collective-permute-start = (f32[512,256]{1,0:T(8,128)S(1)}, f32[512,256]{1,0:T(8,128)S(1)}, u32[]{:S(2)}, u32[]{:S(2)}) collective-permute-start(f32[512,256]{1,0:T(8,128)S(1)} %fusion.32), channel_id=1, source_target_pairs={{0,1},{1,0},{2,3},{3,2},{4,5},{5,4},{6,7},{7,6},{8,9},{9,8},{10,11... | collective-permute-start | bytes 1572872 | tf_op jit(solution)/shard_map/ppermute | solution.py:143
  35.6 8.4 %collective-permute-start.1 = (f32[256,256]{1,0:T(8,128)S(1)}, f32[256,256]{1,0:T(8,128)S(1)}, u32[]{:S(2)}, u32[]{:S(2)}) collective-permute-start(f32[256,256]{1,0:T(8,128)S(1)} %dynamic-slice_add_fusion), channel_id=1, source_target_pairs={{0,2},{1,3},{2,0},{3,1},{4,6},{5,7},{6,4},{7,5},{8,10},{9,11},{10,... | collective-permute-start | bytes 786440 | tf_op jit(solution)/shard_map/ppermute | solution.py:147
  44.1 1.6 %collective-permute-start.2 = (f32[256,256]{1,0:T(8,128)S(1)}, f32[256,256]{1,0:T(8,128)S(1)}, u32[]{:S(2)}, u32[]{:S(2)}) collective-permute-start(f32[256,256]{1,0:T(8,128)S(1)} %add_subtract_fusion), channel_id=1, source_target_pairs={{0,1},{1,0},{2,3},{3,2},{4,5},{5,4},{6,7},{7,6},{8,9},{9,8},{10,11... | collective-permute-start | bytes 786440 | tf_op jit(solution)/shard_map/ppermute | solution.py:149

commit v9 on v8

--- a/solution.py
+++ b/solution.py
@@ -143,8 +143,8 @@
         pair_sum = gradient + lax.ppermute(gradient, "ptcl", on_chip)
         half = gradient.shape[0] // 2
         core = me % 2
-        mine = lax.dynamic_slice_in_dim(pair_sum, core * half, half, axis=0)
-        total = mine + lax.ppermute(mine, "ptcl", across)
+        mine = lax.dynamic_slice_in_dim(pair_sum, core * half, half, axis=0).astype(jnp.bfloat16)
+        total = mine.astype(jnp.float32) + lax.ppermute(mine, "ptcl", across).astype(jnp.float32)
         updated = lax.dynamic_slice_in_dim(volume, core * half, half, axis=0) - learn_rate * total
         other = lax.ppermute(updated, "ptcl", on_chip)
         return jnp.where(

time: 47 us -> 44.2 us (0.940)
  waiting for transfers between devices: 17 us -> 14.2 us
    ppermute x1, waiting for transfers between devices: 6.86 us -> 4.05 us  [local(): lax.ppermute(mine, 'ptcl', across).astype(jnp.float32)]
  transfers between devices with their start and end apart: 5 -> 5, of which waited for: 5 -> 5; matrix products, arithmetic and copies ran while one was open for 23% -> 25% of each run, Pallas kernels for 0% -> 0%
where the time goes in v9:
time: 44.2 us; the launch traced here: 43.7 us
  waiting for transfers between devices  14.2 us (32%)
  starting transfers between devices  12.4 us (28%)
  other arithmetic  10.1 us (23%)
  matrix products  3.53 us (8%)
  local copies, waits for them, and re-layouts  2.5 us (6%)
  between operations  0.98 us (2%)
    all_to_all x1, starting transfers between devices, local(): lax.all_to_all(meta, 'vol', split_axis=0, concat_axis=0, tiled=True)  7.28 us
    ppermute x1, waiting for transfers between devices, local(): lax.ppermute(mine, 'ptcl', across).astype(jnp.float32)  4.05 us
    all_to_all x1, waiting for transfers between devices, local(): lax.all_to_all(rows, 'vol', split_axis=0, concat_axis=0, tiled=True)  3.92 us
    neg x1, other arithmetic, ctf_rows(): -jnp.sin(math.pi * focus.astype(jnp.float32)[..., None] * radius + phase_...  3.56 us
    all_to_all x1, starting transfers between devices, local(): lax.all_to_all(rows, 'vol', split_axis=0, concat_axis=0, tiled=True)  3.45 us
    all_to_all x1, waiting for transfers between devices, local(): lax.all_to_all(meta, 'vol', split_axis=0, concat_axis=0, tiled=True)  2.8 us
    ppermute x1, waiting for transfers between devices, local(): pair_sum = gradient + lax.ppermute(gradient, 'ptcl', on_chip)  1.88 us
    reduce_sum x1, other arithmetic, tap_matrix_t(): return jnp.sum(picked, axis=0, dtype=jnp.bfloat16)  1.66 us
  transfers between devices with their start and end apart: 5, of which 5 were waited for; matrix products, arithmetic and copies ran while one was open for 25% of the time, Pallas kernels for 0%

profile of v9, /device:TPU:0, one launch (start us, length us, event | category | flops | bytes accessed | tf_op | source)
XLA Modules:
  0.0 43.7 jit_solution(11536815403756396528)
XLA Ops:
  0.7 0.7 %iota_compare_fusion.5 = pred[8,1,96]{2,1,0:T(4,128)(4,1)S(1)} fusion(s32[8]{0:T(128)} %bitcast.79), kind=kLoop, calls=%fused_computation.70 | loop fusion | flops 768 | bytes 800 | tf_op jit(solution)/shard_map/lt | solution.py:96
  1.5 0.7 %fusion.31 = (bf16[8,1,96]{2,1,0:T(2,128)(2,1)S(1)}, s32[8,1,96]{2,1,0:T(1,128)S(1)}) fusion(s32[8,1,96]{2,1,0:T(1,128)} %bitcast.77), kind=kLoop, calls=%fused_computation.73 | loop fusion | flops 20736 | bytes 7680 | tf_op jit(solution)/shard_map/convert_element_type | solution.py:84
  2.2 0.8 %fusion.16 = (bf16[8,8,96]{2,1,0:T(8,128)(2,1)S(1)}, bf16[8,8,96]{2,1,0:T(8,128)(2,1)S(1)}) fusion(s32[1,1,8,8,96]{4,3,2,1,0:T(8,128)} %param.14), kind=kLoop, calls=%fused_computation.32 | loop fusion | flops 129024 | bytes 49152 | tf_op jit(solution)/shard_map/convert_element_type | solution.py:84
  3.1 1.4 %fusion.15 = bf16[8,28,96]{2,1,0:T(8,128)(2,1)} fusion(pred[8,1,96]{2,1,0:T(4,128)(4,1)S(1)} %iota_compare_fusion.5, bf16[8,1,96]{2,1,0:T(2,128)(2,1)S(1)} %fusion.27, bf16[8,1,96]{2,1,0:T(2,128)(2,1)S(1)} %get-tuple-element.5, bf16[8,8,96]{2,1,0:T(8,128)(2,1)} %bitcast.78, bf16[8,8,96]{2,1,0:T(8,128)(2,1)S(1)} %get-tuple-element.8, ...), kind=kLoop, calls=%fused_computation.26 | loop fusion | flops 322560 | bytes 83768 | tf_op jit(solution)/shard_map/add | solution.py:113
  4.5 7.3 %all-to-all-start = ((bf16[8,28,96]{2,1,0:T(8,128)(2,1)}), bf16[8,28,96]{2,1,0:T(8,128)(2,1)S(1)}, u32[]{:S(2)}, u32[]{:S(2)}) async-start(bf16[8,28,96]{2,1,0:T(8,128)(2,1)} %fusion.15), calls=%async_computation | async-start | bytes 131072 | tf_op jit(solution)/shard_map/all_to_all | solution.py:115
  11.8 0.8 %eq.46 = s32[768]{0:T(1024)S(1)} reshape(s32[1,1,8,96]{3,2,1,0:T(8,128)} %param.13) | data formatting | bytes 6144 | tf_op jit(solution)/shard_map/eq | solution.py:118
  12.6 1.2 %convolution_convert_fusion.2 = bf16[2,256,256]{1,2,0:T(8,128)(2,1)S(1)} fusion(bf16[2,256,256]{2,1,0:T(8,128)(2,1)} %constant.123.clone, bf16[1,256,256]{2,1,0:T(8,128)(2,1)S(1)} %copy-done), kind=kOutput, calls=%fused_computation.8 | convolution fusion | flops 67239936 | bytes 655360 | tf_op jit(solution)/shard_map/iyx,jkx->ijyk/dot_general | solution.py:37
  13.8 0.4 fusion.4
  14.2 0.5 %copy.20 = bf16[1,2,256,2,128]{4,1,3,2,0:T(2,128)(2,1)S(1)} copy(bf16[1,2,256,2,128]{2,1,4,3,0:T(2,128)(2,1)S(1)} %convert_element_type.148) | data formatting | bytes 524288 | tf_op jit(solution)/shard_map/convert_element_type | solution.py:47
  14.7 1.2 %fusion.3 = bf16[768,256]{1,0:T(8,128)(2,1)} fusion(s32[768]{0:T(1024)S(1)} %eq.46, bf16[64,8,2,128]{3,2,1,0:T(2,128)(2,1)S(1)} %bitcast.73), kind=kOutput, calls=%fused_computation.5 | convolution fusion | flops 201916416 | bytes 658432 | tf_op jit(solution)/shard_map/dot_general | solution.py:119
  15.9 2.8 %all-to-all-done = bf16[8,28,96]{2,1,0:T(8,128)(2,1)S(1)} async-done(((bf16[8,28,96]{2,1,0:T(8,128)(2,1)}), bf16[8,28,96]{2,1,0:T(8,128)(2,1)S(1)}, u32[]{:S(2)}, u32[]{:S(2)}) %all-to-all-start) | async-done | bytes 43040 | tf_op jit(solution)/shard_map/all_to_all | solution.py:115
  18.7 3.5 %all-to-all-start.1 = ((bf16[8,96,256]{2,1,0:T(8,128)(2,1)}), bf16[8,96,256]{2,1,0:T(8,128)(2,1)S(1)}, u32[]{:S(2)}, u32[]{:S(2)}) async-start(bf16[8,96,256]{2,1,0:T(8,128)(2,1)} %bitcast.18), calls=%async_computation.1 | async-start | bytes 786432 | tf_op jit(solution)/shard_map/all_to_all | solution.py:121
  22.3 3.6 %sine_negate_fusion = f32[8,96,128]{2,1,0:T(8,128)S(1)} fusion(f32[8,96]{1,0:T(8,128)S(1)} %fusion.26, s32[8,96]{1,0:T(8,128)S(1)} %fusion.22, f32[8,96]{1,0:T(8,128)S(1)} %bitcast.76), kind=kLoop, calls=%fused_computation.17 | loop fusion | flops 884736 | bytes 402432 | tf_op jit(solution)/shard_map/neg | solution.py:57
  26.1 0.3 mul.96
  26.4 0.6 %mul.97 = f32[8,96,256]{2,1,0:T(8,128)S(1)} reshape(f32[8,96,2,128]{3,2,1,0:T(2,128)S(1)} %mul.96) | data formatting | bytes 1572864 | tf_op jit(solution)/shard_map/mul | solution.py:65
  27.0 1.7 %fusion.1 = bf16[512,768]{1,0:T(8,128)(2,1)S(1)} fusion(s32[8,768]{1,0:T(8,128)S(1)} %eq.42, bf16[8,768]{1,0:T(8,128)(2,1)S(1)} %broadcast_in_dim.22), kind=kLoop, calls=%fused_computation.2 | loop fusion | flops 9043968 | bytes 823296 | tf_op jit(solution)/shard_map/reduce_sum | solution.py:80
  28.7 0.4 convolution_convert_fusion
  29.1 3.9 %all-to-all-done.1 = bf16[8,96,256]{2,1,0:T(8,128)(2,1)S(1)} async-done(((bf16[8,96,256]{2,1,0:T(8,128)(2,1)}), bf16[8,96,256]{2,1,0:T(8,128)(2,1)S(1)}, u32[]{:S(2)}, u32[]{:S(2)}) %all-to-all-start.1) | async-done | bytes 393248 | tf_op jit(solution)/shard_map/all_to_all | solution.py:121
  33.2 0.4 fusion.33
  33.7 1.9 %collective-permute-done = f32[512,256]{1,0:T(8,128)S(1)} collective-permute-done((f32[512,256]{1,0:T(8,128)S(1)}, f32[512,256]{1,0:T(8,128)S(1)}, u32[]{:S(2)}, u32[]{:S(2)}) %collective-permute-start) | collective-permute-done | bytes 524320 | tf_op jit(solution)/shard_map/ppermute | solution.py:143
  35.6 1.6 %collective-permute-start.1 = (bf16[256,256]{1,0:T(8,128)(2,1)S(1)}, bf16[256,256]{1,0:T(8,128)(2,1)S(1)}, u32[]{:S(2)}, u32[]{:S(2)}) collective-permute-start(bf16[256,256]{1,0:T(8,128)(2,1)S(1)} %fusion.12), channel_id=1, source_target_pairs={{0,2},{1,3},{2,0},{3,1},{4,6},{5,7},{6,4},{7,5},{8,10},{9,11},{10,... | collective-permute-start | bytes 393224 | tf_op jit(solution)/shard_map/ppermute | solution.py:147
  37.2 4.0 %collective-permute-done.1 = bf16[256,256]{1,0:T(8,128)(2,1)S(1)} collective-permute-done((bf16[256,256]{1,0:T(8,128)(2,1)S(1)}, bf16[256,256]{1,0:T(8,128)(2,1)S(1)}, u32[]{:S(2)}, u32[]{:S(2)}) %collective-permute-start.1) | collective-permute-done | bytes 131104 | tf_op jit(solution)/shard_map/ppermute | solution.py:147
  41.3 1.5 %collective-permute-done.2 = f32[256,256]{1,0:T(8,128)S(1)} collective-permute-done((f32[256,256]{1,0:T(8,128)S(1)}, f32[256,256]{1,0:T(8,128)S(1)}, u32[]{:S(2)}, u32[]{:S(2)}) %collective-permute-start.2) | collective-permute-done | bytes 262176 | tf_op jit(solution)/shard_map/ppermute | solution.py:149
  42.8 0.8 %maximum_select_fusion = f32[512,256]{1,0:T(8,128)} fusion(f32[256,256]{1,0:T(8,128)S(1)} %collective-permute-done.2, f32[256,256]{1,0:T(8,128)S(1)} %add_subtract_fusion, pred[]{:T(512)S(6)} %eq.41), kind=kLoop, calls=%fused_computation.16 | loop fusion | flops 393216 | bytes 1048577 | tf_op jit(solution)/shard_map/jit(_where)/select_n | solution.py:150
  (28 shorter events, 0.8 us)
Async XLA Ops:
  0.0 12.6 %copy-start = (bf16[1,256,256]{2,1,0:T(8,128)(2,1)S(1)}, bf16[1,256,256]{2,1,0:T(8,128)(2,1)}, u32[]{:S(2)}) copy-start(bf16[1,256,256]{2,1,0:T(8,128)(2,1)} %param.9) | copy-start | bytes 393220
  0.0 13.8 %copy-start.2 = (bf16[512,512]{1,0:T(8,128)(2,1)S(1)}, bf16[512,512]{1,0:T(8,128)(2,1)}, u32[]{:S(2)}) copy-start(bf16[512,512]{1,0:T(8,128)(2,1)} %constant.124.clone) | copy-start | bytes 1572868
  4.5 14.2 %all-to-all-start = ((bf16[8,28,96]{2,1,0:T(8,128)(2,1)}), bf16[8,28,96]{2,1,0:T(8,128)(2,1)S(1)}, u32[]{:S(2)}, u32[]{:S(2)}) async-start(bf16[8,28,96]{2,1,0:T(8,128)(2,1)} %fusion.15), calls=%async_computation | async-start | bytes 131072 | tf_op jit(solution)/shard_map/all_to_all | solution.py:115
  18.7 14.3 %all-to-all-start.1 = ((bf16[8,96,256]{2,1,0:T(8,128)(2,1)}), bf16[8,96,256]{2,1,0:T(8,128)(2,1)S(1)}, u32[]{:S(2)}, u32[]{:S(2)}) async-start(bf16[8,96,256]{2,1,0:T(8,128)(2,1)} %bitcast.18), calls=%async_computation.1 | async-start | bytes 786432 | tf_op jit(solution)/shard_map/all_to_all | solution.py:121
  27.0 1.7 %copy-start.1 = (f32[512,256]{1,0:T(8,128)S(1)}, f32[512,256]{1,0:T(8,128)}, u32[]{:S(2)}) copy-start(f32[512,256]{1,0:T(8,128)} %param.11) | copy-start | bytes 1572868
  33.6 2.0 %collective-permute-start = (f32[512,256]{1,0:T(8,128)S(1)}, f32[512,256]{1,0:T(8,128)S(1)}, u32[]{:S(2)}, u32[]{:S(2)}) collective-permute-start(f32[512,256]{1,0:T(8,128)S(1)} %fusion.33), channel_id=1, source_target_pairs={{0,1},{1,0},{2,3},{3,2},{4,5},{5,4},{6,7},{7,6},{8,9},{9,8},{10,11... | collective-permute-start | bytes 1572872 | tf_op jit(solution)/shard_map/ppermute | solution.py:143
  35.6 5.6 %collective-permute-start.1 = (bf16[256,256]{1,0:T(8,128)(2,1)S(1)}, bf16[256,256]{1,0:T(8,128)(2,1)S(1)}, u32[]{:S(2)}, u32[]{:S(2)}) collective-permute-start(bf16[256,256]{1,0:T(8,128)(2,1)S(1)} %fusion.12), channel_id=1, source_target_pairs={{0,2},{1,3},{2,0},{3,1},{4,6},{5,7},{6,4},{7,5},{8,10},{9,11},{10,... | collective-permute-start | bytes 393224 | tf_op jit(solution)/shard_map/ppermute | solution.py:147
  41.2 1.6 %collective-permute-start.2 = (f32[256,256]{1,0:T(8,128)S(1)}, f32[256,256]{1,0:T(8,128)S(1)}, u32[]{:S(2)}, u32[]{:S(2)}) collective-permute-start(f32[256,256]{1,0:T(8,128)S(1)} %add_subtract_fusion), channel_id=1, source_target_pairs={{0,1},{1,0},{2,3},{3,2},{4,5},{5,4},{6,7},{7,6},{8,9},{9,8},{10,11... | collective-permute-start | bytes 786440 | tf_op jit(solution)/shard_map/ppermute | solution.py:149

commit v10 on v9

--- a/solution.py
+++ b/solution.py
@@ -112,13 +112,20 @@
         rows_of = piece.shape[1]
         meta = meta + jnp.pad(piece, ((0, 0), (offset, fields - offset - rows_of), (0, 0)))
         offset += rows_of
-    got_meta = lax.all_to_all(meta, "vol", split_axis=0, concat_axis=0, tiled=True)
     observed = transform(images, first, second)
     flat_pixels = pixel_ids.reshape(-1)
     onehot = (flat_pixels[:, None] == jnp.arange(observed.shape[0], dtype=jnp.int32)[None, :])
     rows = jnp.dot(onehot.astype(jnp.bfloat16), observed, preferred_element_type=jnp.float32)
     rows = rows.astype(jnp.bfloat16).reshape(owners, capacity, width)
-    got_rows = lax.all_to_all(rows, "vol", split_axis=0, concat_axis=0, tiled=True)
+    meta_rows = -(-fields * capacity // width)
+    flat_meta = meta.reshape(owners, fields * capacity)
+    flat_meta = jnp.pad(flat_meta, ((0, 0), (0, meta_rows * width - fields * capacity)))
+    packet = jnp.concatenate([rows, flat_meta.reshape(owners, meta_rows, width)], axis=1)
+    got = lax.all_to_all(packet, "vol", split_axis=0, concat_axis=0, tiled=True)
+    extract = lax.optimization_barrier(extract)
+    got_rows = got[:, :capacity]
+    got_meta = got[:, capacity:].reshape(owners, meta_rows * width)[:, : fields * capacity]
+    got_meta = got_meta.reshape(owners, fields, capacity)
     whole = got_meta[:, : 2 * taps].astype(jnp.int32)
     got_taps = whole[:, :taps] * 256 + whole[:, taps:]
     got_weights = got_meta[:, 2 * taps : 3 * taps]

time: 44.2 us -> 46.8 us (1.059)
  waiting for transfers between devices: 14.2 us -> 20.5 us
  starting transfers between devices: 12.4 us -> 8.97 us
  matrix products: 3.53 us -> 2.79 us
    all_to_all x2 -> x1, waiting for transfers between devices: 6.73 us -> 13 us  [local(): got = lax.all_to_all(packet, 'vol', split_axis=0, concat_axis=0, tiled=True)]
    all_to_all x2 -> x1, starting transfers between devices: 10.7 us -> 7.28 us  [local(): got = lax.all_to_all(packet, 'vol', split_axis=0, concat_axis=0, tiled=True)]
    concatenate x0 -> x1, other arithmetic: none -> 0.8 us  [local(): jnp.concatenate([rows, flat_meta.reshape(owners, meta_rows, width)], axis=1)]
    dot_general x1, matrix products: 1.19 us -> 0.44 us  [local(): jnp.dot(onehot.astype(jnp.bfloat16), observed, preferred_element_type=jnp...]
    add x1, other arithmetic: 1.42 us -> 0.8 us  [local(): meta + jnp.pad(piece, ((0, 0), (offset, fields - offset - rows_of), (0, 0)))]
  transfers between devices with their start and end apart: 5 -> 4, of which waited for: 5 -> 4; matrix products, arithmetic and copies ran while one was open for 25% -> 0% of each run, Pallas kernels for 0% -> 0%
where the time goes in v10:
time: 46.8 us; the launch traced here: 46.4 us
  waiting for transfers between devices  20.5 us (44%)
  other arithmetic  10.3 us (22%)
  starting transfers between devices  8.97 us (19%)
  local copies, waits for them, and re-layouts  2.81 us (6%)
  matrix products  2.79 us (6%)
  between operations  1.03 us (2%)
    all_to_all x1, waiting for transfers between devices, local(): got = lax.all_to_all(packet, 'vol', split_axis=0, concat_axis=0, tiled=True)  13 us
    all_to_all x1, starting transfers between devices, local(): got = lax.all_to_all(packet, 'vol', split_axis=0, concat_axis=0, tiled=True)  7.28 us
    ppermute x1, waiting for transfers between devices, local(): lax.ppermute(mine, 'ptcl', across).astype(jnp.float32)  4.05 us
    neg x1, other arithmetic, ctf_rows(): -jnp.sin(math.pi * focus.astype(jnp.float32)[..., None] * radius + phase_...  3.56 us
    ppermute x1, waiting for transfers between devices, local(): pair_sum = gradient + lax.ppermute(gradient, 'ptcl', on_chip)  1.88 us
    reduce_sum x1, other arithmetic, tap_matrix_t(): return jnp.sum(picked, axis=0, dtype=jnp.bfloat16)  1.66 us
    ppermute x1, starting transfers between devices, local(): lax.ppermute(mine, 'ptcl', across).astype(jnp.float32)  1.55 us
    convert_element_type x2, other arithmetic, split_whole(): (values // 256).astype(jnp.bfloat16)  1.52 us
  transfers between devices with their start and end apart: 4, of which 4 were waited for; matrix products, arithmetic and copies ran while one was open for 0% of the time, Pallas kernels for 0%

profile of v10, /device:TPU:0, one launch (start us, length us, event | category | flops | bytes accessed | tf_op | source)
XLA Modules:
  0.0 46.4 jit_solution(479869348170565516)
XLA Ops:
  0.7 0.7 %iota_compare_fusion.5 = pred[8,1,96]{2,1,0:T(4,128)(4,1)S(1)} fusion(s32[8]{0:T(128)} %bitcast.87), kind=kLoop, calls=%fused_computation.71 | loop fusion | flops 768 | bytes 800 | tf_op jit(solution)/shard_map/lt | solution.py:96
  1.5 0.8 %eq.42 = s32[768]{0:T(1024)S(1)} reshape(s32[1,1,8,96]{3,2,1,0:T(8,128)} %param.13) | data formatting | bytes 6144 | tf_op jit(solution)/shard_map/eq | solution.py:117
  2.2 0.7 %fusion.30 = (bf16[8,1,96]{2,1,0:T(2,128)(2,1)S(1)}, s32[8,1,96]{2,1,0:T(1,128)S(1)}) fusion(s32[8,1,96]{2,1,0:T(1,128)} %bitcast.84), kind=kLoop, calls=%fused_computation.74 | loop fusion | flops 20736 | bytes 7680 | tf_op jit(solution)/shard_map/convert_element_type | solution.py:84
  3.0 0.8 %fusion.15 = (bf16[8,8,96]{2,1,0:T(8,128)(2,1)S(1)}, bf16[8,8,96]{2,1,0:T(8,128)(2,1)S(1)}) fusion(s32[1,1,8,8,96]{4,3,2,1,0:T(8,128)} %param.14), kind=kLoop, calls=%fused_computation.32 | loop fusion | flops 129024 | bytes 49152 | tf_op jit(solution)/shard_map/convert_element_type | solution.py:84
  3.9 0.8 %fusion.14 = bf16[8,28,96]{2,1,0:T(8,128)(2,1)S(1)} fusion(pred[8,1,96]{2,1,0:T(4,128)(4,1)S(1)} %iota_compare_fusion.5, bf16[8,1,96]{2,1,0:T(2,128)(2,1)S(1)} %fusion.26, bf16[8,1,96]{2,1,0:T(2,128)(2,1)S(1)} %get-tuple-element.5, bf16[8,8,96]{2,1,0:T(8,128)(2,1)} %bitcast.85, bf16[8,8,96]{2,1,0:T(8,128)(2,1)S(1)} %get-tuple-element.8, ...), kind=kLoop, calls=%fused_computation.26 | loop fusion | flops 322560 | bytes 83768 | tf_op jit(solution)/shard_map/add | solution.py:113
  4.8 1.2 %convolution_convert_fusion.2 = bf16[2,256,256]{1,2,0:T(8,128)(2,1)S(1)} fusion(bf16[2,256,256]{2,1,0:T(8,128)(2,1)} %constant.123.clone, bf16[1,256,256]{2,1,0:T(8,128)(2,1)S(1)} %copy-done), kind=kOutput, calls=%fused_computation.8 | convolution fusion | flops 67239936 | bytes 655360 | tf_op jit(solution)/shard_map/iyx,jkx->ijyk/dot_general | solution.py:37
  6.1 0.3 fusion.4
  6.5 0.5 %copy.34 = bf16[1,2,256,2,128]{4,1,3,2,0:T(2,128)(2,1)S(1)} copy(bf16[1,2,256,2,128]{2,1,4,3,0:T(2,128)(2,1)S(1)} %convert_element_type.137) | data formatting | bytes 524288 | tf_op jit(solution)/shard_map/convert_element_type | solution.py:47
  7.0 0.4 fusion.3
  7.4 0.8 %pad_maximum_fusion = bf16[8,107,256]{2,1,0:T(8,128)(2,1)} fusion(bf16[8,11,256]{2,1,0:T(8,128)(2,1)S(1)} %copy.35, bf16[8,96,256]{2,1,0:T(8,128)(2,1)S(1)} %bitcast.77), kind=kLoop, calls=%fused_computation.17 | loop fusion | flops 876544 | bytes 876544 | tf_op jit(solution)/shard_map/concatenate | solution.py:123
  8.2 7.3 %all-to-all-start = ((bf16[8,107,256]{2,1,0:T(8,128)(2,1)}), bf16[8,107,256]{2,1,0:T(8,128)(2,1)S(1)}, u32[]{:S(2)}, u32[]{:S(2)}) async-start(bf16[8,107,256]{2,1,0:T(8,128)(2,1)} %pad_maximum_fusion), calls=%async_computation | async-start | bytes 917504 | tf_op jit(solution)/shard_map/all_to_all | solution.py:124
  15.6 13.0 %all-to-all-done = bf16[8,107,256]{2,1,0:T(8,128)(2,1)S(1)} async-done(((bf16[8,107,256]{2,1,0:T(8,128)(2,1)}), bf16[8,107,256]{2,1,0:T(8,128)(2,1)S(1)}, u32[]{:S(2)}, u32[]{:S(2)}) %all-to-all-start) | async-done | bytes 438304 | tf_op jit(solution)/shard_map/all_to_all | solution.py:124
  29.1 3.6 %sine_negate_fusion = f32[8,96,128]{2,1,0:T(8,128)S(1)} fusion(f32[8,96]{1,0:T(8,128)S(1)} %fusion.25, s32[8,96]{1,0:T(8,128)S(1)} %fusion.21, f32[8,96]{1,0:T(8,128)S(1)} %bitcast.83), kind=kLoop, calls=%fused_computation.18 | loop fusion | flops 884736 | bytes 402432 | tf_op jit(solution)/shard_map/neg | solution.py:57
  32.7 0.3 mul.96
  33.0 0.6 %mul.97 = f32[8,96,256]{2,1,0:T(8,128)S(1)} reshape(f32[8,96,2,128]{3,2,1,0:T(2,128)S(1)} %mul.96) | data formatting | bytes 1572864 | tf_op jit(solution)/shard_map/mul | solution.py:65
  33.6 1.7 %fusion.1 = bf16[512,768]{1,0:T(8,128)(2,1)S(1)} fusion(s32[8,768]{1,0:T(8,128)S(1)} %eq.46, bf16[8,768]{1,0:T(8,128)(2,1)S(1)} %broadcast_in_dim.22), kind=kLoop, calls=%fused_computation.2 | loop fusion | flops 9043968 | bytes 823296 | tf_op jit(solution)/shard_map/reduce_sum | solution.py:80
  35.3 0.4 convolution_convert_fusion
  35.7 0.2 fusion.8
  35.9 0.4 fusion.32
  36.4 1.9 %collective-permute-done = f32[512,256]{1,0:T(8,128)S(1)} collective-permute-done((f32[512,256]{1,0:T(8,128)S(1)}, f32[512,256]{1,0:T(8,128)S(1)}, u32[]{:S(2)}, u32[]{:S(2)}) %collective-permute-start) | collective-permute-done | bytes 524320 | tf_op jit(solution)/shard_map/ppermute | solution.py:150
  38.3 1.6 %collective-permute-start.1 = (bf16[256,256]{1,0:T(8,128)(2,1)S(1)}, bf16[256,256]{1,0:T(8,128)(2,1)S(1)}, u32[]{:S(2)}, u32[]{:S(2)}) collective-permute-start(bf16[256,256]{1,0:T(8,128)(2,1)S(1)} %fusion.12), channel_id=1, source_target_pairs={{0,2},{1,3},{2,0},{3,1},{4,6},{5,7},{6,4},{7,5},{8,10},{9,11},{10,... | collective-permute-start | bytes 393224 | tf_op jit(solution)/shard_map/ppermute | solution.py:154
  39.9 4.0 %collective-permute-done.1 = bf16[256,256]{1,0:T(8,128)(2,1)S(1)} collective-permute-done((bf16[256,256]{1,0:T(8,128)(2,1)S(1)}, bf16[256,256]{1,0:T(8,128)(2,1)S(1)}, u32[]{:S(2)}, u32[]{:S(2)}) %collective-permute-start.1) | collective-permute-done | bytes 131104 | tf_op jit(solution)/shard_map/ppermute | solution.py:154
  44.0 1.5 %collective-permute-done.2 = f32[256,256]{1,0:T(8,128)S(1)} collective-permute-done((f32[256,256]{1,0:T(8,128)S(1)}, f32[256,256]{1,0:T(8,128)S(1)}, u32[]{:S(2)}, u32[]{:S(2)}) %collective-permute-start.2) | collective-permute-done | bytes 262176 | tf_op jit(solution)/shard_map/ppermute | solution.py:156
  45.5 0.8 %maximum_select_fusion = f32[512,256]{1,0:T(8,128)} fusion(f32[256,256]{1,0:T(8,128)S(1)} %collective-permute-done.2, f32[256,256]{1,0:T(8,128)S(1)} %add_subtract_fusion, pred[]{:T(512)S(6)} %eq.41), kind=kLoop, calls=%fused_computation.16 | loop fusion | flops 393216 | bytes 1048577 | tf_op jit(solution)/shard_map/jit(_where)/select_n | solution.py:157
  (35 shorter events, 1.0 us)
Async XLA Ops:
  0.0 4.8 %copy-start = (bf16[1,256,256]{2,1,0:T(8,128)(2,1)S(1)}, bf16[1,256,256]{2,1,0:T(8,128)(2,1)}, u32[]{:S(2)}) copy-start(bf16[1,256,256]{2,1,0:T(8,128)(2,1)} %param.9) | copy-start | bytes 393220
  0.0 6.1 %copy-start.2 = (bf16[512,512]{1,0:T(8,128)(2,1)S(1)}, bf16[512,512]{1,0:T(8,128)(2,1)}, u32[]{:S(2)}) copy-start(bf16[512,512]{1,0:T(8,128)(2,1)} %constant.124.clone) | copy-start | bytes 1572868
  7.4 8.1 %copy-start.1 = (f32[512,256]{1,0:T(8,128)S(1)}, f32[512,256]{1,0:T(8,128)}, u32[]{:S(2)}) copy-start(f32[512,256]{1,0:T(8,128)} %param.11) | copy-start | bytes 1572868
  8.2 20.4 %all-to-all-start = ((bf16[8,107,256]{2,1,0:T(8,128)(2,1)}), bf16[8,107,256]{2,1,0:T(8,128)(2,1)S(1)}, u32[]{:S(2)}, u32[]{:S(2)}) async-start(bf16[8,107,256]{2,1,0:T(8,128)(2,1)} %pad_maximum_fusion), calls=%async_computation | async-start | bytes 917504 | tf_op jit(solution)/shard_map/all_to_all | solution.py:124
  36.3 2.0 %collective-permute-start = (f32[512,256]{1,0:T(8,128)S(1)}, f32[512,256]{1,0:T(8,128)S(1)}, u32[]{:S(2)}, u32[]{:S(2)}) collective-permute-start(f32[512,256]{1,0:T(8,128)S(1)} %fusion.32), channel_id=1, source_target_pairs={{0,1},{1,0},{2,3},{3,2},{4,5},{5,4},{6,7},{7,6},{8,9},{9,8},{10,11... | collective-permute-start | bytes 1572872 | tf_op jit(solution)/shard_map/ppermute | solution.py:150
  38.3 5.6 %collective-permute-start.1 = (bf16[256,256]{1,0:T(8,128)(2,1)S(1)}, bf16[256,256]{1,0:T(8,128)(2,1)S(1)}, u32[]{:S(2)}, u32[]{:S(2)}) collective-permute-start(bf16[256,256]{1,0:T(8,128)(2,1)S(1)} %fusion.12), channel_id=1, source_target_pairs={{0,2},{1,3},{2,0},{3,1},{4,6},{5,7},{6,4},{7,5},{8,10},{9,11},{10,... | collective-permute-start | bytes 393224 | tf_op jit(solution)/shard_map/ppermute | solution.py:154
  43.9 1.6 %collective-permute-start.2 = (f32[256,256]{1,0:T(8,128)S(1)}, f32[256,256]{1,0:T(8,128)S(1)}, u32[]{:S(2)}, u32[]{:S(2)}) collective-permute-start(f32[256,256]{1,0:T(8,128)S(1)} %add_subtract_fusion), channel_id=1, source_target_pairs={{0,1},{1,0},{2,3},{3,2},{4,5},{5,4},{6,7},{7,6},{8,9},{9,8},{10,11... | collective-permute-start | bytes 786440 | tf_op jit(solution)/shard_map/ppermute | solution.py:156

commit v11 on v9

--- a/solution.py
+++ b/solution.py
@@ -144,7 +144,12 @@
         half = gradient.shape[0] // 2
         core = me % 2
         mine = lax.dynamic_slice_in_dim(pair_sum, core * half, half, axis=0).astype(jnp.bfloat16)
-        total = mine.astype(jnp.float32) + lax.ppermute(mine, "ptcl", across).astype(jnp.float32)
+        quarter = half // 2
+        crossed = jnp.concatenate(
+            [lax.ppermute(mine[:quarter], "ptcl", across), lax.ppermute(mine[quarter:], "ptcl", across)],
+            axis=0,
+        )
+        total = mine.astype(jnp.float32) + crossed.astype(jnp.float32)
         updated = lax.dynamic_slice_in_dim(volume, core * half, half, axis=0) - learn_rate * total
         other = lax.ppermute(updated, "ptcl", on_chip)
         return jnp.where(

time: 44.2 us -> 44.5 us (level)
  starting transfers between devices: 12.4 us -> 13 us
    ppermute x1 -> x2, starting transfers between devices: 1.55 us -> 2.09 us  [the longest x1 1.59 us: local(): lax.ppermute(mine[:quarter], 'ptcl', across)]
    ppermute x1 -> x2, waiting for transfers between devices: 4.05 us -> 3.76 us  [the longest x1 2.65 us: local(): lax.ppermute(mine[:quarter], 'ptcl', across)]
  transfers between devices with their start and end apart: 5 -> 6, of which waited for: 5 -> 6; matrix products, arithmetic and copies ran while one was open for 25% -> 25% of each run, Pallas kernels for 0% -> 0%
where the time goes in v11:
time: 44.5 us; the launch traced here: 44 us
  waiting for transfers between devices  13.9 us (31%)
  starting transfers between devices  13 us (29%)
  other arithmetic  10.1 us (23%)
  matrix products  3.53 us (8%)
  local copies, waits for them, and re-layouts  2.51 us (6%)
  between operations  0.99 us (2%)
    all_to_all x1, starting transfers between devices, local(): lax.all_to_all(meta, 'vol', split_axis=0, concat_axis=0, tiled=True)  7.28 us
    all_to_all x1, waiting for transfers between devices, local(): lax.all_to_all(rows, 'vol', split_axis=0, concat_axis=0, tiled=True)  3.92 us
    neg x1, other arithmetic, ctf_rows(): -jnp.sin(math.pi * focus.astype(jnp.float32)[..., None] * radius + phase_...  3.56 us
    all_to_all x1, starting transfers between devices, local(): lax.all_to_all(rows, 'vol', split_axis=0, concat_axis=0, tiled=True)  3.45 us
    all_to_all x1, waiting for transfers between devices, local(): lax.all_to_all(meta, 'vol', split_axis=0, concat_axis=0, tiled=True)  2.8 us
    ppermute x1, waiting for transfers between devices, local(): lax.ppermute(mine[:quarter], 'ptcl', across)  2.65 us
    ppermute x1, waiting for transfers between devices, local(): pair_sum = gradient + lax.ppermute(gradient, 'ptcl', on_chip)  1.88 us
    reduce_sum x1, other arithmetic, tap_matrix_t(): return jnp.sum(picked, axis=0, dtype=jnp.bfloat16)  1.66 us
  transfers between devices with their start and end apart: 6, of which 6 were waited for; matrix products, arithmetic and copies ran while one was open for 25% of the time, Pallas kernels for 0%

profile of v11, /device:TPU:0, one launch (start us, length us, event | category | flops | bytes accessed | tf_op | source)
XLA Modules:
  0.0 44.0 jit_solution(18282408409159726941)
XLA Ops:
  0.7 0.7 %iota_compare_fusion.5 = pred[8,1,96]{2,1,0:T(4,128)(4,1)S(1)} fusion(s32[8]{0:T(128)} %bitcast.79), kind=kLoop, calls=%fused_computation.70 | loop fusion | flops 768 | bytes 800 | tf_op jit(solution)/shard_map/lt | solution.py:96
  1.5 0.7 %fusion.31 = (bf16[8,1,96]{2,1,0:T(2,128)(2,1)S(1)}, s32[8,1,96]{2,1,0:T(1,128)S(1)}) fusion(s32[8,1,96]{2,1,0:T(1,128)} %bitcast.77), kind=kLoop, calls=%fused_computation.73 | loop fusion | flops 20736 | bytes 7680 | tf_op jit(solution)/shard_map/convert_element_type | solution.py:84
  2.2 0.8 %fusion.16 = (bf16[8,8,96]{2,1,0:T(8,128)(2,1)S(1)}, bf16[8,8,96]{2,1,0:T(8,128)(2,1)S(1)}) fusion(s32[1,1,8,8,96]{4,3,2,1,0:T(8,128)} %param.14), kind=kLoop, calls=%fused_computation.32 | loop fusion | flops 129024 | bytes 49152 | tf_op jit(solution)/shard_map/convert_element_type | solution.py:84
  3.1 1.4 %fusion.15 = bf16[8,28,96]{2,1,0:T(8,128)(2,1)} fusion(pred[8,1,96]{2,1,0:T(4,128)(4,1)S(1)} %iota_compare_fusion.5, bf16[8,1,96]{2,1,0:T(2,128)(2,1)S(1)} %fusion.27, bf16[8,1,96]{2,1,0:T(2,128)(2,1)S(1)} %get-tuple-element.5, bf16[8,8,96]{2,1,0:T(8,128)(2,1)} %bitcast.78, bf16[8,8,96]{2,1,0:T(8,128)(2,1)S(1)} %get-tuple-element.10, ...), kind=kLoop, calls=%fused_computation.26 | loop fusion | flops 322560 | bytes 83768 | tf_op jit(solution)/shard_map/add | solution.py:113
  4.5 7.3 %all-to-all-start = ((bf16[8,28,96]{2,1,0:T(8,128)(2,1)}), bf16[8,28,96]{2,1,0:T(8,128)(2,1)S(1)}, u32[]{:S(2)}, u32[]{:S(2)}) async-start(bf16[8,28,96]{2,1,0:T(8,128)(2,1)} %fusion.15), calls=%async_computation | async-start | bytes 131072 | tf_op jit(solution)/shard_map/all_to_all | solution.py:115
  11.8 0.8 %eq.46 = s32[768]{0:T(1024)S(1)} reshape(s32[1,1,8,96]{3,2,1,0:T(8,128)} %param.13) | data formatting | bytes 6144 | tf_op jit(solution)/shard_map/eq | solution.py:118
  12.6 1.2 %convolution_convert_fusion.2 = bf16[2,256,256]{1,2,0:T(8,128)(2,1)S(1)} fusion(bf16[2,256,256]{2,1,0:T(8,128)(2,1)} %constant.123.clone, bf16[1,256,256]{2,1,0:T(8,128)(2,1)S(1)} %copy-done), kind=kOutput, calls=%fused_computation.8 | convolution fusion | flops 67239936 | bytes 655360 | tf_op jit(solution)/shard_map/iyx,jkx->ijyk/dot_general | solution.py:37
  14.2 0.5 %copy.20 = bf16[1,2,256,2,128]{4,1,3,2,0:T(2,128)(2,1)S(1)} copy(bf16[1,2,256,2,128]{2,1,4,3,0:T(2,128)(2,1)S(1)} %convert_element_type.148) | data formatting | bytes 524288 | tf_op jit(solution)/shard_map/convert_element_type | solution.py:47
  14.7 1.2 %fusion.3 = bf16[768,256]{1,0:T(8,128)(2,1)} fusion(s32[768]{0:T(1024)S(1)} %eq.46, bf16[64,8,2,128]{3,2,1,0:T(2,128)(2,1)S(1)} %bitcast.73), kind=kOutput, calls=%fused_computation.5 | convolution fusion | flops 201916416 | bytes 658432 | tf_op jit(solution)/shard_map/dot_general | solution.py:119
  15.9 2.8 %all-to-all-done = bf16[8,28,96]{2,1,0:T(8,128)(2,1)S(1)} async-done(((bf16[8,28,96]{2,1,0:T(8,128)(2,1)}), bf16[8,28,96]{2,1,0:T(8,128)(2,1)S(1)}, u32[]{:S(2)}, u32[]{:S(2)}) %all-to-all-start) | async-done | bytes 43040 | tf_op jit(solution)/shard_map/all_to_all | solution.py:115
  18.7 3.5 %all-to-all-start.1 = ((bf16[8,96,256]{2,1,0:T(8,128)(2,1)}), bf16[8,96,256]{2,1,0:T(8,128)(2,1)S(1)}, u32[]{:S(2)}, u32[]{:S(2)}) async-start(bf16[8,96,256]{2,1,0:T(8,128)(2,1)} %bitcast.18), calls=%async_computation.1 | async-start | bytes 786432 | tf_op jit(solution)/shard_map/all_to_all | solution.py:121
  22.3 3.6 %sine_negate_fusion = f32[8,96,128]{2,1,0:T(8,128)S(1)} fusion(f32[8,96]{1,0:T(8,128)S(1)} %fusion.26, s32[8,96]{1,0:T(8,128)S(1)} %fusion.22, f32[8,96]{1,0:T(8,128)S(1)} %bitcast.76), kind=kLoop, calls=%fused_computation.17 | loop fusion | flops 884736 | bytes 402432 | tf_op jit(solution)/shard_map/neg | solution.py:57
  26.4 0.6 %mul.97 = f32[8,96,256]{2,1,0:T(8,128)S(1)} reshape(f32[8,96,2,128]{3,2,1,0:T(2,128)S(1)} %mul.96) | data formatting | bytes 1572864 | tf_op jit(solution)/shard_map/mul | solution.py:65
  27.0 1.7 %fusion.1 = bf16[512,768]{1,0:T(8,128)(2,1)S(1)} fusion(s32[8,768]{1,0:T(8,128)S(1)} %eq.42, bf16[8,768]{1,0:T(8,128)(2,1)S(1)} %broadcast_in_dim.22), kind=kLoop, calls=%fused_computation.2 | loop fusion | flops 9043968 | bytes 823296 | tf_op jit(solution)/shard_map/reduce_sum | solution.py:80
  28.7 0.4 convolution_convert_fusion
  29.1 3.9 %all-to-all-done.1 = bf16[8,96,256]{2,1,0:T(8,128)(2,1)S(1)} async-done(((bf16[8,96,256]{2,1,0:T(8,128)(2,1)}), bf16[8,96,256]{2,1,0:T(8,128)(2,1)S(1)}, u32[]{:S(2)}, u32[]{:S(2)}) %all-to-all-start.1) | async-done | bytes 393248 | tf_op jit(solution)/shard_map/all_to_all | solution.py:121
  33.2 0.4 fusion.34
  33.7 1.9 %collective-permute-done = f32[512,256]{1,0:T(8,128)S(1)} collective-permute-done((f32[512,256]{1,0:T(8,128)S(1)}, f32[512,256]{1,0:T(8,128)S(1)}, u32[]{:S(2)}, u32[]{:S(2)}) %collective-permute-start) | collective-permute-done | bytes 524320 | tf_op jit(solution)/shard_map/ppermute | solution.py:143
  35.6 1.6 %collective-permute-start.1 = (bf16[128,256]{1,0:T(8,128)(2,1)S(1)}, bf16[128,256]{1,0:T(8,128)(2,1)S(1)}, u32[]{:S(2)}, u32[]{:S(2)}) collective-permute-start(bf16[128,256]{1,0:T(8,128)(2,1)S(1)} %get-tuple-element.7), channel_id=1, source_target_pairs={{0,2},{1,3},{2,0},{3,1},{4,6},{5,7},{6,4},{7,5},{8,10},{9,11},{10,... | collective-permute-start | bytes 196616 | tf_op jit(solution)/shard_map/ppermute | solution.py:149
  37.2 0.5 %collective-permute-start.2 = (bf16[128,256]{1,0:T(8,128)(2,1)S(1)}, bf16[128,256]{1,0:T(8,128)(2,1)S(1)}, u32[]{:S(2)}, u32[]{:S(2)}) collective-permute-start(bf16[128,256]{1,0:T(8,128)(2,1)S(1)} %get-tuple-element.8), channel_id=1, source_target_pairs={{0,2},{1,3},{2,0},{3,1},{4,6},{5,7},{6,4},{7,5},{8,10},{9,11},{10,... | collective-permute-start | bytes 196616 | tf_op jit(solution)/shard_map/ppermute | solution.py:149
  37.7 2.6 %collective-permute-done.1 = bf16[128,256]{1,0:T(8,128)(2,1)S(1)} collective-permute-done((bf16[128,256]{1,0:T(8,128)(2,1)S(1)}, bf16[128,256]{1,0:T(8,128)(2,1)S(1)}, u32[]{:S(2)}, u32[]{:S(2)}) %collective-permute-start.1) | collective-permute-done | bytes 65568 | tf_op jit(solution)/shard_map/ppermute | solution.py:149
  40.4 1.1 %collective-permute-done.2 = bf16[128,256]{1,0:T(8,128)(2,1)S(1)} collective-permute-done((bf16[128,256]{1,0:T(8,128)(2,1)S(1)}, bf16[128,256]{1,0:T(8,128)(2,1)S(1)}, u32[]{:S(2)}, u32[]{:S(2)}) %collective-permute-start.2) | collective-permute-done | bytes 65568 | tf_op jit(solution)/shard_map/ppermute | solution.py:149
  41.6 1.5 %collective-permute-done.3 = f32[256,256]{1,0:T(8,128)S(1)} collective-permute-done((f32[256,256]{1,0:T(8,128)S(1)}, f32[256,256]{1,0:T(8,128)S(1)}, u32[]{:S(2)}, u32[]{:S(2)}) %collective-permute-start.3) | collective-permute-done | bytes 262176 | tf_op jit(solution)/shard_map/ppermute | solution.py:154
  43.1 0.8 %maximum_select_fusion = f32[512,256]{1,0:T(8,128)} fusion(f32[256,256]{1,0:T(8,128)S(1)} %collective-permute-done.3, f32[256,256]{1,0:T(8,128)S(1)} %add_subtract_fusion, pred[]{:T(512)S(6)} %eq.41), kind=kLoop, calls=%fused_computation.16 | loop fusion | flops 393216 | bytes 1048577 | tf_op jit(solution)/shard_map/jit(_where)/select_n | solution.py:155
  (31 shorter events, 1.5 us)
Async XLA Ops:
  0.0 12.6 %copy-start = (bf16[1,256,256]{2,1,0:T(8,128)(2,1)S(1)}, bf16[1,256,256]{2,1,0:T(8,128)(2,1)}, u32[]{:S(2)}) copy-start(bf16[1,256,256]{2,1,0:T(8,128)(2,1)} %param.9) | copy-start | bytes 393220
  0.0 13.8 %copy-start.2 = (bf16[512,512]{1,0:T(8,128)(2,1)S(1)}, bf16[512,512]{1,0:T(8,128)(2,1)}, u32[]{:S(2)}) copy-start(bf16[512,512]{1,0:T(8,128)(2,1)} %constant.124.clone) | copy-start | bytes 1572868
  4.5 14.2 %all-to-all-start = ((bf16[8,28,96]{2,1,0:T(8,128)(2,1)}), bf16[8,28,96]{2,1,0:T(8,128)(2,1)S(1)}, u32[]{:S(2)}, u32[]{:S(2)}) async-start(bf16[8,28,96]{2,1,0:T(8,128)(2,1)} %fusion.15), calls=%async_computation | async-start | bytes 131072 | tf_op jit(solution)/shard_map/all_to_all | solution.py:115
  18.7 14.3 %all-to-all-start.1 = ((bf16[8,96,256]{2,1,0:T(8,128)(2,1)}), bf16[8,96,256]{2,1,0:T(8,128)(2,1)S(1)}, u32[]{:S(2)}, u32[]{:S(2)}) async-start(bf16[8,96,256]{2,1,0:T(8,128)(2,1)} %bitcast.18), calls=%async_computation.1 | async-start | bytes 786432 | tf_op jit(solution)/shard_map/all_to_all | solution.py:121
  27.0 1.7 %copy-start.1 = (f32[512,256]{1,0:T(8,128)S(1)}, f32[512,256]{1,0:T(8,128)}, u32[]{:S(2)}) copy-start(f32[512,256]{1,0:T(8,128)} %param.11) | copy-start | bytes 1572868
  33.6 2.0 %collective-permute-start = (f32[512,256]{1,0:T(8,128)S(1)}, f32[512,256]{1,0:T(8,128)S(1)}, u32[]{:S(2)}, u32[]{:S(2)}) collective-permute-start(f32[512,256]{1,0:T(8,128)S(1)} %fusion.34), channel_id=1, source_target_pairs={{0,1},{1,0},{2,3},{3,2},{4,5},{5,4},{6,7},{7,6},{8,9},{9,8},{10,11... | collective-permute-start | bytes 1572872 | tf_op jit(solution)/shard_map/ppermute | solution.py:143
  35.6 4.7 %collective-permute-start.1 = (bf16[128,256]{1,0:T(8,128)(2,1)S(1)}, bf16[128,256]{1,0:T(8,128)(2,1)S(1)}, u32[]{:S(2)}, u32[]{:S(2)}) collective-permute-start(bf16[128,256]{1,0:T(8,128)(2,1)S(1)} %get-tuple-element.7), channel_id=1, source_target_pairs={{0,2},{1,3},{2,0},{3,1},{4,6},{5,7},{6,4},{7,5},{8,10},{9,11},{10,... | collective-permute-start | bytes 196616 | tf_op jit(solution)/shard_map/ppermute | solution.py:149
  37.2 4.3 %collective-permute-start.2 = (bf16[128,256]{1,0:T(8,128)(2,1)S(1)}, bf16[128,256]{1,0:T(8,128)(2,1)S(1)}, u32[]{:S(2)}, u32[]{:S(2)}) collective-permute-start(bf16[128,256]{1,0:T(8,128)(2,1)S(1)} %get-tuple-element.8), channel_id=1, source_target_pairs={{0,2},{1,3},{2,0},{3,1},{4,6},{5,7},{6,4},{7,5},{8,10},{9,11},{10,... | collective-permute-start | bytes 196616 | tf_op jit(solution)/shard_map/ppermute | solution.py:149
  41.5 1.6 %collective-permute-start.3 = (f32[256,256]{1,0:T(8,128)S(1)}, f32[256,256]{1,0:T(8,128)S(1)}, u32[]{:S(2)}, u32[]{:S(2)}) collective-permute-start(f32[256,256]{1,0:T(8,128)S(1)} %add_subtract_fusion), channel_id=1, source_target_pairs={{0,1},{1,0},{2,3},{3,2},{4,5},{5,4},{6,7},{7,6},{8,9},{9,8},{10,11... | collective-permute-start | bytes 786440 | tf_op jit(solution)/shard_map/ppermute | solution.py:154

commit v12 on v9

--- a/solution.py
+++ b/solution.py
@@ -5,6 +5,8 @@
 import ml_dtypes
 import numpy as np
 from jax import lax
+from jax.experimental import pallas as pl
+from jax.experimental.pallas import tpu as pltpu
 from jax.sharding import PartitionSpec as P
 
 L = 256
@@ -84,6 +86,42 @@
     return (values // 256).astype(jnp.bfloat16), (values % 256).astype(jnp.bfloat16)
 
 
+def meta_kernel(counts_ref, taps_ref, weights_ref, pixel_ref, focus_ref, out_ref):
+    owners, taps, capacity = taps_ref.shape
+    out_ref[:, 0:taps, :] = taps_ref[...].astype(jnp.float32)
+    out_ref[:, taps : 2 * taps, :] = weights_ref[...].astype(jnp.float32)
+    pixels = pixel_ref[...]
+    image = pixels // PB
+    focus_all = focus_ref[...].astype(jnp.float32)
+    focus = jnp.zeros(pixels.shape, jnp.float32)
+    for index in range(focus_all.shape[1]):
+        focus = jnp.where(image == index, focus_all[:, index : index + 1], focus)
+    block = (pixels % PB).astype(jnp.float32)
+    lanes = lax.broadcasted_iota(jnp.int32, (1, capacity), 1)
+    for owner in range(owners):
+        out_ref[owner, 2 * taps : 2 * taps + 1, :] = block[owner : owner + 1]
+        out_ref[owner, 2 * taps + 1 : 2 * taps + 2, :] = focus[owner : owner + 1]
+        live = (lanes < counts_ref[owner]).astype(jnp.float32)
+        out_ref[owner, 2 * taps + 2 : 2 * taps + 3, :] = live
+
+
+def slot_meta(counts, tap_ids, weights, pixel_ids, defocus):
+    owners, taps, capacity = tap_ids.shape
+    vmem = pltpu.MemorySpace.VMEM
+    return pl.pallas_call(
+        meta_kernel,
+        out_shape=jax.ShapeDtypeStruct((owners, 2 * taps + 3, capacity), jnp.float32),
+        in_specs=[
+            pl.BlockSpec(memory_space=pltpu.MemorySpace.SMEM),
+            pl.BlockSpec(memory_space=vmem),
+            pl.BlockSpec(memory_space=vmem),
+            pl.BlockSpec(memory_space=vmem),
+            pl.BlockSpec(memory_space=vmem),
+        ],
+        out_specs=pl.BlockSpec(memory_space=vmem),
+    )(counts, tap_ids, weights, pixel_ids, defocus.reshape(1, -1))
+
+
 def local(images, defocus, volume, counts, slot_pixel, slot_taps, slot_weights):
     first, second = dft_tables()
     extract = volume.astype(jnp.bfloat16)
@@ -93,25 +131,7 @@
     tap_ids = slot_taps[0, 0]
     weights = slot_weights[0, 0]
     owners, taps, capacity = tap_ids.shape
-    live_slots = jnp.arange(capacity, dtype=jnp.int32)[None, :] < slot_count[:, None]
-    tap_hi, tap_lo = split_whole(tap_ids)
-    block_hi, block_lo = split_whole(pixel_ids % PB)
-    pieces = [
-        tap_hi,
-        tap_lo,
-        weights,
-        block_hi[:, None, :],
-        block_lo[:, None, :],
-        defocus[pixel_ids // PB][:, None, :],
-        live_slots.astype(jnp.bfloat16)[:, None, :],
-    ]
-    fields = sum(piece.shape[1] for piece in pieces)
-    meta = jnp.zeros((owners, fields, capacity), jnp.bfloat16)
-    offset = 0
-    for piece in pieces:
-        rows_of = piece.shape[1]
-        meta = meta + jnp.pad(piece, ((0, 0), (offset, fields - offset - rows_of), (0, 0)))
-        offset += rows_of
+    meta = slot_meta(slot_count, tap_ids, weights, pixel_ids, defocus)
     got_meta = lax.all_to_all(meta, "vol", split_axis=0, concat_axis=0, tiled=True)
     observed = transform(images, first, second)
     flat_pixels = pixel_ids.reshape(-1)
@@ -119,13 +139,11 @@
     rows = jnp.dot(onehot.astype(jnp.bfloat16), observed, preferred_element_type=jnp.float32)
     rows = rows.astype(jnp.bfloat16).reshape(owners, capacity, width)
     got_rows = lax.all_to_all(rows, "vol", split_axis=0, concat_axis=0, tiled=True)
-    whole = got_meta[:, : 2 * taps].astype(jnp.int32)
-    got_taps = whole[:, :taps] * 256 + whole[:, taps:]
-    got_weights = got_meta[:, 2 * taps : 3 * taps]
-    block_parts = got_meta[:, 3 * taps : 3 * taps + 2].astype(jnp.int32)
-    got_block = block_parts[:, 0] * 256 + block_parts[:, 1]
-    got_focus = got_meta[:, 3 * taps + 2]
-    got_live = got_meta[:, 3 * taps + 3] > 0.5
+    got_taps = got_meta[:, :taps].astype(jnp.int32)
+    got_weights = got_meta[:, taps : 2 * taps].astype(jnp.bfloat16)
+    got_block = got_meta[:, 2 * taps].astype(jnp.int32)
+    got_focus = got_meta[:, 2 * taps + 1]
+    got_live = got_meta[:, 2 * taps + 2] > 0.5
     matrix_t = tap_matrix_t(got_taps, got_weights, volume.shape[0])
     prediction = lax.dot_general(
         matrix_t, extract, (((0,), (0,)), ((), ())), preferred_element_type=jnp.float32

time: 44.2 us -> 41.8 us (0.946)
  other arithmetic: 10.1 us -> 6.37 us
  Pallas kernels: 0 us -> 1.47 us
    convert_element_type x5 -> x0, other arithmetic: 1.56 us -> none  [the longest x2 1.53 us: split_whole(): (values // 256).astype(jnp.bfloat16)]
    pallas_call x0 -> x1, Pallas kernels: none -> 1.47 us  [slot_meta(): pl.pallas_call(meta_kernel, out_shape=jax.ShapeDtypeStruct((owners, 2 * t...]
    add x2 -> x0, other arithmetic: 1.42 us -> none  [the longest x1 1.42 us: local(): meta + jnp.pad(piece, ((0, 0), (offset, fields - offset - rows_of), (0, 0)))]
    lt x1 -> x0, other arithmetic: 0.73 us -> none  [local(): jnp.arange(capacity, dtype=jnp.int32)[None, :] < slot_count[:, None]]
  transfers between devices with their start and end apart: 5 -> 5, of which waited for: 5 -> 5; matrix products, arithmetic and copies ran while one was open for 25% -> 26% of each run, Pallas kernels for 0% -> 0%
where the time goes in v12:
time: 41.8 us; the launch traced here: 41.4 us
  waiting for transfers between devices  14.2 us (34%)
  starting transfers between devices  12.4 us (30%)
  other arithmetic  6.37 us (15%)
  matrix products  3.54 us (8%)
  local copies, waits for them, and re-layouts  2.42 us (6%)
  Pallas kernels  1.47 us (4%)
  between operations  0.93 us (2%)
    all_to_all x1, starting transfers between devices, local(): lax.all_to_all(meta, 'vol', split_axis=0, concat_axis=0, tiled=True)  7.28 us
    ppermute x1, waiting for transfers between devices, local(): lax.ppermute(mine, 'ptcl', across).astype(jnp.float32)  4.05 us
    all_to_all x1, waiting for transfers between devices, local(): lax.all_to_all(rows, 'vol', split_axis=0, concat_axis=0, tiled=True)  3.75 us
    neg x1, other arithmetic, ctf_rows(): -jnp.sin(math.pi * focus.astype(jnp.float32)[..., None] * radius + phase_...  3.56 us
    all_to_all x1, starting transfers between devices, local(): lax.all_to_all(rows, 'vol', split_axis=0, concat_axis=0, tiled=True)  3.45 us
    all_to_all x1, waiting for transfers between devices, local(): lax.all_to_all(meta, 'vol', split_axis=0, concat_axis=0, tiled=True)  3.02 us
    ppermute x1, waiting for transfers between devices, local(): pair_sum = gradient + lax.ppermute(gradient, 'ptcl', on_chip)  1.88 us
    reduce_sum x1, other arithmetic, tap_matrix_t(): return jnp.sum(picked, axis=0, dtype=jnp.bfloat16)  1.66 us
  transfers between devices with their start and end apart: 5, of which 5 were waited for; matrix products, arithmetic and copies ran while one was open for 26% of the time, Pallas kernels for 0%

profile of v12, /device:TPU:0, one launch (start us, length us, event | category | flops | bytes accessed | tf_op | source)
XLA Modules:
  0.0 41.4 jit_solution(9858705309619971253)
XLA Ops:
  0.7 1.5 %shard_map.91 = f32[8,19,96]{2,1,0:T(8,128)} custom-call(s32[8]{0:T(128)} %bitcast.59, s32[8,8,96]{2,1,0:T(8,128)} %bitcast.54, bf16[8,8,96]{2,1,0:T(8,128)(2,1)} %bitcast.56, s32[8,96]{1,0:T(8,128)} %bitcast.57, bf16[1,1]{1,0:T(2,128)(2,1)} %bitcast.47.focus_ref), custom_call_target="tpu_custom_call" | custom-call | tf_op jit(solution)/shard_map/pallas_call | solution.py:111
  2.2 7.3 %all-to-all-start = ((f32[8,19,96]{2,1,0:T(8,128)}), f32[8,19,96]{2,1,0:T(8,128)S(1)}, u32[]{:S(2)}, u32[]{:S(2)}) async-start(f32[8,19,96]{2,1,0:T(8,128)} %shard_map.91), calls=%async_computation | async-start | bytes 196608 | tf_op jit(solution)/shard_map/all_to_all | solution.py:135
  9.5 0.8 %eq.42 = s32[768]{0:T(1024)S(1)} reshape(s32[1,1,8,96]{3,2,1,0:T(8,128)} %param.13) | data formatting | bytes 6144 | tf_op jit(solution)/shard_map/eq | solution.py:138
  10.2 1.2 %convolution_convert_fusion.2 = bf16[2,256,256]{1,2,0:T(8,128)(2,1)S(1)} fusion(bf16[2,256,256]{2,1,0:T(8,128)(2,1)} %constant.66.clone, bf16[1,256,256]{2,1,0:T(8,128)(2,1)S(1)} %copy-done), kind=kOutput, calls=%fused_computation.8 | convolution fusion | flops 67239936 | bytes 655360 | tf_op jit(solution)/shard_map/iyx,jkx->ijyk/dot_general | solution.py:39
  11.5 0.4 fusion.4
  11.9 0.5 %copy.15 = bf16[1,2,256,2,128]{4,1,3,2,0:T(2,128)(2,1)S(1)} copy(bf16[1,2,256,2,128]{2,1,4,3,0:T(2,128)(2,1)S(1)} %convert_element_type.99) | data formatting | bytes 524288 | tf_op jit(solution)/shard_map/convert_element_type | solution.py:49
  12.4 1.2 %fusion.3 = bf16[768,256]{1,0:T(8,128)(2,1)} fusion(s32[768]{0:T(1024)S(1)} %eq.42, bf16[64,8,2,128]{3,2,1,0:T(2,128)(2,1)S(1)} %bitcast.51), kind=kOutput, calls=%fused_computation.5 | convolution fusion | flops 201916416 | bytes 658432 | tf_op jit(solution)/shard_map/dot_general | solution.py:139
  13.6 3.0 %all-to-all-done = f32[8,19,96]{2,1,0:T(8,128)S(1)} async-done(((f32[8,19,96]{2,1,0:T(8,128)}), f32[8,19,96]{2,1,0:T(8,128)S(1)}, u32[]{:S(2)}, u32[]{:S(2)}) %all-to-all-start) | async-done | bytes 58400 | tf_op jit(solution)/shard_map/all_to_all | solution.py:135
  16.6 3.5 %all-to-all-start.1 = ((bf16[8,96,256]{2,1,0:T(8,128)(2,1)}), bf16[8,96,256]{2,1,0:T(8,128)(2,1)S(1)}, u32[]{:S(2)}, u32[]{:S(2)}) async-start(bf16[8,96,256]{2,1,0:T(8,128)(2,1)} %bitcast.18), calls=%async_computation.1 | async-start | bytes 786432 | tf_op jit(solution)/shard_map/all_to_all | solution.py:141
  20.1 3.6 %sine_negate_fusion = f32[8,96,128]{2,1,0:T(8,128)S(1)} fusion(f32[8,96]{1,0:T(8,128)S(1)} %fusion.21, s32[8,96]{1,0:T(8,128)S(1)} %fusion.17, f32[8,96]{1,0:T(8,128)S(1)} %bitcast.55), kind=kLoop, calls=%fused_computation.17 | loop fusion | flops 884736 | bytes 402432 | tf_op jit(solution)/shard_map/neg | solution.py:59
  23.8 0.1 eq.38
  23.9 0.1 broadcast_in_dim.33
  23.9 0.3 mul.78
  24.2 0.6 %mul.79 = f32[8,96,256]{2,1,0:T(8,128)S(1)} reshape(f32[8,96,2,128]{3,2,1,0:T(2,128)S(1)} %mul.78) | data formatting | bytes 1572864 | tf_op jit(solution)/shard_map/mul | solution.py:67
  24.9 1.7 %fusion.1 = bf16[512,768]{1,0:T(8,128)(2,1)S(1)} fusion(s32[8,768]{1,0:T(8,128)S(1)} %eq.38, bf16[8,768]{1,0:T(8,128)(2,1)S(1)} %broadcast_in_dim.33), kind=kLoop, calls=%fused_computation.2 | loop fusion | flops 9043968 | bytes 823296 | tf_op jit(solution)/shard_map/reduce_sum | solution.py:82
  26.5 0.4 %convolution_convert_fusion = bf16[768,256]{1,0:T(8,128)(2,1)S(1)} fusion(bf16[512,768]{1,0:T(8,128)(2,1)S(1)} %fusion.1, f32[512,256]{1,0:T(8,128)S(1)} %copy-done.1), kind=kOutput, calls=%fused_computation.6 | convolution fusion | flops 201654272 | bytes 1703936 | tf_op jit(solution)/shard_map/dot_general | solution.py:148
  27.0 3.7 %all-to-all-done.1 = bf16[8,96,256]{2,1,0:T(8,128)(2,1)S(1)} async-done(((bf16[8,96,256]{2,1,0:T(8,128)(2,1)}), bf16[8,96,256]{2,1,0:T(8,128)(2,1)S(1)}, u32[]{:S(2)}, u32[]{:S(2)}) %all-to-all-start.1) | async-done | bytes 393248 | tf_op jit(solution)/shard_map/all_to_all | solution.py:141
  30.7 0.2 fusion.8
  30.9 0.4 fusion.24
  31.4 1.9 %collective-permute-done = f32[512,256]{1,0:T(8,128)S(1)} collective-permute-done((f32[512,256]{1,0:T(8,128)S(1)}, f32[512,256]{1,0:T(8,128)S(1)}, u32[]{:S(2)}, u32[]{:S(2)}) %collective-permute-start) | collective-permute-done | bytes 524320 | tf_op jit(solution)/shard_map/ppermute | solution.py:161
  33.3 1.6 %collective-permute-start.1 = (bf16[256,256]{1,0:T(8,128)(2,1)S(1)}, bf16[256,256]{1,0:T(8,128)(2,1)S(1)}, u32[]{:S(2)}, u32[]{:S(2)}) collective-permute-start(bf16[256,256]{1,0:T(8,128)(2,1)S(1)} %fusion.12), channel_id=1, source_target_pairs={{0,2},{1,3},{2,0},{3,1},{4,6},{5,7},{6,4},{7,5},{8,10},{9,11},{10,... | collective-permute-start | bytes 393224 | tf_op jit(solution)/shard_map/ppermute | solution.py:165
  34.8 4.0 %collective-permute-done.1 = bf16[256,256]{1,0:T(8,128)(2,1)S(1)} collective-permute-done((bf16[256,256]{1,0:T(8,128)(2,1)S(1)}, bf16[256,256]{1,0:T(8,128)(2,1)S(1)}, u32[]{:S(2)}, u32[]{:S(2)}) %collective-permute-start.1) | collective-permute-done | bytes 131104 | tf_op jit(solution)/shard_map/ppermute | solution.py:165
  39.0 1.5 %collective-permute-done.2 = f32[256,256]{1,0:T(8,128)S(1)} collective-permute-done((f32[256,256]{1,0:T(8,128)S(1)}, f32[256,256]{1,0:T(8,128)S(1)}, u32[]{:S(2)}, u32[]{:S(2)}) %collective-permute-start.2) | collective-permute-done | bytes 262176 | tf_op jit(solution)/shard_map/ppermute | solution.py:167
  40.5 0.8 %maximum_select_fusion = f32[512,256]{1,0:T(8,128)} fusion(f32[256,256]{1,0:T(8,128)S(1)} %collective-permute-done.2, f32[256,256]{1,0:T(8,128)S(1)} %add_subtract_fusion, pred[]{:T(512)S(6)} %eq.37), kind=kLoop, calls=%fused_computation.16 | loop fusion | flops 393216 | bytes 1048577 | tf_op jit(solution)/shard_map/jit(_where)/select_n | solution.py:168
  (20 shorter events, 0.4 us)
Async XLA Ops:
  0.0 10.2 %copy-start = (bf16[1,256,256]{2,1,0:T(8,128)(2,1)S(1)}, bf16[1,256,256]{2,1,0:T(8,128)(2,1)}, u32[]{:S(2)}) copy-start(bf16[1,256,256]{2,1,0:T(8,128)(2,1)} %param.9) | copy-start | bytes 393220
  0.0 11.5 %copy-start.2 = (bf16[512,512]{1,0:T(8,128)(2,1)S(1)}, bf16[512,512]{1,0:T(8,128)(2,1)}, u32[]{:S(2)}) copy-start(bf16[512,512]{1,0:T(8,128)(2,1)} %constant.67.clone) | copy-start | bytes 1572868
  2.2 14.4 %all-to-all-start = ((f32[8,19,96]{2,1,0:T(8,128)}), f32[8,19,96]{2,1,0:T(8,128)S(1)}, u32[]{:S(2)}, u32[]{:S(2)}) async-start(f32[8,19,96]{2,1,0:T(8,128)} %shard_map.91), calls=%async_computation | async-start | bytes 196608 | tf_op jit(solution)/shard_map/all_to_all | solution.py:135
  16.6 14.1 %all-to-all-start.1 = ((bf16[8,96,256]{2,1,0:T(8,128)(2,1)}), bf16[8,96,256]{2,1,0:T(8,128)(2,1)S(1)}, u32[]{:S(2)}, u32[]{:S(2)}) async-start(bf16[8,96,256]{2,1,0:T(8,128)(2,1)} %bitcast.18), calls=%async_computation.1 | async-start | bytes 786432 | tf_op jit(solution)/shard_map/all_to_all | solution.py:141
  24.9 1.7 %copy-start.1 = (f32[512,256]{1,0:T(8,128)S(1)}, f32[512,256]{1,0:T(8,128)}, u32[]{:S(2)}) copy-start(f32[512,256]{1,0:T(8,128)} %param.11) | copy-start | bytes 1572868
  31.3 2.0 %collective-permute-start = (f32[512,256]{1,0:T(8,128)S(1)}, f32[512,256]{1,0:T(8,128)S(1)}, u32[]{:S(2)}, u32[]{:S(2)}) collective-permute-start(f32[512,256]{1,0:T(8,128)S(1)} %fusion.24), channel_id=1, source_target_pairs={{0,1},{1,0},{2,3},{3,2},{4,5},{5,4},{6,7},{7,6},{8,9},{9,8},{10,11... | collective-permute-start | bytes 1572872 | tf_op jit(solution)/shard_map/ppermute | solution.py:161
  33.3 5.6 %collective-permute-start.1 = (bf16[256,256]{1,0:T(8,128)(2,1)S(1)}, bf16[256,256]{1,0:T(8,128)(2,1)S(1)}, u32[]{:S(2)}, u32[]{:S(2)}) collective-permute-start(bf16[256,256]{1,0:T(8,128)(2,1)S(1)} %fusion.12), channel_id=1, source_target_pairs={{0,2},{1,3},{2,0},{3,1},{4,6},{5,7},{6,4},{7,5},{8,10},{9,11},{10,... | collective-permute-start | bytes 393224 | tf_op jit(solution)/shard_map/ppermute | solution.py:165
  38.9 1.6 %collective-permute-start.2 = (f32[256,256]{1,0:T(8,128)S(1)}, f32[256,256]{1,0:T(8,128)S(1)}, u32[]{:S(2)}, u32[]{:S(2)}) collective-permute-start(f32[256,256]{1,0:T(8,128)S(1)} %add_subtract_fusion), channel_id=1, source_target_pairs={{0,1},{1,0},{2,3},{3,2},{4,5},{5,4},{6,7},{7,6},{8,9},{9,8},{10,11... | collective-permute-start | bytes 786440 | tf_op jit(solution)/shard_map/ppermute | solution.py:167

commit v13 on v12

--- a/solution.py
+++ b/solution.py
@@ -132,12 +132,13 @@
     weights = slot_weights[0, 0]
     owners, taps, capacity = tap_ids.shape
     meta = slot_meta(slot_count, tap_ids, weights, pixel_ids, defocus)
-    got_meta = lax.all_to_all(meta, "vol", split_axis=0, concat_axis=0, tiled=True)
     observed = transform(images, first, second)
     flat_pixels = pixel_ids.reshape(-1)
     onehot = (flat_pixels[:, None] == jnp.arange(observed.shape[0], dtype=jnp.int32)[None, :])
     rows = jnp.dot(onehot.astype(jnp.bfloat16), observed, preferred_element_type=jnp.float32)
     rows = rows.astype(jnp.bfloat16).reshape(owners, capacity, width)
+    meta, rows = lax.optimization_barrier((meta, rows))
+    got_meta = lax.all_to_all(meta, "vol", split_axis=0, concat_axis=0, tiled=True)
     got_rows = lax.all_to_all(rows, "vol", split_axis=0, concat_axis=0, tiled=True)
     got_taps = got_meta[:, :taps].astype(jnp.int32)
     got_weights = got_meta[:, taps : 2 * taps].astype(jnp.bfloat16)

time: 41.8 us -> 45.8 us (1.096)
  blocking collectives: 0 us -> 14.4 us
  starting transfers between devices: 12.4 us -> 5.15 us
  waiting for transfers between devices: 14.2 us -> 11.1 us
    all_to_all x0 -> x1, blocking collectives: none -> 14.4 us  [local(): lax.all_to_all(meta, 'vol', split_axis=0, concat_axis=0, tiled=True)]
    all_to_all x1 -> x0, starting transfers between devices: 7.28 us -> none  [local(): lax.all_to_all(meta, 'vol', split_axis=0, concat_axis=0, tiled=True)]
    all_to_all x1 -> x0, waiting for transfers between devices: 3.02 us -> none  [local(): lax.all_to_all(meta, 'vol', split_axis=0, concat_axis=0, tiled=True)]
  transfers between devices with their start and end apart: 5 -> 4, of which waited for: 5 -> 4; matrix products, arithmetic and copies ran while one was open for 26% -> 15% of each run, Pallas kernels for 0% -> 0%
where the time goes in v13:
time: 45.8 us; the launch traced here: 45.4 us
  blocking collectives  14.4 us (31%)
  waiting for transfers between devices  11.1 us (24%)
  other arithmetic  6.37 us (14%)
  starting transfers between devices  5.15 us (11%)
  matrix products  3.53 us (8%)
  local copies, waits for them, and re-layouts  2.42 us (5%)
  Pallas kernels  1.48 us (3%)
  between operations  0.93 us (2%)
    all_to_all x1, blocking collectives, local(): lax.all_to_all(meta, 'vol', split_axis=0, concat_axis=0, tiled=True)  14.4 us
    ppermute x1, waiting for transfers between devices, local(): lax.ppermute(mine, 'ptcl', across).astype(jnp.float32)  4.05 us
    all_to_all x1, waiting for transfers between devices, local(): lax.all_to_all(rows, 'vol', split_axis=0, concat_axis=0, tiled=True)  3.66 us
    neg x1, other arithmetic, ctf_rows(): -jnp.sin(math.pi * focus.astype(jnp.float32)[..., None] * radius + phase_...  3.56 us
    all_to_all x1, starting transfers between devices, local(): lax.all_to_all(rows, 'vol', split_axis=0, concat_axis=0, tiled=True)  3.45 us
    ppermute x1, waiting for transfers between devices, local(): pair_sum = gradient + lax.ppermute(gradient, 'ptcl', on_chip)  1.88 us
    reduce_sum x1, other arithmetic, tap_matrix_t(): return jnp.sum(picked, axis=0, dtype=jnp.bfloat16)  1.66 us
    ppermute x1, starting transfers between devices, local(): lax.ppermute(mine, 'ptcl', across).astype(jnp.float32)  1.55 us
  transfers between devices with their start and end apart: 4, of which 4 were waited for; matrix products, arithmetic and copies ran while one was open for 15% of the time, Pallas kernels for 0%

profile of v13, /device:TPU:0, one launch (start us, length us, event | category | flops | bytes accessed | tf_op | source)
XLA Modules:
  0.0 45.4 jit_solution(15010561075591259754)
XLA Ops:
  0.7 0.8 %eq.38 = s32[768]{0:T(1024)S(1)} reshape(s32[1,1,8,96]{3,2,1,0:T(8,128)} %param.13) | data formatting | bytes 6144 | tf_op jit(solution)/shard_map/eq | solution.py:137
  1.5 1.2 %convolution_convert_fusion.2 = bf16[2,256,256]{1,2,0:T(8,128)(2,1)S(1)} fusion(bf16[2,256,256]{2,1,0:T(8,128)(2,1)} %constant.66.clone, bf16[1,256,256]{2,1,0:T(8,128)(2,1)S(1)} %copy-done), kind=kOutput, calls=%fused_computation.8 | convolution fusion | flops 67239936 | bytes 655360 | tf_op jit(solution)/shard_map/iyx,jkx->ijyk/dot_general | solution.py:39
  2.7 0.3 fusion.4
  3.1 0.5 %copy.13 = bf16[1,2,256,2,128]{4,1,3,2,0:T(2,128)(2,1)S(1)} copy(bf16[1,2,256,2,128]{2,1,4,3,0:T(2,128)(2,1)S(1)} %convert_element_type.90) | data formatting | bytes 524288 | tf_op jit(solution)/shard_map/convert_element_type | solution.py:49
  3.6 1.2 %fusion.3 = bf16[768,256]{1,0:T(8,128)(2,1)} fusion(s32[768]{0:T(1024)S(1)} %eq.38, bf16[64,8,2,128]{3,2,1,0:T(2,128)(2,1)S(1)} %bitcast.51), kind=kOutput, calls=%fused_computation.5 | convolution fusion | flops 201916416 | bytes 658432 | tf_op jit(solution)/shard_map/dot_general | solution.py:138
  4.8 1.5 %shard_map.91 = f32[8,19,96]{2,1,0:T(8,128)} custom-call(s32[8]{0:T(128)} %bitcast.59, s32[8,8,96]{2,1,0:T(8,128)} %bitcast.54, bf16[8,8,96]{2,1,0:T(8,128)(2,1)} %bitcast.56, s32[8,96]{1,0:T(8,128)} %bitcast.57, bf16[1,1]{1,0:T(2,128)(2,1)} %bitcast.47.focus_ref), custom_call_target="tpu_custom_call" | custom-call | tf_op jit(solution)/shard_map/pallas_call | solution.py:111
  6.3 14.4 %all_to_all.10 = f32[8,19,96]{2,1,0:T(8,128)S(1)} all-to-all(f32[8,19,96]{2,1,0:T(8,128)} %shard_map.91), channel_id=1, replica_groups=mesh['vol'=8,'ptcl'=4] {'vol'}, dimensions={0} | all-to-all | bytes 116736 | tf_op jit(solution)/shard_map/all_to_all | solution.py:141
  20.7 3.5 %all-to-all-start.1 = ((bf16[8,96,256]{2,1,0:T(8,128)(2,1)}), bf16[8,96,256]{2,1,0:T(8,128)(2,1)S(1)}, u32[]{:S(2)}, u32[]{:S(2)}) async-start(bf16[8,96,256]{2,1,0:T(8,128)(2,1)} %bitcast.13), calls=%async_computation.1 | async-start | bytes 786432 | tf_op jit(solution)/shard_map/all_to_all | solution.py:142
  24.2 3.6 %sine_negate_fusion = f32[8,96,128]{2,1,0:T(8,128)S(1)} fusion(f32[8,96]{1,0:T(8,128)S(1)} %fusion.21, s32[8,96]{1,0:T(8,128)S(1)} %fusion.17, f32[8,96]{1,0:T(8,128)S(1)} %bitcast.55), kind=kLoop, calls=%fused_computation.17 | loop fusion | flops 884736 | bytes 402432 | tf_op jit(solution)/shard_map/neg | solution.py:59
  27.9 0.1 eq.42
  28.0 0.1 broadcast_in_dim.33
  28.1 0.3 mul.78
  28.3 0.6 %mul.79 = f32[8,96,256]{2,1,0:T(8,128)S(1)} reshape(f32[8,96,2,128]{3,2,1,0:T(2,128)S(1)} %mul.78) | data formatting | bytes 1572864 | tf_op jit(solution)/shard_map/mul | solution.py:67
  29.0 1.7 %fusion.1 = bf16[512,768]{1,0:T(8,128)(2,1)S(1)} fusion(s32[8,768]{1,0:T(8,128)S(1)} %eq.42, bf16[8,768]{1,0:T(8,128)(2,1)S(1)} %broadcast_in_dim.33), kind=kLoop, calls=%fused_computation.2 | loop fusion | flops 9043968 | bytes 823296 | tf_op jit(solution)/shard_map/reduce_sum | solution.py:82
  30.6 0.4 convolution_convert_fusion
  31.1 3.7 %all-to-all-done.1 = bf16[8,96,256]{2,1,0:T(8,128)(2,1)S(1)} async-done(((bf16[8,96,256]{2,1,0:T(8,128)(2,1)}), bf16[8,96,256]{2,1,0:T(8,128)(2,1)S(1)}, u32[]{:S(2)}, u32[]{:S(2)}) %all-to-all-start.1) | async-done | bytes 393248 | tf_op jit(solution)/shard_map/all_to_all | solution.py:142
  34.7 0.2 fusion.8
  34.9 0.4 fusion.24
  35.3 0.1 collective-permute-start
  35.4 1.9 %collective-permute-done = f32[512,256]{1,0:T(8,128)S(1)} collective-permute-done((f32[512,256]{1,0:T(8,128)S(1)}, f32[512,256]{1,0:T(8,128)S(1)}, u32[]{:S(2)}, u32[]{:S(2)}) %collective-permute-start) | collective-permute-done | bytes 524320 | tf_op jit(solution)/shard_map/ppermute | solution.py:162
  37.3 1.6 %collective-permute-start.1 = (bf16[256,256]{1,0:T(8,128)(2,1)S(1)}, bf16[256,256]{1,0:T(8,128)(2,1)S(1)}, u32[]{:S(2)}, u32[]{:S(2)}) collective-permute-start(bf16[256,256]{1,0:T(8,128)(2,1)S(1)} %fusion.12), channel_id=1, source_target_pairs={{0,2},{1,3},{2,0},{3,1},{4,6},{5,7},{6,4},{7,5},{8,10},{9,11},{10,... | collective-permute-start | bytes 393224 | tf_op jit(solution)/shard_map/ppermute | solution.py:166
  38.9 4.0 %collective-permute-done.1 = bf16[256,256]{1,0:T(8,128)(2,1)S(1)} collective-permute-done((bf16[256,256]{1,0:T(8,128)(2,1)S(1)}, bf16[256,256]{1,0:T(8,128)(2,1)S(1)}, u32[]{:S(2)}, u32[]{:S(2)}) %collective-permute-start.1) | collective-permute-done | bytes 131104 | tf_op jit(solution)/shard_map/ppermute | solution.py:166
  43.0 1.5 %collective-permute-done.2 = f32[256,256]{1,0:T(8,128)S(1)} collective-permute-done((f32[256,256]{1,0:T(8,128)S(1)}, f32[256,256]{1,0:T(8,128)S(1)}, u32[]{:S(2)}, u32[]{:S(2)}) %collective-permute-start.2) | collective-permute-done | bytes 262176 | tf_op jit(solution)/shard_map/ppermute | solution.py:168
  44.6 0.8 %maximum_select_fusion = f32[512,256]{1,0:T(8,128)} fusion(f32[256,256]{1,0:T(8,128)S(1)} %collective-permute-done.2, f32[256,256]{1,0:T(8,128)S(1)} %add_subtract_fusion, pred[]{:T(512)S(6)} %eq.37), kind=kLoop, calls=%fused_computation.16 | loop fusion | flops 393216 | bytes 1048577 | tf_op jit(solution)/shard_map/jit(_where)/select_n | solution.py:169
  (19 shorter events, 0.3 us)
Async XLA Ops:
  0.0 1.5 %copy-start = (bf16[1,256,256]{2,1,0:T(8,128)(2,1)S(1)}, bf16[1,256,256]{2,1,0:T(8,128)(2,1)}, u32[]{:S(2)}) copy-start(bf16[1,256,256]{2,1,0:T(8,128)(2,1)} %param.9) | copy-start | bytes 393220
  0.0 2.7 %copy-start.2 = (bf16[512,512]{1,0:T(8,128)(2,1)S(1)}, bf16[512,512]{1,0:T(8,128)(2,1)}, u32[]{:S(2)}) copy-start(bf16[512,512]{1,0:T(8,128)(2,1)} %constant.67.clone) | copy-start | bytes 1572868
  20.7 14.0 %all-to-all-start.1 = ((bf16[8,96,256]{2,1,0:T(8,128)(2,1)}), bf16[8,96,256]{2,1,0:T(8,128)(2,1)S(1)}, u32[]{:S(2)}, u32[]{:S(2)}) async-start(bf16[8,96,256]{2,1,0:T(8,128)(2,1)} %bitcast.13), calls=%async_computation.1 | async-start | bytes 786432 | tf_op jit(solution)/shard_map/all_to_all | solution.py:142
  29.0 1.7 %copy-start.1 = (f32[512,256]{1,0:T(8,128)S(1)}, f32[512,256]{1,0:T(8,128)}, u32[]{:S(2)}) copy-start(f32[512,256]{1,0:T(8,128)} %param.11) | copy-start | bytes 1572868
  35.3 2.0 %collective-permute-start = (f32[512,256]{1,0:T(8,128)S(1)}, f32[512,256]{1,0:T(8,128)S(1)}, u32[]{:S(2)}, u32[]{:S(2)}) collective-permute-start(f32[512,256]{1,0:T(8,128)S(1)} %fusion.24), channel_id=1, source_target_pairs={{0,1},{1,0},{2,3},{3,2},{4,5},{5,4},{6,7},{7,6},{8,9},{9,8},{10,11... | collective-permute-start | bytes 1572872 | tf_op jit(solution)/shard_map/ppermute | solution.py:162
  37.3 5.6 %collective-permute-start.1 = (bf16[256,256]{1,0:T(8,128)(2,1)S(1)}, bf16[256,256]{1,0:T(8,128)(2,1)S(1)}, u32[]{:S(2)}, u32[]{:S(2)}) collective-permute-start(bf16[256,256]{1,0:T(8,128)(2,1)S(1)} %fusion.12), channel_id=1, source_target_pairs={{0,2},{1,3},{2,0},{3,1},{4,6},{5,7},{6,4},{7,5},{8,10},{9,11},{10,... | collective-permute-start | bytes 393224 | tf_op jit(solution)/shard_map/ppermute | solution.py:166
  43.0 1.6 %collective-permute-start.2 = (f32[256,256]{1,0:T(8,128)S(1)}, f32[256,256]{1,0:T(8,128)S(1)}, u32[]{:S(2)}, u32[]{:S(2)}) collective-permute-start(f32[256,256]{1,0:T(8,128)S(1)} %add_subtract_fusion), channel_id=1, source_target_pairs={{0,1},{1,0},{2,3},{3,2},{4,5},{5,4},{6,7},{7,6},{8,9},{9,8},{10,11... | collective-permute-start | bytes 786440 | tf_op jit(solution)/shard_map/ppermute | solution.py:168

commit v14 on v12

--- a/solution.py
+++ b/solution.py
@@ -152,16 +152,25 @@
     ctf_values = ctf_rows(got_block, got_focus)
     weighted = residual_terms(prediction, got_rows, ctf_values, got_live)
     flat_residual = weighted.reshape(-1, width)
-    gradient = jnp.dot(matrix_t, flat_residual, preferred_element_type=jnp.float32)
     shards = lax.axis_size("ptcl")
     if shards == 4:
         me = lax.axis_index("ptcl")
         on_chip = [(i, i ^ 1) for i in range(shards)]
         across = [(i, i ^ 2) for i in range(shards)]
-        pair_sum = gradient + lax.ppermute(gradient, "ptcl", on_chip)
-        half = gradient.shape[0] // 2
+        half = matrix_t.shape[0] // 2
         core = me % 2
-        mine = lax.dynamic_slice_in_dim(pair_sum, core * half, half, axis=0).astype(jnp.bfloat16)
+        for_sibling = jnp.dot(
+            lax.dynamic_slice_in_dim(matrix_t, (1 - core) * half, half, axis=0),
+            flat_residual,
+            preferred_element_type=jnp.float32,
+        )
+        arrived = lax.ppermute(for_sibling, "ptcl", on_chip)
+        own = jnp.dot(
+            lax.dynamic_slice_in_dim(matrix_t, core * half, half, axis=0),
+            flat_residual,
+            preferred_element_type=jnp.float32,
+        )
+        mine = (own + arrived).astype(jnp.bfloat16)
         total = mine.astype(jnp.float32) + lax.ppermute(mine, "ptcl", across).astype(jnp.float32)
         updated = lax.dynamic_slice_in_dim(volume, core * half, half, axis=0) - learn_rate * total
         other = lax.ppermute(updated, "ptcl", on_chip)
@@ -170,6 +179,7 @@
             jnp.concatenate([updated, other], axis=0),
             jnp.concatenate([other, updated], axis=0),
         )
+    gradient = jnp.dot(matrix_t, flat_residual, preferred_element_type=jnp.float32)
     partial = gradient.astype(jnp.bfloat16)
     parts = partial.reshape(shards, -1, gradient.shape[1])
     got_parts = lax.all_to_all(parts, "ptcl", split_axis=0, concat_axis=0, tiled=True)

time: 41.8 us -> 41.5 us (level)
  no operation moved by 1% of the time
where the time goes in v14:
time: 41.5 us; the launch traced here: 41.1 us
  waiting for transfers between devices  13.8 us (33%)
  starting transfers between devices  12.4 us (30%)
  other arithmetic  6.34 us (15%)
  matrix products  3.7 us (9%)
  local copies, waits for them, and re-layouts  2.42 us (6%)
  Pallas kernels  1.47 us (4%)
  between operations  0.93 us (2%)
    all_to_all x1, starting transfers between devices, local(): lax.all_to_all(meta, 'vol', split_axis=0, concat_axis=0, tiled=True)  7.28 us
    ppermute x1, waiting for transfers between devices, local(): lax.ppermute(mine, 'ptcl', across).astype(jnp.float32)  4.05 us
    all_to_all x1, waiting for transfers between devices, local(): lax.all_to_all(rows, 'vol', split_axis=0, concat_axis=0, tiled=True)  3.75 us
    neg x1, other arithmetic, ctf_rows(): -jnp.sin(math.pi * focus.astype(jnp.float32)[..., None] * radius + phase_...  3.56 us
    all_to_all x1, starting transfers between devices, local(): lax.all_to_all(rows, 'vol', split_axis=0, concat_axis=0, tiled=True)  3.45 us
    all_to_all x1, waiting for transfers between devices, local(): lax.all_to_all(meta, 'vol', split_axis=0, concat_axis=0, tiled=True)  3.02 us
    reduce_sum x1, other arithmetic, tap_matrix_t(): return jnp.sum(picked, axis=0, dtype=jnp.bfloat16)  1.66 us
    ppermute x1, starting transfers between devices, local(): lax.ppermute(mine, 'ptcl', across).astype(jnp.float32)  1.55 us
  transfers between devices with their start and end apart: 5, of which 5 were waited for; matrix products, arithmetic and copies ran while one was open for 26% of the time, Pallas kernels for 0%

profile of v14, /device:TPU:0, one launch (start us, length us, event | category | flops | bytes accessed | tf_op | source)
XLA Modules:
  0.0 41.1 jit_solution(1074112078958347494)
XLA Ops:
  0.7 1.5 %shard_map.91 = f32[8,19,96]{2,1,0:T(8,128)} custom-call(s32[8]{0:T(128)} %bitcast.60, s32[8,8,96]{2,1,0:T(8,128)} %bitcast.55, bf16[8,8,96]{2,1,0:T(8,128)(2,1)} %bitcast.57, s32[8,96]{1,0:T(8,128)} %bitcast.58, bf16[1,1]{1,0:T(2,128)(2,1)} %bitcast.47.focus_ref), custom_call_target="tpu_custom_call" | custom-call | tf_op jit(solution)/shard_map/pallas_call | solution.py:111
  2.2 7.3 %all-to-all-start = ((f32[8,19,96]{2,1,0:T(8,128)}), f32[8,19,96]{2,1,0:T(8,128)S(1)}, u32[]{:S(2)}, u32[]{:S(2)}) async-start(f32[8,19,96]{2,1,0:T(8,128)} %shard_map.91), calls=%async_computation | async-start | bytes 196608 | tf_op jit(solution)/shard_map/all_to_all | solution.py:135
  9.5 0.8 %eq.42 = s32[768]{0:T(1024)S(1)} reshape(s32[1,1,8,96]{3,2,1,0:T(8,128)} %param.13) | data formatting | bytes 6144 | tf_op jit(solution)/shard_map/eq | solution.py:138
  10.2 1.2 %convolution_convert_fusion.2 = bf16[2,256,256]{1,2,0:T(8,128)(2,1)S(1)} fusion(bf16[2,256,256]{2,1,0:T(8,128)(2,1)} %constant.67.clone, bf16[1,256,256]{2,1,0:T(8,128)(2,1)S(1)} %copy-done), kind=kOutput, calls=%fused_computation.8 | convolution fusion | flops 67239936 | bytes 655360 | tf_op jit(solution)/shard_map/iyx,jkx->ijyk/dot_general | solution.py:39
  11.5 0.4 fusion.4
  11.9 0.5 %copy.15 = bf16[1,2,256,2,128]{4,1,3,2,0:T(2,128)(2,1)S(1)} copy(bf16[1,2,256,2,128]{2,1,4,3,0:T(2,128)(2,1)S(1)} %convert_element_type.99) | data formatting | bytes 524288 | tf_op jit(solution)/shard_map/convert_element_type | solution.py:49
  12.4 1.2 %fusion.3 = bf16[768,256]{1,0:T(8,128)(2,1)} fusion(s32[768]{0:T(1024)S(1)} %eq.42, bf16[64,8,2,128]{3,2,1,0:T(2,128)(2,1)S(1)} %bitcast.52), kind=kOutput, calls=%fused_computation.5 | convolution fusion | flops 201916416 | bytes 658432 | tf_op jit(solution)/shard_map/dot_general | solution.py:139
  13.6 3.0 %all-to-all-done = f32[8,19,96]{2,1,0:T(8,128)S(1)} async-done(((f32[8,19,96]{2,1,0:T(8,128)}), f32[8,19,96]{2,1,0:T(8,128)S(1)}, u32[]{:S(2)}, u32[]{:S(2)}) %all-to-all-start) | async-done | bytes 58400 | tf_op jit(solution)/shard_map/all_to_all | solution.py:135
  16.6 3.5 %all-to-all-start.1 = ((bf16[8,96,256]{2,1,0:T(8,128)(2,1)}), bf16[8,96,256]{2,1,0:T(8,128)(2,1)S(1)}, u32[]{:S(2)}, u32[]{:S(2)}) async-start(bf16[8,96,256]{2,1,0:T(8,128)(2,1)} %bitcast.18), calls=%async_computation.1 | async-start | bytes 786432 | tf_op jit(solution)/shard_map/all_to_all | solution.py:141
  20.1 3.6 %sine_negate_fusion = f32[8,96,128]{2,1,0:T(8,128)S(1)} fusion(f32[8,96]{1,0:T(8,128)S(1)} %fusion.24, s32[8,96]{1,0:T(8,128)S(1)} %fusion.20, f32[8,96]{1,0:T(8,128)S(1)} %bitcast.56), kind=kLoop, calls=%fused_computation.21 | loop fusion | flops 884736 | bytes 402432 | tf_op jit(solution)/shard_map/neg | solution.py:59
  23.9 0.1 broadcast_in_dim.33
  23.9 0.3 mul.81
  24.2 0.6 %mul.82 = f32[8,96,256]{2,1,0:T(8,128)S(1)} reshape(f32[8,96,2,128]{3,2,1,0:T(2,128)S(1)} %mul.81) | data formatting | bytes 1572864 | tf_op jit(solution)/shard_map/mul | solution.py:67
  24.9 1.7 %fusion.1 = bf16[512,768]{1,0:T(8,128)(2,1)S(1)} fusion(s32[8,768]{1,0:T(8,128)S(1)} %eq.38, bf16[8,768]{1,0:T(8,128)(2,1)S(1)} %broadcast_in_dim.33), kind=kLoop, calls=%fused_computation.2 | loop fusion | flops 9043968 | bytes 823296 | tf_op jit(solution)/shard_map/reduce_sum | solution.py:82
  26.5 0.4 %convolution_convert_fusion = bf16[768,256]{1,0:T(8,128)(2,1)S(1)} fusion(bf16[512,768]{1,0:T(8,128)(2,1)S(1)} %fusion.1, f32[512,256]{1,0:T(8,128)S(1)} %copy-done.1), kind=kOutput, calls=%fused_computation.6 | convolution fusion | flops 201654272 | bytes 1703936 | tf_op jit(solution)/shard_map/dot_general | solution.py:148
  27.0 3.7 %all-to-all-done.1 = bf16[8,96,256]{2,1,0:T(8,128)(2,1)S(1)} async-done(((bf16[8,96,256]{2,1,0:T(8,128)(2,1)}), bf16[8,96,256]{2,1,0:T(8,128)(2,1)S(1)}, u32[]{:S(2)}, u32[]{:S(2)}) %all-to-all-start.1) | async-done | bytes 393248 | tf_op jit(solution)/shard_map/all_to_all | solution.py:141
  30.7 0.2 fusion.9
  30.9 0.3 fusion.11
  31.3 1.5 %collective-permute-done = f32[256,256]{1,0:T(8,128)S(1)} collective-permute-done((f32[256,256]{1,0:T(8,128)S(1)}, f32[256,256]{1,0:T(8,128)S(1)}, u32[]{:S(2)}, u32[]{:S(2)}) %collective-permute-start) | collective-permute-done | bytes 262176 | tf_op jit(solution)/shard_map/ppermute | solution.py:167
  32.8 0.3 fusion.5
  33.1 1.6 %collective-permute-start.1 = (bf16[256,256]{1,0:T(8,128)(2,1)S(1)}, bf16[256,256]{1,0:T(8,128)(2,1)S(1)}, u32[]{:S(2)}, u32[]{:S(2)}) collective-permute-start(bf16[256,256]{1,0:T(8,128)(2,1)S(1)} %fusion.5), channel_id=1, source_target_pairs={{0,2},{1,3},{2,0},{3,1},{4,6},{5,7},{6,4},{7,5},{8,10},{9,11},{10,... | collective-permute-start | bytes 393224 | tf_op jit(solution)/shard_map/ppermute | solution.py:174
  34.6 4.0 %collective-permute-done.1 = bf16[256,256]{1,0:T(8,128)(2,1)S(1)} collective-permute-done((bf16[256,256]{1,0:T(8,128)(2,1)S(1)}, bf16[256,256]{1,0:T(8,128)(2,1)S(1)}, u32[]{:S(2)}, u32[]{:S(2)}) %collective-permute-start.1) | collective-permute-done | bytes 131104 | tf_op jit(solution)/shard_map/ppermute | solution.py:174
  38.8 1.5 %collective-permute-done.2 = f32[256,256]{1,0:T(8,128)S(1)} collective-permute-done((f32[256,256]{1,0:T(8,128)S(1)}, f32[256,256]{1,0:T(8,128)S(1)}, u32[]{:S(2)}, u32[]{:S(2)}) %collective-permute-start.2) | collective-permute-done | bytes 262176 | tf_op jit(solution)/shard_map/ppermute | solution.py:176
  40.3 0.8 %maximum_select_fusion = f32[512,256]{1,0:T(8,128)} fusion(f32[256,256]{1,0:T(8,128)S(1)} %collective-permute-done.2, f32[256,256]{1,0:T(8,128)S(1)} %add_subtract_fusion, pred[]{:T(512)S(6)} %eq.37), kind=kLoop, calls=%fused_computation.18 | loop fusion | flops 393216 | bytes 1048577 | tf_op jit(solution)/shard_map/jit(_where)/select_n | solution.py:177
  (20 shorter events, 0.4 us)
Async XLA Ops:
  0.0 10.2 %copy-start = (bf16[1,256,256]{2,1,0:T(8,128)(2,1)S(1)}, bf16[1,256,256]{2,1,0:T(8,128)(2,1)}, u32[]{:S(2)}) copy-start(bf16[1,256,256]{2,1,0:T(8,128)(2,1)} %param.9) | copy-start | bytes 393220
  0.0 11.5 %copy-start.2 = (bf16[512,512]{1,0:T(8,128)(2,1)S(1)}, bf16[512,512]{1,0:T(8,128)(2,1)}, u32[]{:S(2)}) copy-start(bf16[512,512]{1,0:T(8,128)(2,1)} %constant.68.clone) | copy-start | bytes 1572868
  2.2 14.4 %all-to-all-start = ((f32[8,19,96]{2,1,0:T(8,128)}), f32[8,19,96]{2,1,0:T(8,128)S(1)}, u32[]{:S(2)}, u32[]{:S(2)}) async-start(f32[8,19,96]{2,1,0:T(8,128)} %shard_map.91), calls=%async_computation | async-start | bytes 196608 | tf_op jit(solution)/shard_map/all_to_all | solution.py:135
  16.6 14.1 %all-to-all-start.1 = ((bf16[8,96,256]{2,1,0:T(8,128)(2,1)}), bf16[8,96,256]{2,1,0:T(8,128)(2,1)S(1)}, u32[]{:S(2)}, u32[]{:S(2)}) async-start(bf16[8,96,256]{2,1,0:T(8,128)(2,1)} %bitcast.18), calls=%async_computation.1 | async-start | bytes 786432 | tf_op jit(solution)/shard_map/all_to_all | solution.py:141
  24.9 1.7 %copy-start.1 = (f32[512,256]{1,0:T(8,128)S(1)}, f32[512,256]{1,0:T(8,128)}, u32[]{:S(2)}) copy-start(f32[512,256]{1,0:T(8,128)} %param.11) | copy-start | bytes 1572868
  31.2 1.6 %collective-permute-start = (f32[256,256]{1,0:T(8,128)S(1)}, f32[256,256]{1,0:T(8,128)S(1)}, u32[]{:S(2)}, u32[]{:S(2)}) collective-permute-start(f32[256,256]{1,0:T(8,128)S(1)} %fusion.11), channel_id=1, source_target_pairs={{0,1},{1,0},{2,3},{3,2},{4,5},{5,4},{6,7},{7,6},{8,9},{9,8},{10,11... | collective-permute-start | bytes 786440 | tf_op jit(solution)/shard_map/ppermute | solution.py:167
  33.1 5.6 %collective-permute-start.1 = (bf16[256,256]{1,0:T(8,128)(2,1)S(1)}, bf16[256,256]{1,0:T(8,128)(2,1)S(1)}, u32[]{:S(2)}, u32[]{:S(2)}) collective-permute-start(bf16[256,256]{1,0:T(8,128)(2,1)S(1)} %fusion.5), channel_id=1, source_target_pairs={{0,2},{1,3},{2,0},{3,1},{4,6},{5,7},{6,4},{7,5},{8,10},{9,11},{10,... | collective-permute-start | bytes 393224 | tf_op jit(solution)/shard_map/ppermute | solution.py:174
  38.7 1.6 %collective-permute-start.2 = (f32[256,256]{1,0:T(8,128)S(1)}, f32[256,256]{1,0:T(8,128)S(1)}, u32[]{:S(2)}, u32[]{:S(2)}) collective-permute-start(f32[256,256]{1,0:T(8,128)S(1)} %add_subtract_fusion), channel_id=1, source_target_pairs={{0,1},{1,0},{2,3},{3,2},{4,5},{5,4},{6,7},{7,6},{8,9},{9,8},{10,11... | collective-permute-start | bytes 786440 | tf_op jit(solution)/shard_map/ppermute | solution.py:176

commit v15 on v14

--- a/solution.py
+++ b/solution.py
@@ -131,7 +131,10 @@
     tap_ids = slot_taps[0, 0]
     weights = slot_weights[0, 0]
     owners, taps, capacity = tap_ids.shape
+    warm = lax.ppermute(slot_count[:1].astype(jnp.float32), "vol",
+                        [(i, (i + 1) % lax.axis_size("vol")) for i in range(lax.axis_size("vol"))])
     meta = slot_meta(slot_count, tap_ids, weights, pixel_ids, defocus)
+    meta, warm = lax.optimization_barrier((meta, warm))
     got_meta = lax.all_to_all(meta, "vol", split_axis=0, concat_axis=0, tiled=True)
     observed = transform(images, first, second)
     flat_pixels = pixel_ids.reshape(-1)
@@ -174,7 +177,8 @@
         total = mine.astype(jnp.float32) + lax.ppermute(mine, "ptcl", across).astype(jnp.float32)
         updated = lax.dynamic_slice_in_dim(volume, core * half, half, axis=0) - learn_rate * total
         other = lax.ppermute(updated, "ptcl", on_chip)
-        return jnp.where(
+        zero = warm[0] * 0.0
+        return zero + jnp.where(
             core == 0,
             jnp.concatenate([updated, other], axis=0),
             jnp.concatenate([other, updated], axis=0),

time: 41.5 us -> 46.1 us (1.11)
  starting transfers between devices: 12.4 us -> 14.3 us
  waiting for transfers between devices: 13.8 us -> 15.2 us
  between operations: 0.93 us -> 2.2 us
    ppermute x0 -> x1, starting transfers between devices: none -> 4.32 us  [local(): lax.ppermute(slot_count[:1].astype(jnp.float32), 'vol', [(i, (i + 1) % la...]
    all_to_all x1, waiting for transfers between devices: 3.02 us -> 5.94 us  [local(): lax.all_to_all(meta, 'vol', split_axis=0, concat_axis=0, tiled=True)]
    all_to_all x1, starting transfers between devices: 7.28 us -> 4.88 us  [local(): lax.all_to_all(meta, 'vol', split_axis=0, concat_axis=0, tiled=True)]
    all_to_all x1, waiting for transfers between devices: 3.75 us -> 2.8 us  [local(): lax.all_to_all(rows, 'vol', split_axis=0, concat_axis=0, tiled=True)]
    add x0 -> x1, other arithmetic: none -> 0.84 us  [local(): zero + jnp.where(core == 0, jnp.concatenate([updated, other], axis=0), jn...]
    select_n x1 -> x0, other arithmetic: 0.84 us -> none  [local(): jnp.where(core == 0, jnp.concatenate([updated, other], axis=0), jnp.conca...]
    ppermute x1, waiting for transfers between devices: 1.52 us -> 0.9 us  [local(): other = lax.ppermute(updated, 'ptcl', on_chip)]
  transfers between devices with their start and end apart: 5 -> 6, of which waited for: 5 -> 5; matrix products, arithmetic and copies ran while one was open for 26% -> 24% of each run, Pallas kernels for 0% -> 3%
where the time goes in v15:
time: 46.1 us; the launch traced here: 45.7 us
  waiting for transfers between devices  15.2 us (33%)
  starting transfers between devices  14.3 us (31%)
  other arithmetic  6.34 us (14%)
  matrix products  3.69 us (8%)
  local copies, waits for them, and re-layouts  2.42 us (5%)
  between operations  2.2 us (5%)
  Pallas kernels  1.48 us (3%)
    all_to_all x1, waiting for transfers between devices, local(): lax.all_to_all(meta, 'vol', split_axis=0, concat_axis=0, tiled=True)  5.94 us
    all_to_all x1, starting transfers between devices, local(): lax.all_to_all(meta, 'vol', split_axis=0, concat_axis=0, tiled=True)  4.88 us
    ppermute x1, starting transfers between devices, local(): lax.ppermute(slot_count[:1].astype(jnp.float32), 'vol', [(i, (i + 1) % la...  4.32 us
    ppermute x1, waiting for transfers between devices, local(): lax.ppermute(mine, 'ptcl', across).astype(jnp.float32)  4.05 us
    neg x1, other arithmetic, ctf_rows(): -jnp.sin(math.pi * focus.astype(jnp.float32)[..., None] * radius + phase_...  3.56 us
    all_to_all x1, starting transfers between devices, local(): lax.all_to_all(rows, 'vol', split_axis=0, concat_axis=0, tiled=True)  3.45 us
    all_to_all x1, waiting for transfers between devices, local(): lax.all_to_all(rows, 'vol', split_axis=0, concat_axis=0, tiled=True)  2.8 us
    reduce_sum x1, other arithmetic, tap_matrix_t(): return jnp.sum(picked, axis=0, dtype=jnp.bfloat16)  1.66 us
  transfers between devices with their start and end apart: 6, of which 5 were waited for; matrix products, arithmetic and copies ran while one was open for 24% of the time, Pallas kernels for 3%

profile of v15, /device:TPU:0, one launch (start us, length us, event | category | flops | bytes accessed | tf_op | source)
XLA Modules:
  0.0 45.7 jit_solution(14821475951088482822)
XLA Ops:
  0.7 4.3 %collective-permute-start = (f32[1]{0:T(128)}, f32[1]{0:T(128)}, u32[]{:S(2)}, u32[]{:S(2)}) collective-permute-start(f32[1]{0:T(128)} %bitcast.5), channel_id=1, source_target_pairs={{0,4},{4,8},{8,12},{12,16},{16,20},{20,24},{24,28},{28,0},{1,5},{5... | collective-permute-start | bytes 20 | tf_op jit(solution)/shard_map/ppermute | solution.py:134
  5.7 0.8 %eq.42 = s32[768]{0:T(1024)S(1)} reshape(s32[1,1,8,96]{3,2,1,0:T(8,128)} %param.13) | data formatting | bytes 6144 | tf_op jit(solution)/shard_map/eq | solution.py:141
  6.5 1.2 %convolution_convert_fusion.2 = bf16[2,256,256]{1,2,0:T(8,128)(2,1)S(1)} fusion(bf16[2,256,256]{2,1,0:T(8,128)(2,1)} %constant.69.clone, bf16[1,256,256]{2,1,0:T(8,128)(2,1)S(1)} %copy-done), kind=kOutput, calls=%fused_computation.8 | convolution fusion | flops 67239936 | bytes 655360 | tf_op jit(solution)/shard_map/iyx,jkx->ijyk/dot_general | solution.py:39
  7.7 0.3 fusion.4
  8.1 0.5 %copy.15 = bf16[1,2,256,2,128]{4,1,3,2,0:T(2,128)(2,1)S(1)} copy(bf16[1,2,256,2,128]{2,1,4,3,0:T(2,128)(2,1)S(1)} %convert_element_type.107) | data formatting | bytes 524288 | tf_op jit(solution)/shard_map/convert_element_type | solution.py:49
  8.6 1.5 %shard_map.91 = f32[8,19,96]{2,1,0:T(8,128)} custom-call(s32[8]{0:T(128)} %bitcast.64, s32[8,8,96]{2,1,0:T(8,128)} %bitcast.58, bf16[8,8,96]{2,1,0:T(8,128)(2,1)} %bitcast.60, s32[8,96]{1,0:T(8,128)} %bitcast.61, bf16[1,1]{1,0:T(2,128)(2,1)} %bitcast.50.focus_ref), custom_call_target="tpu_custom_call" | custom-call | tf_op jit(solution)/shard_map/pallas_call | solution.py:111
  10.1 4.9 %all-to-all-start = ((f32[8,19,96]{2,1,0:T(8,128)}), f32[8,19,96]{2,1,0:T(8,128)S(1)}, u32[]{:S(2)}, u32[]{:S(2)}) async-start(f32[8,19,96]{2,1,0:T(8,128)} %shard_map.91), calls=%async_computation | async-start | bytes 196608 | tf_op jit(solution)/shard_map/all_to_all | solution.py:138
  15.0 1.2 %fusion.3 = bf16[768,256]{1,0:T(8,128)(2,1)} fusion(s32[768]{0:T(1024)S(1)} %eq.42, bf16[64,8,2,128]{3,2,1,0:T(2,128)(2,1)S(1)} %bitcast.55), kind=kOutput, calls=%fused_computation.5 | convolution fusion | flops 201916416 | bytes 658432 | tf_op jit(solution)/shard_map/dot_general | solution.py:142
  16.2 5.9 %all-to-all-done = f32[8,19,96]{2,1,0:T(8,128)S(1)} async-done(((f32[8,19,96]{2,1,0:T(8,128)}), f32[8,19,96]{2,1,0:T(8,128)S(1)}, u32[]{:S(2)}, u32[]{:S(2)}) %all-to-all-start) | async-done | bytes 58400 | tf_op jit(solution)/shard_map/all_to_all | solution.py:138
  22.1 3.5 %all-to-all-start.1 = ((bf16[8,96,256]{2,1,0:T(8,128)(2,1)}), bf16[8,96,256]{2,1,0:T(8,128)(2,1)S(1)}, u32[]{:S(2)}, u32[]{:S(2)}) async-start(bf16[8,96,256]{2,1,0:T(8,128)(2,1)} %bitcast.20), calls=%async_computation.1 | async-start | bytes 786432 | tf_op jit(solution)/shard_map/all_to_all | solution.py:144
  25.6 3.6 %sine_negate_fusion = f32[8,96,128]{2,1,0:T(8,128)S(1)} fusion(f32[8,96]{1,0:T(8,128)S(1)} %fusion.25, s32[8,96]{1,0:T(8,128)S(1)} %fusion.21, f32[8,96]{1,0:T(8,128)S(1)} %bitcast.59), kind=kLoop, calls=%fused_computation.22 | loop fusion | flops 884736 | bytes 402432 | tf_op jit(solution)/shard_map/neg | solution.py:59
  29.4 0.3 mul.89
  29.7 0.6 %mul.90 = f32[8,96,256]{2,1,0:T(8,128)S(1)} reshape(f32[8,96,2,128]{3,2,1,0:T(2,128)S(1)} %mul.89) | data formatting | bytes 1572864 | tf_op jit(solution)/shard_map/mul | solution.py:67
  30.4 1.7 %fusion.1 = bf16[512,768]{1,0:T(8,128)(2,1)S(1)} fusion(s32[8,768]{1,0:T(8,128)S(1)} %eq.38, bf16[8,768]{1,0:T(8,128)(2,1)S(1)} %broadcast_in_dim.33), kind=kLoop, calls=%fused_computation.2 | loop fusion | flops 9043968 | bytes 823296 | tf_op jit(solution)/shard_map/reduce_sum | solution.py:82
  32.0 0.4 convolution_convert_fusion
  32.5 2.8 %all-to-all-done.1 = bf16[8,96,256]{2,1,0:T(8,128)(2,1)S(1)} async-done(((bf16[8,96,256]{2,1,0:T(8,128)(2,1)}), bf16[8,96,256]{2,1,0:T(8,128)(2,1)S(1)}, u32[]{:S(2)}, u32[]{:S(2)}) %all-to-all-start.1) | async-done | bytes 393248 | tf_op jit(solution)/shard_map/all_to_all | solution.py:144
  35.3 0.2 fusion.9
  35.4 0.3 fusion.12
  35.8 1.5 %collective-permute-done.1 = f32[256,256]{1,0:T(8,128)S(1)} collective-permute-done((f32[256,256]{1,0:T(8,128)S(1)}, f32[256,256]{1,0:T(8,128)S(1)}, u32[]{:S(2)}, u32[]{:S(2)}) %collective-permute-start.1) | collective-permute-done | bytes 262176 | tf_op jit(solution)/shard_map/ppermute | solution.py:170
  37.3 0.3 fusion.5
  37.6 1.6 %collective-permute-start.2 = (bf16[256,256]{1,0:T(8,128)(2,1)S(1)}, bf16[256,256]{1,0:T(8,128)(2,1)S(1)}, u32[]{:S(2)}, u32[]{:S(2)}) collective-permute-start(bf16[256,256]{1,0:T(8,128)(2,1)S(1)} %fusion.5), channel_id=1, source_target_pairs={{0,2},{1,3},{2,0},{3,1},{4,6},{5,7},{6,4},{7,5},{8,10},{9,11},{10,... | collective-permute-start | bytes 393224 | tf_op jit(solution)/shard_map/ppermute | solution.py:177
  39.2 4.0 %collective-permute-done.2 = bf16[256,256]{1,0:T(8,128)(2,1)S(1)} collective-permute-done((bf16[256,256]{1,0:T(8,128)(2,1)S(1)}, bf16[256,256]{1,0:T(8,128)(2,1)S(1)}, u32[]{:S(2)}, u32[]{:S(2)}) %collective-permute-start.2) | collective-permute-done | bytes 131104 | tf_op jit(solution)/shard_map/ppermute | solution.py:177
  44.0 0.9 %collective-permute-done.3 = f32[256,256]{1,0:T(8,128)S(1)} collective-permute-done((f32[256,256]{1,0:T(8,128)S(1)}, f32[256,256]{1,0:T(8,128)S(1)}, u32[]{:S(2)}, u32[]{:S(2)}) %collective-permute-start.3) | collective-permute-done | bytes 262176 | tf_op jit(solution)/shard_map/ppermute | solution.py:179
  44.8 0.8 %fusion.11 = f32[512,256]{1,0:T(8,128)} fusion(f32[256,256]{1,0:T(8,128)S(1)} %collective-permute-done.3, f32[256,256]{1,0:T(8,128)S(1)} %add_subtract_fusion, f32[]{:T(128)} %bitcast.6, pred[]{:T(512)S(6)} %eq.37), kind=kLoop, calls=%fused_computation.19 | loop fusion | flops 524288 | bytes 1048581 | tf_op jit(solution)/shard_map/add | solution.py:181
  (22 shorter events, 0.5 us)
Async XLA Ops:
  0.0 6.5 %copy-start = (bf16[1,256,256]{2,1,0:T(8,128)(2,1)S(1)}, bf16[1,256,256]{2,1,0:T(8,128)(2,1)}, u32[]{:S(2)}) copy-start(bf16[1,256,256]{2,1,0:T(8,128)(2,1)} %param.9) | copy-start | bytes 393220
  0.0 7.7 %copy-start.2 = (bf16[512,512]{1,0:T(8,128)(2,1)S(1)}, bf16[512,512]{1,0:T(8,128)(2,1)}, u32[]{:S(2)}) copy-start(bf16[512,512]{1,0:T(8,128)(2,1)} %constant.70.clone) | copy-start | bytes 1572868
  0.7 9.4 %collective-permute-start = (f32[1]{0:T(128)}, f32[1]{0:T(128)}, u32[]{:S(2)}, u32[]{:S(2)}) collective-permute-start(f32[1]{0:T(128)} %bitcast.5), channel_id=1, source_target_pairs={{0,4},{4,8},{8,12},{12,16},{16,20},{20,24},{24,28},{28,0},{1,5},{5... | collective-permute-start | bytes 20 | tf_op jit(solution)/shard_map/ppermute | solution.py:134
  10.1 12.0 %all-to-all-start = ((f32[8,19,96]{2,1,0:T(8,128)}), f32[8,19,96]{2,1,0:T(8,128)S(1)}, u32[]{:S(2)}, u32[]{:S(2)}) async-start(f32[8,19,96]{2,1,0:T(8,128)} %shard_map.91), calls=%async_computation | async-start | bytes 196608 | tf_op jit(solution)/shard_map/all_to_all | solution.py:138
  22.1 13.2 %all-to-all-start.1 = ((bf16[8,96,256]{2,1,0:T(8,128)(2,1)}), bf16[8,96,256]{2,1,0:T(8,128)(2,1)S(1)}, u32[]{:S(2)}, u32[]{:S(2)}) async-start(bf16[8,96,256]{2,1,0:T(8,128)(2,1)} %bitcast.20), calls=%async_computation.1 | async-start | bytes 786432 | tf_op jit(solution)/shard_map/all_to_all | solution.py:144
  30.3 1.7 %copy-start.1 = (f32[512,256]{1,0:T(8,128)S(1)}, f32[512,256]{1,0:T(8,128)}, u32[]{:S(2)}) copy-start(f32[512,256]{1,0:T(8,128)} %param.11) | copy-start | bytes 1572868
  35.7 1.6 %collective-permute-start.1 = (f32[256,256]{1,0:T(8,128)S(1)}, f32[256,256]{1,0:T(8,128)S(1)}, u32[]{:S(2)}, u32[]{:S(2)}) collective-permute-start(f32[256,256]{1,0:T(8,128)S(1)} %fusion.12), channel_id=1, source_target_pairs={{0,1},{1,0},{2,3},{3,2},{4,5},{5,4},{6,7},{7,6},{8,9},{9,8},{10,11... | collective-permute-start | bytes 786440 | tf_op jit(solution)/shard_map/ppermute | solution.py:170
  37.6 5.6 %collective-permute-start.2 = (bf16[256,256]{1,0:T(8,128)(2,1)S(1)}, bf16[256,256]{1,0:T(8,128)(2,1)S(1)}, u32[]{:S(2)}, u32[]{:S(2)}) collective-permute-start(bf16[256,256]{1,0:T(8,128)(2,1)S(1)} %fusion.5), channel_id=1, source_target_pairs={{0,2},{1,3},{2,0},{3,1},{4,6},{5,7},{6,4},{7,5},{8,10},{9,11},{10,... | collective-permute-start | bytes 393224 | tf_op jit(solution)/shard_map/ppermute | solution.py:177
  43.2 1.6 %collective-permute-start.3 = (f32[256,256]{1,0:T(8,128)S(1)}, f32[256,256]{1,0:T(8,128)S(1)}, u32[]{:S(2)}, u32[]{:S(2)}) collective-permute-start(f32[256,256]{1,0:T(8,128)S(1)} %add_subtract_fusion), channel_id=1, source_target_pairs={{0,1},{1,0},{2,3},{3,2},{4,5},{5,4},{6,7},{7,6},{8,9},{9,8},{10,11... | collective-permute-start | bytes 786440 | tf_op jit(solution)/shard_map/ppermute | solution.py:179

commit v16 on v14

--- a/solution.py
+++ b/solution.py
@@ -174,11 +174,8 @@
         total = mine.astype(jnp.float32) + lax.ppermute(mine, "ptcl", across).astype(jnp.float32)
         updated = lax.dynamic_slice_in_dim(volume, core * half, half, axis=0) - learn_rate * total
         other = lax.ppermute(updated, "ptcl", on_chip)
-        return jnp.where(
-            core == 0,
-            jnp.concatenate([updated, other], axis=0),
-            jnp.concatenate([other, updated], axis=0),
-        )
+        result = lax.dynamic_update_slice_in_dim(volume, updated, core * half, axis=0)
+        return lax.dynamic_update_slice_in_dim(result, other, (1 - core) * half, axis=0)
     gradient = jnp.dot(matrix_t, flat_residual, preferred_element_type=jnp.float32)
     partial = gradient.astype(jnp.bfloat16)
     parts = partial.reshape(shards, -1, gradient.shape[1])

time: 41.5 us -> 42.4 us (1.022)
  waiting for transfers between devices: 13.8 us -> 15.4 us
  local copies, waits for them, and re-layouts: 2.42 us -> 3.6 us
  matrix products: 3.7 us -> 2.75 us
  other arithmetic: 6.34 us -> 5.52 us
    all_to_all x1, waiting for transfers between devices: 3.02 us -> 4.65 us  [local(): lax.all_to_all(meta, 'vol', split_axis=0, concat_axis=0, tiled=True)]
    unnamed x7 -> x12, local copies, waits for them, and re-layouts: 0.02 us -> 1.16 us
    dot_general x1, matrix products: 1.21 us -> 0.26 us  [transform(): jnp.einsum('iyx,jkx->ijyk', pictures, jnp.asarray(first), preferred_eleme...]
    select_n x1 -> x0, other arithmetic: 0.84 us -> none  [local(): jnp.where(core == 0, jnp.concatenate([updated, other], axis=0), jnp.conca...]
    dynamic_update_slice x0 -> x1, local copies, waits for them, and re-layouts: none -> 0.72 us  [local(): lax.dynamic_update_slice_in_dim(result, other, (1 - core) * half, axis=0)]
    eq x1, local copies, waits for them, and re-layouts: 0.76 us -> 0.07 us  [local(): flat_pixels[:, None]]
  transfers between devices with their start and end apart: 5 -> 5, of which waited for: 5 -> 5; matrix products, arithmetic and copies ran while one was open for 26% -> 22% of each run, Pallas kernels for 0% -> 0%
where the time goes in v16:
time: 42.4 us; the launch traced here: 42.1 us
  waiting for transfers between devices  15.4 us (36%)
  starting transfers between devices  12.4 us (29%)
  other arithmetic  5.52 us (13%)
  local copies, waits for them, and re-layouts  3.6 us (8%)
  matrix products  2.75 us (6%)
  Pallas kernels  1.48 us (3%)
  between operations  0.86 us (2%)
    all_to_all x1, starting transfers between devices, local(): lax.all_to_all(meta, 'vol', split_axis=0, concat_axis=0, tiled=True)  7.29 us
    all_to_all x1, waiting for transfers between devices, local(): lax.all_to_all(meta, 'vol', split_axis=0, concat_axis=0, tiled=True)  4.65 us
    ppermute x1, waiting for transfers between devices, local(): lax.ppermute(mine, 'ptcl', across).astype(jnp.float32)  4.05 us
    all_to_all x1, waiting for transfers between devices, local(): lax.all_to_all(rows, 'vol', split_axis=0, concat_axis=0, tiled=True)  3.69 us
    neg x1, other arithmetic, ctf_rows(): -jnp.sin(math.pi * focus.astype(jnp.float32)[..., None] * radius + phase_...  3.56 us
    all_to_all x1, starting transfers between devices, local(): lax.all_to_all(rows, 'vol', split_axis=0, concat_axis=0, tiled=True)  3.45 us
    reduce_sum x1, other arithmetic, tap_matrix_t(): return jnp.sum(picked, axis=0, dtype=jnp.bfloat16)  1.66 us
    ppermute x1, starting transfers between devices, local(): lax.ppermute(mine, 'ptcl', across).astype(jnp.float32)  1.56 us
  transfers between devices with their start and end apart: 5, of which 5 were waited for; matrix products, arithmetic and copies ran while one was open for 22% of the time, Pallas kernels for 0%

profile of v16, /device:TPU:0, one launch (start us, length us, event | category | flops | bytes accessed | tf_op | source)
XLA Modules:
  0.0 42.1 jit_solution(7062486314021984344)
XLA Ops:
  0.0 1.1 %copy.28 = f32[512,256]{1,0:T(8,128)S(1)} copy(f32[512,256]{1,0:T(8,128)} %param.11) | data formatting | bytes 1048576
  1.8 1.5 %shard_map.91 = f32[8,19,96]{2,1,0:T(8,128)} custom-call(s32[8]{0:T(128)} %bitcast.60, s32[8,8,96]{2,1,0:T(8,128)} %bitcast.55, bf16[8,8,96]{2,1,0:T(8,128)(2,1)} %bitcast.57, s32[8,96]{1,0:T(8,128)} %bitcast.58, bf16[1,1]{1,0:T(2,128)(2,1)} %bitcast.47.focus_ref), custom_call_target="tpu_custom_call" | custom-call | tf_op jit(solution)/shard_map/pallas_call | solution.py:111
  3.3 7.3 %all-to-all-start = ((f32[8,19,96]{2,1,0:T(8,128)}), f32[8,19,96]{2,1,0:T(8,128)S(1)}, u32[]{:S(2)}, u32[]{:S(2)}) async-start(f32[8,19,96]{2,1,0:T(8,128)} %shard_map.91), calls=%async_computation | async-start | bytes 196608 | tf_op jit(solution)/shard_map/all_to_all | solution.py:135
  10.7 0.3 convolution_convert_fusion.2
  10.9 0.4 fusion.4
  11.4 0.5 %copy.15 = bf16[1,2,256,2,128]{4,1,3,2,0:T(2,128)(2,1)S(1)} copy(bf16[1,2,256,2,128]{2,1,4,3,0:T(2,128)(2,1)S(1)} %convert_element_type.99) | data formatting | bytes 524288 | tf_op jit(solution)/shard_map/convert_element_type | solution.py:49
  11.9 1.2 %fusion.3 = bf16[768,256]{1,0:T(8,128)(2,1)} fusion(s32[768]{0:T(1024)S(1)} %eq.38, bf16[64,8,2,128]{3,2,1,0:T(2,128)(2,1)S(1)} %bitcast.52), kind=kOutput, calls=%fused_computation.5 | convolution fusion | flops 201916416 | bytes 658432 | tf_op jit(solution)/shard_map/dot_general | solution.py:139
  13.0 4.6 %all-to-all-done = f32[8,19,96]{2,1,0:T(8,128)S(1)} async-done(((f32[8,19,96]{2,1,0:T(8,128)}), f32[8,19,96]{2,1,0:T(8,128)S(1)}, u32[]{:S(2)}, u32[]{:S(2)}) %all-to-all-start) | async-done | bytes 58400 | tf_op jit(solution)/shard_map/all_to_all | solution.py:135
  17.7 3.5 %all-to-all-start.1 = ((bf16[8,96,256]{2,1,0:T(8,128)(2,1)}), bf16[8,96,256]{2,1,0:T(8,128)(2,1)S(1)}, u32[]{:S(2)}, u32[]{:S(2)}) async-start(bf16[8,96,256]{2,1,0:T(8,128)(2,1)} %bitcast.18), calls=%async_computation.1 | async-start | bytes 786432 | tf_op jit(solution)/shard_map/all_to_all | solution.py:141
  21.2 3.6 %sine_negate_fusion = f32[8,96,128]{2,1,0:T(8,128)S(1)} fusion(f32[8,96]{1,0:T(8,128)S(1)} %fusion.24, s32[8,96]{1,0:T(8,128)S(1)} %fusion.20, f32[8,96]{1,0:T(8,128)S(1)} %bitcast.56), kind=kLoop, calls=%fused_computation.20 | loop fusion | flops 884736 | bytes 402432 | tf_op jit(solution)/shard_map/neg | solution.py:59
  24.9 0.1 broadcast_in_dim.33
  25.0 0.3 mul.83
  25.3 0.6 %mul.84 = f32[8,96,256]{2,1,0:T(8,128)S(1)} reshape(f32[8,96,2,128]{3,2,1,0:T(2,128)S(1)} %mul.83) | data formatting | bytes 1572864 | tf_op jit(solution)/shard_map/mul | solution.py:67
  25.9 1.7 %fusion.1 = bf16[512,768]{1,0:T(8,128)(2,1)S(1)} fusion(s32[8,768]{1,0:T(8,128)S(1)} %eq.34, bf16[8,768]{1,0:T(8,128)(2,1)S(1)} %broadcast_in_dim.33), kind=kLoop, calls=%fused_computation.2 | loop fusion | flops 9043968 | bytes 823296 | tf_op jit(solution)/shard_map/reduce_sum | solution.py:82
  27.6 0.4 convolution_convert_fusion
  28.0 3.7 %all-to-all-done.1 = bf16[8,96,256]{2,1,0:T(8,128)(2,1)S(1)} async-done(((bf16[8,96,256]{2,1,0:T(8,128)(2,1)}), bf16[8,96,256]{2,1,0:T(8,128)(2,1)S(1)}, u32[]{:S(2)}, u32[]{:S(2)}) %all-to-all-start.1) | async-done | bytes 393248 | tf_op jit(solution)/shard_map/all_to_all | solution.py:141
  31.7 0.2 fusion.9
  31.9 0.3 fusion.11
  32.3 1.5 %collective-permute-done = f32[256,256]{1,0:T(8,128)S(1)} collective-permute-done((f32[256,256]{1,0:T(8,128)S(1)}, f32[256,256]{1,0:T(8,128)S(1)}, u32[]{:S(2)}, u32[]{:S(2)}) %collective-permute-start) | collective-permute-done | bytes 262176 | tf_op jit(solution)/shard_map/ppermute | solution.py:167
  33.8 0.3 fusion.5
  34.1 1.6 %collective-permute-start.1 = (bf16[256,256]{1,0:T(8,128)(2,1)S(1)}, bf16[256,256]{1,0:T(8,128)(2,1)S(1)}, u32[]{:S(2)}, u32[]{:S(2)}) collective-permute-start(bf16[256,256]{1,0:T(8,128)(2,1)S(1)} %fusion.5), channel_id=1, source_target_pairs={{0,2},{1,3},{2,0},{3,1},{4,6},{5,7},{6,4},{7,5},{8,10},{9,11},{10,... | collective-permute-start | bytes 393224 | tf_op jit(solution)/shard_map/ppermute | solution.py:174
  35.6 4.0 %collective-permute-done.1 = bf16[256,256]{1,0:T(8,128)(2,1)S(1)} collective-permute-done((bf16[256,256]{1,0:T(8,128)(2,1)S(1)}, bf16[256,256]{1,0:T(8,128)(2,1)S(1)}, u32[]{:S(2)}, u32[]{:S(2)}) %collective-permute-start.1) | collective-permute-done | bytes 131104 | tf_op jit(solution)/shard_map/ppermute | solution.py:174
  39.8 1.5 %collective-permute-done.2 = f32[256,256]{1,0:T(8,128)S(1)} collective-permute-done((f32[256,256]{1,0:T(8,128)S(1)}, f32[256,256]{1,0:T(8,128)S(1)}, u32[]{:S(2)}, u32[]{:S(2)}) %collective-permute-start.2) | collective-permute-done | bytes 262176 | tf_op jit(solution)/shard_map/ppermute | solution.py:176
  41.3 0.7 %constant_dynamic-update-slice_fusion = f32[512,256]{1,0:T(8,128)} fusion(f32[512,256]{1,0:T(8,128)} %copy-done.1, f32[256,256]{1,0:T(8,128)S(1)} %collective-permute-done.2, s32[]{:T(128)S(6)} %select_n.50), kind=kLoop, calls=%fused_computation.48 | loop fusion | bytes 524292 | tf_op jit(solution)/shard_map/dynamic_update_slice | solution.py:178
  (25 shorter events, 0.5 us)
Async XLA Ops:
  0.0 10.7 %copy-start = (bf16[1,256,256]{2,1,0:T(8,128)(2,1)S(1)}, bf16[1,256,256]{2,1,0:T(8,128)(2,1)}, u32[]{:S(2)}) copy-start(bf16[1,256,256]{2,1,0:T(8,128)(2,1)} %param.9) | copy-start | bytes 393220
  0.0 10.7 %copy-start.3 = (bf16[2,256,256]{2,1,0:T(8,128)(2,1)S(1)}, bf16[2,256,256]{2,1,0:T(8,128)(2,1)}, u32[]{:S(2)}) copy-start(bf16[2,256,256]{2,1,0:T(8,128)(2,1)} %constant.67.clone) | copy-start | bytes 786436
  0.0 10.9 %copy-start.2 = (bf16[512,512]{1,0:T(8,128)(2,1)S(1)}, bf16[512,512]{1,0:T(8,128)(2,1)}, u32[]{:S(2)}) copy-start(bf16[512,512]{1,0:T(8,128)(2,1)} %constant.68.clone) | copy-start | bytes 1572868
  0.0 10.6 %copy-start.4 = (s32[1,1,8,96]{3,2,1,0:T(8,128)S(1)}, s32[1,1,8,96]{3,2,1,0:T(8,128)}, u32[]{:S(2)}) copy-start(s32[1,1,8,96]{3,2,1,0:T(8,128)} %param.13) | copy-start | bytes 9220
  3.3 14.4 %all-to-all-start = ((f32[8,19,96]{2,1,0:T(8,128)}), f32[8,19,96]{2,1,0:T(8,128)S(1)}, u32[]{:S(2)}, u32[]{:S(2)}) async-start(f32[8,19,96]{2,1,0:T(8,128)} %shard_map.91), calls=%async_computation | async-start | bytes 196608 | tf_op jit(solution)/shard_map/all_to_all | solution.py:135
  17.7 14.0 %all-to-all-start.1 = ((bf16[8,96,256]{2,1,0:T(8,128)(2,1)}), bf16[8,96,256]{2,1,0:T(8,128)(2,1)S(1)}, u32[]{:S(2)}, u32[]{:S(2)}) async-start(bf16[8,96,256]{2,1,0:T(8,128)(2,1)} %bitcast.18), calls=%async_computation.1 | async-start | bytes 786432 | tf_op jit(solution)/shard_map/all_to_all | solution.py:141
  32.2 1.6 %collective-permute-start = (f32[256,256]{1,0:T(8,128)S(1)}, f32[256,256]{1,0:T(8,128)S(1)}, u32[]{:S(2)}, u32[]{:S(2)}) collective-permute-start(f32[256,256]{1,0:T(8,128)S(1)} %fusion.11), channel_id=1, source_target_pairs={{0,1},{1,0},{2,3},{3,2},{4,5},{5,4},{6,7},{7,6},{8,9},{9,8},{10,11... | collective-permute-start | bytes 786440 | tf_op jit(solution)/shard_map/ppermute | solution.py:167
  34.1 5.6 %collective-permute-start.1 = (bf16[256,256]{1,0:T(8,128)(2,1)S(1)}, bf16[256,256]{1,0:T(8,128)(2,1)S(1)}, u32[]{:S(2)}, u32[]{:S(2)}) collective-permute-start(bf16[256,256]{1,0:T(8,128)(2,1)S(1)} %fusion.5), channel_id=1, source_target_pairs={{0,2},{1,3},{2,0},{3,1},{4,6},{5,7},{6,4},{7,5},{8,10},{9,11},{10,... | collective-permute-start | bytes 393224 | tf_op jit(solution)/shard_map/ppermute | solution.py:174
  39.7 1.6 %copy-start.1 = (f32[512,256]{1,0:T(8,128)}, f32[512,256]{1,0:T(8,128)S(1)}, u32[]{:S(2)}) copy-start(f32[512,256]{1,0:T(8,128)S(1)} %get-tuple-element.5) | copy-start | bytes 1572868
  39.7 1.6 %collective-permute-start.2 = (f32[256,256]{1,0:T(8,128)S(1)}, f32[256,256]{1,0:T(8,128)S(1)}, u32[]{:S(2)}, u32[]{:S(2)}) collective-permute-start(f32[256,256]{1,0:T(8,128)S(1)} %get-tuple-element.6), channel_id=1, source_target_pairs={{0,1},{1,0},{2,3},{3,2},{4,5},{5,4},{6,7},{7,6},{8,9},{9,8},{10,11... | collective-permute-start | bytes 786440 | tf_op jit(solution)/shard_map/ppermute | solution.py:176
